TPU v7x, 32 devices: a whole 2x2x4 slice. The times are simulated.
32 devices in a mesh: depth: 4 (over z), region: 8 (over y, x, core).
Axes of the slice: x: 2, y: 2, z: 4, core: 2. Of those that a mesh axis runs over, the one named last changes fastest.
Arguments:
- thermal_grid: float32 [8, 128, 4096], P('depth', None, 'region'), may hold values from -6 to 6
- colormap_samples: float32 [4, 256], replicated, may hold values from 0.05 to 1
- sheetgroup_viewer_sequence: int32 [4], replicated, may hold values from 0 to 3, each once
- occupied_lines: int32 [4, 8], P('depth', 'region'), may hold values from 64 to 128
- skew_offsets: int32 [1], replicated, may hold values from 256 to 511
Outputs:
- image: float32 [4, 128, 4096], P(None, 'depth', 'region')
Inputs may be any that keep to these rules, and one draw needn't show every extreme that they name: `sheetgroup_viewer_sequence`: each rank appears once.
All inputs are finite; a program needn't handle non-finite values.
Results may differ from a plain program's by a relative error of at most 0.0003.
Values sent between devices are 32-bit elements; how exact they have to be, the bound alone decides.
No kernel may reach another device: no remote copies, remote signals or barrier semaphores. Data moves between devices by JAX's collectives and lax.ppermute only.
A program may use at most 64 MiB of HBM per device.

v0:
```python
import math

import jax
import jax.numpy as jnp
from jax import lax
from jax.sharding import PartitionSpec as P


def shifted(block, axis, distance):
    devices = range(lax.axis_size(axis))
    route = [(i - distance, i) for i in devices if i - distance in devices]
    return lax.ppermute(block, axis, route)


def transfer(cells, colormap_samples):
    knot_count = colormap_samples.shape[1]
    vertical_extent, horizontal_extent = cells.shape
    block_rows = math.gcd(vertical_extent, 8)
    following = jnp.concatenate([colormap_samples[:, 1:], colormap_samples[:, -1:]], axis=1)
    table = jnp.concatenate([colormap_samples, following - colormap_samples], axis=0)
    knot_ids = jnp.arange(knot_count, dtype=jnp.int32)

    def one_block(block):
        scaled = jnp.clip((block + 3.0) * ((knot_count - 1) / 6.0), 0.0, knot_count - 1.0)
        lower = jnp.minimum(jnp.floor(scaled), knot_count - 2.0)
        fraction = scaled - lower
        index = lower.astype(jnp.int32).reshape(-1)
        one_hot = (knot_ids[:, None] == index[None, :]).astype(jnp.float32)
        looked = jnp.dot(
            table, one_hot, precision=lax.Precision.HIGHEST, preferred_element_type=jnp.float32
        )
        looked = looked.reshape(8, block_rows, horizontal_extent)
        return looked[:4] + fraction[None] * looked[4:]

    blocks = cells.reshape(vertical_extent // block_rows, block_rows, horizontal_extent)
    values = lax.map(one_block, blocks)
    return jnp.transpose(values, (1, 0, 2, 3)).reshape(4, vertical_extent, horizontal_extent)


def render(
    piece_samples,
    occupied_line_flags,
    slab_depth_rank,
    skew_offsets,
    colormap_samples,
    canvas_width,
    layers_overall,
):
    sheet_number, vertical_extent, horizontal_extent = piece_samples.shape

    def one_layer(carry, inputs):
        optical, colors = carry
        cells, layer_index = inputs
        values = transfer(cells, colormap_samples)
        absorb = values[3] * occupied_line_flags * (6.0 / layers_overall)
        opacity = 1.0 - jnp.exp(-absorb)
        offset = (slab_depth_rank * sheet_number + layer_index) * skew_offsets // layers_overall
        stacked = jnp.concatenate([values[:3] * opacity[None], absorb[None]], axis=0)
        canvas = jnp.zeros((4, vertical_extent, canvas_width), piece_samples.dtype)
        canvas = lax.dynamic_update_slice(canvas, stacked, (jnp.int32(0), jnp.int32(0), offset))
        colors = colors + jnp.exp(-optical)[None] * canvas[:3]
        optical = optical + canvas[3]
        return ((optical, colors), None)

    start = (
        jnp.zeros((vertical_extent, canvas_width), piece_samples.dtype),
        jnp.zeros((3, vertical_extent, canvas_width), piece_samples.dtype),
    )
    (optical, colors), unused = lax.scan(
        one_layer, start, (piece_samples, jnp.arange(sheet_number, dtype=jnp.int32))
    )
    return jnp.concatenate([colors, optical[None]], axis=0)


def shards(
    thermal_grid, colormap_samples, sheetgroup_viewer_sequence, occupied_lines, skew_offsets
):
    sheet_number, vertical_extent, horizontal_extent = thermal_grid.shape
    slab_count = lax.axis_size("depth")
    share_rows = vertical_extent // slab_count
    layers_overall = sheet_number * slab_count
    slab_depth_rank = sheetgroup_viewer_sequence[lax.axis_index("depth")]
    occupied_line_flags = (
        jnp.arange(vertical_extent, dtype=jnp.int32)[:, None] < occupied_lines[0, 0]
    ).astype(jnp.float32) * jnp.ones((1, horizontal_extent), jnp.float32)
    canvas = render(
        thermal_grid,
        occupied_line_flags,
        slab_depth_rank,
        skew_offsets[0],
        colormap_samples,
        2 * horizontal_extent,
        layers_overall,
    )
    behind = shifted(canvas[:, :, horizontal_extent:], "region", 1)
    front_part = canvas[:, :, :horizontal_extent]
    fading = jnp.exp(-front_part[3])
    fragment = jnp.concatenate(
        [front_part[:3] + fading[None] * behind[:3], (front_part[3] + behind[3])[None]], axis=0
    )
    received = lax.all_to_all(fragment, "depth", split_axis=1, concat_axis=1, tiled=True)
    pieces = received.reshape(4, slab_count, share_rows, horizontal_extent)
    in_front = (sheetgroup_viewer_sequence[None, :] < sheetgroup_viewer_sequence[:, None]).astype(
        jnp.float32
    )
    prefix = jnp.einsum("kj,jyx->kyx", in_front, pieces[3], precision=lax.Precision.HIGHEST)
    shaded_color = jnp.sum(jnp.exp(-prefix)[None] * pieces[:3], axis=1)
    coverage = 1.0 - jnp.exp(-jnp.sum(pieces[3], axis=0))
    return jnp.concatenate([shaded_color, coverage[None]], axis=0)


def solution(mesh):
    in_specs = (P("depth", None, "region"), P(), P(), P("depth", "region"), P())
    out_specs = P(None, "depth", "region")
    return jax.shard_map(shards, mesh=mesh, in_specs=in_specs, out_specs=out_specs, check_vma=False)
```

profile of v0, /device:TPU:4, one launch (start us, length us, event | category | flops | bytes accessed | tf_op | source)
XLA Modules:
  0.0 131.3 jit_solution(7891410669978871273)
XLA Ops:
  0.0 0.8 slice.82
  0.8 0.8 slice.83
  1.5 0.8 maximum_subtract_fusion
  2.3 0.7 pad_maximum_fusion.4
  3.6 1.3 dynamic_slice.21
  5.6 72.7 %while.37 = (s32[]{:T(128)}, f32[128,1024]{1,0:T(8,128)}, f32[3,128,1024]{2,1,0:T(8,128)}, f32[2,128,512]{2,1,0:T(8,128)}, f32[8,256]{1,0:T(8,128)S(1)}, /*index...) while((s32[]{:T(128)}, f32[128,1024]{1,0:T(8,128)}, ...), condition=%wide.region_3.4_spmd.clone, body=%wide.region_0.3_spmd.clone.sunk | while | flops 104198144 | bytes 30336572 | solution.py:69
  5.7 0.6 dynamic_slice.35
  7.5 1.0 dynamic-slice_bitcast_fusion.2
  8.5 24.4 %while.38 = (s32[]{:T(128)}, f32[16,4,8,512]{3,2,1,0:T(8,128)S(1)}, f32[16,8,512]{2,1,0:T(8,128)S(1)}, f32[8,256]{1,0:T(8,128)S(1)}, s32[]{:T(128)}) while((s32[]{:T(128)}, f32[16,4,8,512]{3,2,1,0:T(8,128)S(1)}, f32[16,8,512]{2,1,0:T(8,128)S(1)}, f32[8,256]{1,0:T(8,128)S(1)}, s32[]{:T(128)}) %tuple.60), condition=%wide.region_2.2_spmd.clone, body=%wide.region_1.1_spmd.clone.sunk | while | flops 101773312 | bytes 712773 | solution.py:36
  8.5 1.4 %convolution_bitcast_fusion.2 = f32[8,4096]{1,0:T(8,128)S(1)} fusion(f32[8,256]{1,0:T(8,128)S(1)} %get-tuple-element.349, s32[4096]{0:T(1024)S(1)} %bitcast.90), kind=kOutput, calls=%fused_computation.2.clone.1 | convolution fusion | flops 101711872 | bytes 155648 | tf_op jit(solution)/shard_map/while/body/eval_jaxpr/while/body/eval_jaxpr/dot_general | solution.py:29
  10.0 1.4 %convolution_bitcast_fusion.2 = f32[8,4096]{1,0:T(8,128)S(1)} fusion(f32[8,256]{1,0:T(8,128)S(1)} %get-tuple-element.349, s32[4096]{0:T(1024)S(1)} %bitcast.90), kind=kOutput, calls=%fused_computation.2.clone.1 | convolution fusion | flops 101711872 | bytes 155648 | tf_op jit(solution)/shard_map/while/body/eval_jaxpr/while/body/eval_jaxpr/dot_general | solution.py:29
  11.6 1.4 %convolution_bitcast_fusion.2 = f32[8,4096]{1,0:T(8,128)S(1)} fusion(f32[8,256]{1,0:T(8,128)S(1)} %get-tuple-element.349, s32[4096]{0:T(1024)S(1)} %bitcast.90), kind=kOutput, calls=%fused_computation.2.clone.1 | convolution fusion | flops 101711872 | bytes 155648 | tf_op jit(solution)/shard_map/while/body/eval_jaxpr/while/body/eval_jaxpr/dot_general | solution.py:29
  13.1 1.4 %convolution_bitcast_fusion.2 = f32[8,4096]{1,0:T(8,128)S(1)} fusion(f32[8,256]{1,0:T(8,128)S(1)} %get-tuple-element.349, s32[4096]{0:T(1024)S(1)} %bitcast.90), kind=kOutput, calls=%fused_computation.2.clone.1 | convolution fusion | flops 101711872 | bytes 155648 | tf_op jit(solution)/shard_map/while/body/eval_jaxpr/while/body/eval_jaxpr/dot_general | solution.py:29
  14.6 1.4 %convolution_bitcast_fusion.2 = f32[8,4096]{1,0:T(8,128)S(1)} fusion(f32[8,256]{1,0:T(8,128)S(1)} %get-tuple-element.349, s32[4096]{0:T(1024)S(1)} %bitcast.90), kind=kOutput, calls=%fused_computation.2.clone.1 | convolution fusion | flops 101711872 | bytes 155648 | tf_op jit(solution)/shard_map/while/body/eval_jaxpr/while/body/eval_jaxpr/dot_general | solution.py:29
  16.1 1.4 %convolution_bitcast_fusion.2 = f32[8,4096]{1,0:T(8,128)S(1)} fusion(f32[8,256]{1,0:T(8,128)S(1)} %get-tuple-element.349, s32[4096]{0:T(1024)S(1)} %bitcast.90), kind=kOutput, calls=%fused_computation.2.clone.1 | convolution fusion | flops 101711872 | bytes 155648 | tf_op jit(solution)/shard_map/while/body/eval_jaxpr/while/body/eval_jaxpr/dot_general | solution.py:29
  17.7 1.4 %convolution_bitcast_fusion.2 = f32[8,4096]{1,0:T(8,128)S(1)} fusion(f32[8,256]{1,0:T(8,128)S(1)} %get-tuple-element.349, s32[4096]{0:T(1024)S(1)} %bitcast.90), kind=kOutput, calls=%fused_computation.2.clone.1 | convolution fusion | flops 101711872 | bytes 155648 | tf_op jit(solution)/shard_map/while/body/eval_jaxpr/while/body/eval_jaxpr/dot_general | solution.py:29
  19.2 1.4 %convolution_bitcast_fusion.2 = f32[8,4096]{1,0:T(8,128)S(1)} fusion(f32[8,256]{1,0:T(8,128)S(1)} %get-tuple-element.349, s32[4096]{0:T(1024)S(1)} %bitcast.90), kind=kOutput, calls=%fused_computation.2.clone.1 | convolution fusion | flops 101711872 | bytes 155648 | tf_op jit(solution)/shard_map/while/body/eval_jaxpr/while/body/eval_jaxpr/dot_general | solution.py:29
  20.7 1.4 %convolution_bitcast_fusion.2 = f32[8,4096]{1,0:T(8,128)S(1)} fusion(f32[8,256]{1,0:T(8,128)S(1)} %get-tuple-element.349, s32[4096]{0:T(1024)S(1)} %bitcast.90), kind=kOutput, calls=%fused_computation.2.clone.1 | convolution fusion | flops 101711872 | bytes 155648 | tf_op jit(solution)/shard_map/while/body/eval_jaxpr/while/body/eval_jaxpr/dot_general | solution.py:29
  22.2 1.4 %convolution_bitcast_fusion.2 = f32[8,4096]{1,0:T(8,128)S(1)} fusion(f32[8,256]{1,0:T(8,128)S(1)} %get-tuple-element.349, s32[4096]{0:T(1024)S(1)} %bitcast.90), kind=kOutput, calls=%fused_computation.2.clone.1 | convolution fusion | flops 101711872 | bytes 155648 | tf_op jit(solution)/shard_map/while/body/eval_jaxpr/while/body/eval_jaxpr/dot_general | solution.py:29
  23.8 1.4 %convolution_bitcast_fusion.2 = f32[8,4096]{1,0:T(8,128)S(1)} fusion(f32[8,256]{1,0:T(8,128)S(1)} %get-tuple-element.349, s32[4096]{0:T(1024)S(1)} %bitcast.90), kind=kOutput, calls=%fused_computation.2.clone.1 | convolution fusion | flops 101711872 | bytes 155648 | tf_op jit(solution)/shard_map/while/body/eval_jaxpr/while/body/eval_jaxpr/dot_general | solution.py:29
  25.3 1.4 %convolution_bitcast_fusion.2 = f32[8,4096]{1,0:T(8,128)S(1)} fusion(f32[8,256]{1,0:T(8,128)S(1)} %get-tuple-element.349, s32[4096]{0:T(1024)S(1)} %bitcast.90), kind=kOutput, calls=%fused_computation.2.clone.1 | convolution fusion | flops 101711872 | bytes 155648 | tf_op jit(solution)/shard_map/while/body/eval_jaxpr/while/body/eval_jaxpr/dot_general | solution.py:29
  26.8 1.4 %convolution_bitcast_fusion.2 = f32[8,4096]{1,0:T(8,128)S(1)} fusion(f32[8,256]{1,0:T(8,128)S(1)} %get-tuple-element.349, s32[4096]{0:T(1024)S(1)} %bitcast.90), kind=kOutput, calls=%fused_computation.2.clone.1 | convolution fusion | flops 101711872 | bytes 155648 | tf_op jit(solution)/shard_map/while/body/eval_jaxpr/while/body/eval_jaxpr/dot_general | solution.py:29
  28.3 1.4 %convolution_bitcast_fusion.2 = f32[8,4096]{1,0:T(8,128)S(1)} fusion(f32[8,256]{1,0:T(8,128)S(1)} %get-tuple-element.349, s32[4096]{0:T(1024)S(1)} %bitcast.90), kind=kOutput, calls=%fused_computation.2.clone.1 | convolution fusion | flops 101711872 | bytes 155648 | tf_op jit(solution)/shard_map/while/body/eval_jaxpr/while/body/eval_jaxpr/dot_general | solution.py:29
  29.8 1.4 %convolution_bitcast_fusion.2 = f32[8,4096]{1,0:T(8,128)S(1)} fusion(f32[8,256]{1,0:T(8,128)S(1)} %get-tuple-element.349, s32[4096]{0:T(1024)S(1)} %bitcast.90), kind=kOutput, calls=%fused_computation.2.clone.1 | convolution fusion | flops 101711872 | bytes 155648 | tf_op jit(solution)/shard_map/while/body/eval_jaxpr/while/body/eval_jaxpr/dot_general | solution.py:29
  31.4 1.4 %convolution_bitcast_fusion.2 = f32[8,4096]{1,0:T(8,128)S(1)} fusion(f32[8,256]{1,0:T(8,128)S(1)} %get-tuple-element.349, s32[4096]{0:T(1024)S(1)} %bitcast.90), kind=kOutput, calls=%fused_computation.2.clone.1 | convolution fusion | flops 101711872 | bytes 155648 | tf_op jit(solution)/shard_map/while/body/eval_jaxpr/while/body/eval_jaxpr/dot_general | solution.py:29
  33.5 4.9 %dynamic_update_slice.15 = f32[4,128,1024]{2,1,0:T(8,128)S(1)} dynamic-update-slice(f32[4,128,1024]{2,1,0:T(8,128)S(1)} %broadcast.169, f32[4,128,512]{2,1,0:T(8,128)S(1)} %pad_maximum_fusion.6, s32[]{:T(128)} %constant.96.clone.1..sunk, s32[]{:T(128)} %constant.96.clone.1..sunk, s32[]{:T(128)S(6)} %select_n.23) | dynamic-update-slice | bytes 2097156 | tf_op jit(solution)/shard_map/while/body/eval_jaxpr/dynamic_update_slice | solution.py:60
  38.4 0.9 negate_exponential_fusion.3
  39.3 0.7 copy-done
  40.0 0.6 fusion.34
  40.6 1.1 copy-done.1
  41.7 0.6 dynamic_slice.35
  43.6 1.0 dynamic-slice_bitcast_fusion.2
  44.5 24.4 %while.38 = (s32[]{:T(128)}, f32[16,4,8,512]{3,2,1,0:T(8,128)S(1)}, f32[16,8,512]{2,1,0:T(8,128)S(1)}, f32[8,256]{1,0:T(8,128)S(1)}, s32[]{:T(128)}) while((s32[]{:T(128)}, f32[16,4,8,512]{3,2,1,0:T(8,128)S(1)}, f32[16,8,512]{2,1,0:T(8,128)S(1)}, f32[8,256]{1,0:T(8,128)S(1)}, s32[]{:T(128)}) %tuple.60), condition=%wide.region_2.2_spmd.clone, body=%wide.region_1.1_spmd.clone.sunk | while | flops 101773312 | bytes 712773 | solution.py:36
  44.6 1.4 %convolution_bitcast_fusion.2 = f32[8,4096]{1,0:T(8,128)S(1)} fusion(f32[8,256]{1,0:T(8,128)S(1)} %get-tuple-element.349, s32[4096]{0:T(1024)S(1)} %bitcast.90), kind=kOutput, calls=%fused_computation.2.clone.1 | convolution fusion | flops 101711872 | bytes 155648 | tf_op jit(solution)/shard_map/while/body/eval_jaxpr/while/body/eval_jaxpr/dot_general | solution.py:29
  46.1 1.4 %convolution_bitcast_fusion.2 = f32[8,4096]{1,0:T(8,128)S(1)} fusion(f32[8,256]{1,0:T(8,128)S(1)} %get-tuple-element.349, s32[4096]{0:T(1024)S(1)} %bitcast.90), kind=kOutput, calls=%fused_computation.2.clone.1 | convolution fusion | flops 101711872 | bytes 155648 | tf_op jit(solution)/shard_map/while/body/eval_jaxpr/while/body/eval_jaxpr/dot_general | solution.py:29
  47.6 1.4 %convolution_bitcast_fusion.2 = f32[8,4096]{1,0:T(8,128)S(1)} fusion(f32[8,256]{1,0:T(8,128)S(1)} %get-tuple-element.349, s32[4096]{0:T(1024)S(1)} %bitcast.90), kind=kOutput, calls=%fused_computation.2.clone.1 | convolution fusion | flops 101711872 | bytes 155648 | tf_op jit(solution)/shard_map/while/body/eval_jaxpr/while/body/eval_jaxpr/dot_general | solution.py:29
  49.2 1.4 %convolution_bitcast_fusion.2 = f32[8,4096]{1,0:T(8,128)S(1)} fusion(f32[8,256]{1,0:T(8,128)S(1)} %get-tuple-element.349, s32[4096]{0:T(1024)S(1)} %bitcast.90), kind=kOutput, calls=%fused_computation.2.clone.1 | convolution fusion | flops 101711872 | bytes 155648 | tf_op jit(solution)/shard_map/while/body/eval_jaxpr/while/body/eval_jaxpr/dot_general | solution.py:29
  50.7 1.4 %convolution_bitcast_fusion.2 = f32[8,4096]{1,0:T(8,128)S(1)} fusion(f32[8,256]{1,0:T(8,128)S(1)} %get-tuple-element.349, s32[4096]{0:T(1024)S(1)} %bitcast.90), kind=kOutput, calls=%fused_computation.2.clone.1 | convolution fusion | flops 101711872 | bytes 155648 | tf_op jit(solution)/shard_map/while/body/eval_jaxpr/while/body/eval_jaxpr/dot_general | solution.py:29
  52.2 1.4 %convolution_bitcast_fusion.2 = f32[8,4096]{1,0:T(8,128)S(1)} fusion(f32[8,256]{1,0:T(8,128)S(1)} %get-tuple-element.349, s32[4096]{0:T(1024)S(1)} %bitcast.90), kind=kOutput, calls=%fused_computation.2.clone.1 | convolution fusion | flops 101711872 | bytes 155648 | tf_op jit(solution)/shard_map/while/body/eval_jaxpr/while/body/eval_jaxpr/dot_general | solution.py:29
  53.7 1.4 %convolution_bitcast_fusion.2 = f32[8,4096]{1,0:T(8,128)S(1)} fusion(f32[8,256]{1,0:T(8,128)S(1)} %get-tuple-element.349, s32[4096]{0:T(1024)S(1)} %bitcast.90), kind=kOutput, calls=%fused_computation.2.clone.1 | convolution fusion | flops 101711872 | bytes 155648 | tf_op jit(solution)/shard_map/while/body/eval_jaxpr/while/body/eval_jaxpr/dot_general | solution.py:29
  55.3 1.4 %convolution_bitcast_fusion.2 = f32[8,4096]{1,0:T(8,128)S(1)} fusion(f32[8,256]{1,0:T(8,128)S(1)} %get-tuple-element.349, s32[4096]{0:T(1024)S(1)} %bitcast.90), kind=kOutput, calls=%fused_computation.2.clone.1 | convolution fusion | flops 101711872 | bytes 155648 | tf_op jit(solution)/shard_map/while/body/eval_jaxpr/while/body/eval_jaxpr/dot_general | solution.py:29
  56.8 1.4 %convolution_bitcast_fusion.2 = f32[8,4096]{1,0:T(8,128)S(1)} fusion(f32[8,256]{1,0:T(8,128)S(1)} %get-tuple-element.349, s32[4096]{0:T(1024)S(1)} %bitcast.90), kind=kOutput, calls=%fused_computation.2.clone.1 | convolution fusion | flops 101711872 | bytes 155648 | tf_op jit(solution)/shard_map/while/body/eval_jaxpr/while/body/eval_jaxpr/dot_general | solution.py:29
  58.3 1.4 %convolution_bitcast_fusion.2 = f32[8,4096]{1,0:T(8,128)S(1)} fusion(f32[8,256]{1,0:T(8,128)S(1)} %get-tuple-element.349, s32[4096]{0:T(1024)S(1)} %bitcast.90), kind=kOutput, calls=%fused_computation.2.clone.1 | convolution fusion | flops 101711872 | bytes 155648 | tf_op jit(solution)/shard_map/while/body/eval_jaxpr/while/body/eval_jaxpr/dot_general | solution.py:29
  59.8 1.4 %convolution_bitcast_fusion.2 = f32[8,4096]{1,0:T(8,128)S(1)} fusion(f32[8,256]{1,0:T(8,128)S(1)} %get-tuple-element.349, s32[4096]{0:T(1024)S(1)} %bitcast.90), kind=kOutput, calls=%fused_computation.2.clone.1 | convolution fusion | flops 101711872 | bytes 155648 | tf_op jit(solution)/shard_map/while/body/eval_jaxpr/while/body/eval_jaxpr/dot_general | solution.py:29
  61.4 1.4 %convolution_bitcast_fusion.2 = f32[8,4096]{1,0:T(8,128)S(1)} fusion(f32[8,256]{1,0:T(8,128)S(1)} %get-tuple-element.349, s32[4096]{0:T(1024)S(1)} %bitcast.90), kind=kOutput, calls=%fused_computation.2.clone.1 | convolution fusion | flops 101711872 | bytes 155648 | tf_op jit(solution)/shard_map/while/body/eval_jaxpr/while/body/eval_jaxpr/dot_general | solution.py:29
  62.9 1.4 %convolution_bitcast_fusion.2 = f32[8,4096]{1,0:T(8,128)S(1)} fusion(f32[8,256]{1,0:T(8,128)S(1)} %get-tuple-element.349, s32[4096]{0:T(1024)S(1)} %bitcast.90), kind=kOutput, calls=%fused_computation.2.clone.1 | convolution fusion | flops 101711872 | bytes 155648 | tf_op jit(solution)/shard_map/while/body/eval_jaxpr/while/body/eval_jaxpr/dot_general | solution.py:29
  64.4 1.4 %convolution_bitcast_fusion.2 = f32[8,4096]{1,0:T(8,128)S(1)} fusion(f32[8,256]{1,0:T(8,128)S(1)} %get-tuple-element.349, s32[4096]{0:T(1024)S(1)} %bitcast.90), kind=kOutput, calls=%fused_computation.2.clone.1 | convolution fusion | flops 101711872 | bytes 155648 | tf_op jit(solution)/shard_map/while/body/eval_jaxpr/while/body/eval_jaxpr/dot_general | solution.py:29
  65.9 1.4 %convolution_bitcast_fusion.2 = f32[8,4096]{1,0:T(8,128)S(1)} fusion(f32[8,256]{1,0:T(8,128)S(1)} %get-tuple-element.349, s32[4096]{0:T(1024)S(1)} %bitcast.90), kind=kOutput, calls=%fused_computation.2.clone.1 | convolution fusion | flops 101711872 | bytes 155648 | tf_op jit(solution)/shard_map/while/body/eval_jaxpr/while/body/eval_jaxpr/dot_general | solution.py:29
  67.5 1.4 %convolution_bitcast_fusion.2 = f32[8,4096]{1,0:T(8,128)S(1)} fusion(f32[8,256]{1,0:T(8,128)S(1)} %get-tuple-element.349, s32[4096]{0:T(1024)S(1)} %bitcast.90), kind=kOutput, calls=%fused_computation.2.clone.1 | convolution fusion | flops 101711872 | bytes 155648 | tf_op jit(solution)/shard_map/while/body/eval_jaxpr/while/body/eval_jaxpr/dot_general | solution.py:29
  69.6 4.9 %dynamic_update_slice.15 = f32[4,128,1024]{2,1,0:T(8,128)S(1)} dynamic-update-slice(f32[4,128,1024]{2,1,0:T(8,128)S(1)} %broadcast.169, f32[4,128,512]{2,1,0:T(8,128)S(1)} %pad_maximum_fusion.6, s32[]{:T(128)} %constant.96.clone.1..sunk, s32[]{:T(128)} %constant.96.clone.1..sunk, s32[]{:T(128)S(6)} %select_n.23) | dynamic-update-slice | bytes 2097156 | tf_op jit(solution)/shard_map/while/body/eval_jaxpr/dynamic_update_slice | solution.py:60
  74.5 2.0 %negate_exponential_fusion.3 = (f32[128,1024]{1,0:T(8,128)S(1)}, f32[128,1024]{1,0:T(8,128)}) fusion(f32[128,1024]{1,0:T(8,128)} %get-tuple-element.369, pred[]{:T(512)S(6)} %compare.9, f32[4,128,1024]{2,1,0:T(8,128)S(1)} %dynamic_update_slice.15), kind=kLoop, calls=%fused_computation.18.clone.1 | loop fusion | flops 393216 | bytes 2097153 | tf_op jit(solution)/shard_map/while/body/eval_jaxpr/exp | solution.py:61
  76.6 0.6 fusion.34
  77.1 1.1 copy-done.1
  78.3 2.5 %copy.18 = f32[3,128,1024]{2,0,1:T(4,128)S(1)} copy(f32[3,128,1024]{2,1,0:T(8,128)} %get-tuple-element.153) | data formatting | bytes 3145728 | tf_op jit(solution)/shard_map/while | solution.py:69
  80.9 0.4 broadcast_in_dim.15
  81.2 0.5 pad_maximum_fusion.1
  81.7 1.9 %collective-permute-start = (f32[4,128,512]{2,0,1:T(4,128)S(1)}, f32[4,128,512]{2,0,1:T(4,128)S(1)}, u32[]{:S(2)}, u32[]{:S(2)}) collective-permute-start(f32[4,128,512]{2,0,1:T(4,128)S(1)} %pad_maximum_fusion.1), channel_id=1, source_target_pairs={{0,1},{1,2},{2,3},{3,4},{4,5},{5,6},{6,7},{8,9},{9,10},{10,11},{11... | collective-permute-start | bytes 3145736 | tf_op jit(solution)/shard_map/ppermute | solution.py:12
  83.6 15.1 %collective-permute-done = f32[4,128,512]{2,0,1:T(4,128)S(1)} collective-permute-done((f32[4,128,512]{2,0,1:T(4,128)S(1)}, f32[4,128,512]{2,0,1:T(4,128)S(1)}, u32[]{:S(2)}, u32[]{:S(2)}) %collective-permute-start) | collective-permute-done | bytes 1048608 | tf_op jit(solution)/shard_map/ppermute | solution.py:12
  98.7 0.6 negate_exponential_fusion.1
  99.4 0.4 fusion.15
  99.8 0.5 pad_maximum_fusion.2
  100.3 28.8 %all_to_all.5 = f32[4,128,512]{2,0,1:T(4,128)S(1)} all-to-all(f32[4,128,512]{2,0,1:T(4,128)S(1)} %pad_maximum_fusion.2), channel_id=1, replica_groups=mesh['depth'=4,'region'=8] {'depth'}, dimensions={1} | all-to-all | bytes 2097152 | tf_op jit(solution)/shard_map/all_to_all | solution.py:101
  129.4 0.5 fusion.14
  130.6 0.8 copy.23
  (162 shorter events, 5.1 us)
Async XLA Ops:
  38.4 1.6 %copy-start = (f32[3,128,1024]{2,1,0:T(8,128)S(1)}, f32[3,128,1024]{2,1,0:T(8,128)}, u32[]{:S(2)}) copy-start(f32[3,128,1024]{2,1,0:T(8,128)} %get-tuple-element.370) | copy-start | bytes 4718596 | tf_op jit(solution)/shard_map/while
  40.6 1.2 copy-start.1
  74.5 2.1 %copy-start = (f32[3,128,1024]{2,1,0:T(8,128)S(1)}, f32[3,128,1024]{2,1,0:T(8,128)}, u32[]{:S(2)}) copy-start(f32[3,128,1024]{2,1,0:T(8,128)} %get-tuple-element.370) | copy-start | bytes 4718596 | tf_op jit(solution)/shard_map/while
  77.1 1.2 copy-start.1
  78.3 2.6 %copy-start.2 = (f32[128,1024]{1,0:T(8,128)S(1)}, f32[128,1024]{1,0:T(8,128)}, u32[]{:S(2)}) copy-start(f32[128,1024]{1,0:T(8,128)} %get-tuple-element.154) | copy-start | bytes 1572868
  81.7 17.0 %collective-permute-start = (f32[4,128,512]{2,0,1:T(4,128)S(1)}, f32[4,128,512]{2,0,1:T(4,128)S(1)}, u32[]{:S(2)}, u32[]{:S(2)}) collective-permute-start(f32[4,128,512]{2,0,1:T(4,128)S(1)} %pad_maximum_fusion.1), channel_id=1, source_target_pairs={{0,1},{1,2},{2,3},{3,4},{4,5},{5,6},{6,7},{8,9},{9,10},{10,11},{11... | collective-permute-start | bytes 3145736 | tf_op jit(solution)/shard_map/ppermute | solution.py:12
  100.2 29.1 %copy-start.3 = (s32[4]{0:T(128)S(1)}, s32[4]{0:T(128)}, u32[]{:S(2)}) copy-start(s32[4]{0:T(128)} %param.11) | copy-start | bytes 52
where the time goes:
time: 131 us
  matrix products  45 us (34%)
  blocking collectives  28.8 us (22%)
  local copies, waits for them, and re-layouts  24.3 us (19%)
  waiting for transfers between devices  15.1 us (12%)
  other arithmetic  10.8 us (8%)
  loops' own time  3.97 us (3%)
  starting transfers between devices  1.92 us (1%)
  between operations  1.5 us (1%)
    dot_general x32, matrix products, one_block(): jnp.dot(table, one_hot, precision=lax.Precision.HIGHEST, preferred_elemen...  44.5 us
    all_to_all x1, blocking collectives, shards(): lax.all_to_all(fragment, 'depth', split_axis=1, concat_axis=1, tiled=True)  28.8 us
    ppermute x1, waiting for transfers between devices, shifted(): return lax.ppermute(block, axis, route)  15.1 us
    dynamic_update_slice x2, local copies, waits for them, and re-layouts, one_layer(): lax.dynamic_update_slice(canvas, stacked, (jnp.int32(0), jnp.int32(0), of...  9.83 us
    while x40, local copies, waits for them, and re-layouts  3.19 us
    exp x2, other arithmetic, one_layer(): colors = colors + jnp.exp(-optical)[None] * canvas[:3]  2.93 us
    another operation x1, loops' own time, render(): lax.scan(one_layer, start, (piece_samples, jnp.arange(sheet_number, dtype...  2.68 us
  transfers between devices with their start and end apart: 1, of which 1 were waited for; matrix products, arithmetic and copies ran while one was open for 0% of the time, Pallas kernels for 0%

commit v1 on v0

v1 whole, which is shorter than its diff:
```python
import functools

import jax
import jax.numpy as jnp
from jax import lax
from jax.experimental import pallas as pl
from jax.experimental.pallas import tpu as pltpu
from jax.sharding import PartitionSpec as P

EMPTY = 1.0e6
LANES = 128
SUBLANES = 8


def lookup(cells, tables, knot_count):
    scaled = jnp.clip((cells + 3.0) * ((knot_count - 1) / 6.0), 0.0, knot_count - 1.0)
    lower = jnp.minimum(jnp.floor(scaled), knot_count - 2.0)
    fraction = scaled - lower
    index = lower.astype(jnp.int32)
    upper_half = index >= LANES
    lane = jnp.where(upper_half, index - LANES, index)
    values = []
    for c in range(4):
        picked = []
        for base in (0, 8):
            low = jnp.take_along_axis(tables[base + 2 * c], lane, axis=1, mode="promise_in_bounds")
            high = jnp.take_along_axis(tables[base + 2 * c + 1], lane, axis=1, mode="promise_in_bounds")
            picked.append(jnp.where(upper_half, high, low))
        values.append(picked[0] + fraction * picked[1])
    return values


def render_kernel(seq_ref, skew_ref, own_ref, left_ref, cmap_ref, out_ref, shifted_ref):
    layers, slabs, rows, width = own_ref.shape
    layers_overall = layers * slabs
    knot_count = cmap_ref.shape[1]
    first_tile = lax.axis_index("region") == 0
    skew = skew_ref[0]

    order = []
    for k in range(slabs):
        s = jnp.int32(0)
        for j in range(slabs):
            s = s + jnp.where(seq_ref[j] == k, j, 0)
        order.append(s)

    for k in range(slabs):
        s = order[k]
        for l in range(layers):
            shift = ((k * layers + l) * skew) // layers_overall
            for r in range(rows // SUBLANES):
                band = pl.ds(r * SUBLANES, SUBLANES)
                left = jnp.where(first_tile, EMPTY, left_ref[l, s, band, :])
                joined = jnp.concatenate([left, own_ref[l, s, band, :]], axis=1)
                shifted_ref[l, k, band, :] = pltpu.roll(joined, shift, 1)[:, width:]

    cmap = cmap_ref[...]
    following = pltpu.roll(cmap, knot_count - 1, 1)
    delta = following - cmap
    tables = []
    for src in (cmap, delta):
        for c in range(4):
            for h in range(knot_count // LANES):
                row = src[c : c + 1, h * LANES : (h + 1) * LANES]
                tables.append(jnp.broadcast_to(row, (SUBLANES, LANES)))

    pieces = width // LANES

    def block(i, carry):
        r = i // pieces
        j = i % pieces
        band = pl.ds(pl.multiple_of(r * SUBLANES, SUBLANES), SUBLANES)
        cols = pl.ds(pl.multiple_of(j * LANES, LANES), LANES)
        depth_sum = jnp.zeros((SUBLANES, LANES), jnp.float32)
        image = [jnp.zeros((SUBLANES, LANES), jnp.float32) for _ in range(3)]
        for k in range(slabs):
            tau = None
            color = None
            for l in range(layers):
                cells = shifted_ref[l, k, band, cols]
                values = lookup(cells, tables, knot_count)
                absorb = jnp.where(cells < 100.0, values[3] * (6.0 / layers_overall), 0.0)
                through = jnp.exp(-absorb)
                opacity = 1.0 - through
                emit = [values[c] * opacity for c in range(3)]
                if tau is None:
                    color = emit
                    tau = absorb
                else:
                    fade = jnp.exp(-tau)
                    color = [color[c] + fade * emit[c] for c in range(3)]
                    tau = tau + absorb
            if k == 0:
                image = color
            else:
                fade = jnp.exp(-depth_sum)
                image = [image[c] + fade * color[c] for c in range(3)]
            depth_sum = depth_sum + tau
        for c in range(3):
            out_ref[c, band, cols] = image[c]
        out_ref[3, band, cols] = 1.0 - jnp.exp(-depth_sum)
        return carry

    lax.fori_loop(0, (rows // SUBLANES) * pieces, block, 0)


def shards(thermal_grid, colormap_samples, sheetgroup_viewer_sequence, occupied_lines, skew_offsets):
    layers, rows, width = thermal_grid.shape
    slabs = lax.axis_size("depth")
    regions = lax.axis_size("region")
    share = rows // slabs
    line = lax.broadcasted_iota(jnp.int32, (1, rows, 1), 1)
    marked = jnp.where(line < occupied_lines[0, 0], thermal_grid, EMPTY)
    blocks = marked.reshape(layers, slabs, share, width)
    own = lax.all_to_all(blocks, "depth", split_axis=1, concat_axis=1, tiled=True)
    left = lax.ppermute(own, "region", [(i, i + 1) for i in range(regions - 1)])
    vmem = pltpu.VMEM
    smem = pltpu.SMEM
    return pl.pallas_call(
        render_kernel,
        out_shape=jax.ShapeDtypeStruct((4, share, width), jnp.float32),
        in_specs=[
            pl.BlockSpec(memory_space=smem),
            pl.BlockSpec(memory_space=smem),
            pl.BlockSpec(memory_space=vmem),
            pl.BlockSpec(memory_space=vmem),
            pl.BlockSpec(memory_space=vmem),
        ],
        out_specs=pl.BlockSpec(memory_space=vmem),
        scratch_shapes=[pltpu.VMEM((layers, slabs, share, width), jnp.float32)],
    )(sheetgroup_viewer_sequence, skew_offsets, own, left, colormap_samples)


def solution(mesh):
    in_specs = (P("depth", None, "region"), P(), P(), P("depth", "region"), P())
    out_specs = P(None, "depth", "region")
    return jax.shard_map(shards, mesh=mesh, in_specs=in_specs, out_specs=out_specs, check_vma=False)
```

time: 131 us -> 39.9 us (0.30)
  matrix products: 45 us -> 0 us
  local copies, waits for them, and re-layouts: 24.3 us -> 0.87 us
  other arithmetic: 10.8 us -> 1.16 us
  blocking collectives: 28.8 us -> 19.2 us
  Pallas kernels: 0 us -> 6.39 us
  waiting for transfers between devices: 15.1 us -> 8.82 us
  loops' own time: 3.97 us -> 0 us
    dot_general x33 -> x0, matrix products: 45 us -> none  [the longest x32 44.5 us: one_block(): jnp.dot(table, one_hot, precision=lax.Precision.HIGHEST, preferred_elemen...]
    dynamic_update_slice x2 -> x0, local copies, waits for them, and re-layouts: 9.83 us -> none  [one_layer(): lax.dynamic_update_slice(canvas, stacked, (jnp.int32(0), jnp.int32(0), of...]
    all_to_all x1, blocking collectives: 28.8 us -> 19.2 us  [shards(): lax.all_to_all(blocks, 'depth', split_axis=1, concat_axis=1, tiled=True)]
    pallas_call x0 -> x1, Pallas kernels: none -> 6.39 us  [shards(): pl.pallas_call(render_kernel, out_shape=jax.ShapeDtypeStruct((4, share, w...]
    ppermute x1, waiting for transfers between devices: 15.1 us -> 8.82 us  [shards(): left = lax.ppermute(own, 'region', [(i, i + 1) for i in range(regions - 1)])]
    while x41 -> x0, local copies, waits for them, and re-layouts: 5.74 us -> none
    another operation x3 -> x0, loops' own time: 3.97 us -> none  [the longest x1 2.68 us: render(): lax.scan(one_layer, start, (piece_samples, jnp.arange(sheet_number, dtype...]
    exp x3 -> x0, other arithmetic: 3.55 us -> none  [the longest x2 2.93 us: one_layer(): colors = colors + jnp.exp(-optical)[None] * canvas[:3]]
where the time goes in v1:
time: 39.9 us; the launch traced here: 39.7 us
  blocking collectives  19.2 us (48%)
  waiting for transfers between devices  8.82 us (22%)
  Pallas kernels  6.39 us (16%)
  starting transfers between devices  1.92 us (5%)
  between operations  1.34 us (3%)
  other arithmetic  1.16 us (3%)
  local copies, waits for them, and re-layouts  0.87 us (2%)
    all_to_all x1, blocking collectives, shards(): lax.all_to_all(blocks, 'depth', split_axis=1, concat_axis=1, tiled=True)  19.2 us
    ppermute x1, waiting for transfers between devices, shards(): left = lax.ppermute(own, 'region', [(i, i + 1) for i in range(regions - 1)])  8.82 us
    pallas_call x1, Pallas kernels, shards(): pl.pallas_call(render_kernel, out_shape=jax.ShapeDtypeStruct((4, share, w...  6.39 us
    ppermute x1, starting transfers between devices, shards(): left = lax.ppermute(own, 'region', [(i, i + 1) for i in range(regions - 1)])  1.92 us
    select_n x1, other arithmetic, shards(): marked = jnp.where(line < occupied_lines[0, 0], thermal_grid, EMPTY)  1.15 us
    unnamed x4, local copies, waits for them, and re-layouts  0.8 us
  transfers between devices with their start and end apart: 1, of which 1 were waited for; matrix products, arithmetic and copies ran while one was open for 0% of the time, Pallas kernels for 0%

profile of v1, /device:TPU:4, one launch (start us, length us, event | category | flops | bytes accessed | tf_op | source)
XLA Modules:
  0.0 39.7 jit_solution(2479697118829408883)
XLA Ops:
  0.7 1.2 %broadcast_select_fusion = f32[2,128,512]{2,1,0:T(8,128)S(1)} fusion(f32[2,128,512]{2,1,0:T(8,128)} %param.5, pred[128]{0:T(512)(128)(4,1)S(1)} %iota_compare_fusion), kind=kLoop, calls=%fused_computation | loop fusion | flops 131072 | bytes 1048704 | tf_op jit(solution)/shard_map/jit(_where)/select_n | solution.py:113
  1.9 19.2 %all_to_all.5 = f32[2,4,32,512]{3,2,0,1:T(8,128)S(1)} all-to-all(f32[2,4,32,512]{3,2,0,1:T(8,128)S(1)} %copy.8), channel_id=1, replica_groups=mesh['depth'=4,'region'=8] {'depth'}, dimensions={1} | all-to-all | bytes 1048576 | tf_op jit(solution)/shard_map/all_to_all | solution.py:115
  21.1 0.0 copy-start
  21.1 1.9 %collective-permute-start = (f32[2,4,32,512]{3,2,1,0:T(8,128)S(1)}, f32[2,4,32,512]{3,2,1,0:T(8,128)S(1)}, u32[]{:S(2)}, u32[]{:S(2)}) collective-permute-start(f32[2,4,32,512]{3,2,1,0:T(8,128)S(1)} %copy.10.own_ref), channel_id=1, source_target_pairs={{0,1},{1,2},{2,3},{3,4},{4,5},{5,6},{6,7},{8,9},{9,10},{10,11},{11... | collective-permute-start | bytes 1572872 | tf_op jit(solution)/shard_map/ppermute | solution.py:116
  23.7 8.8 %collective-permute-done.left_ref = f32[2,4,32,512]{3,2,1,0:T(8,128)S(1)} collective-permute-done((f32[2,4,32,512]{3,2,1,0:T(8,128)S(1)}, f32[2,4,32,512]{3,2,1,0:T(8,128)S(1)}, u32[]{:S(2)}, u32[]{:S(2)}) %collective-permute-start) | collective-permute-done | bytes 524320 | tf_op jit(solution)/shard_map/ppermute | solution.py:116
  32.5 0.0 copy-done
  32.5 0.0 copy-start.1
  32.5 0.8 %copy-done.1 = f32[2,4,32,512]{3,2,1,0:T(8,128)} copy-done((f32[2,4,32,512]{3,2,1,0:T(8,128)}, f32[2,4,32,512]{3,2,1,0:T(8,128)S(1)}, u32[]{:S(2)}) %copy-start.1) | copy-done | bytes 524312
  33.3 6.4 %shard_map.55 = f32[4,32,512]{2,1,0:T(8,128)} custom-call(s32[4]{0:T(128)} %seq_ref.1, s32[1]{0:T(128)S(6)} %copy.12.skew_ref, f32[2,4,32,512]{3,2,1,0:T(8,128)} %copy-done, f32[2,4,32,512]{3,2,1,0:T(8,128)} %copy-done.1, f32[4,256]{1,0:T(4,128)} %cmap_ref.1), custom_call_target="tpu_custom_call" | custom-call | tf_op jit(solution)/shard_map/pallas_call | solution.py:119
  (3 shorter events, 0.1 us)
Async XLA Ops:
  21.1 11.4 %copy-start = (f32[2,4,32,512]{3,2,1,0:T(8,128)}, f32[2,4,32,512]{3,2,1,0:T(8,128)S(1)}, u32[]{:S(2)}) copy-start(f32[2,4,32,512]{3,2,1,0:T(8,128)S(1)} %copy.10.own_ref) | copy-start | bytes 1572868
  21.1 11.4 %collective-permute-start = (f32[2,4,32,512]{3,2,1,0:T(8,128)S(1)}, f32[2,4,32,512]{3,2,1,0:T(8,128)S(1)}, u32[]{:S(2)}, u32[]{:S(2)}) collective-permute-start(f32[2,4,32,512]{3,2,1,0:T(8,128)S(1)} %copy.10.own_ref), channel_id=1, source_target_pairs={{0,1},{1,2},{2,3},{3,4},{4,5},{5,6},{6,7},{8,9},{9,10},{10,11},{11... | collective-permute-start | bytes 1572872 | tf_op jit(solution)/shard_map/ppermute | solution.py:116
  32.5 0.8 %copy-start.1 = (f32[2,4,32,512]{3,2,1,0:T(8,128)}, f32[2,4,32,512]{3,2,1,0:T(8,128)S(1)}, u32[]{:S(2)}) copy-start(f32[2,4,32,512]{3,2,1,0:T(8,128)S(1)} %collective-permute-done.left_ref) | copy-start | bytes 1572868

commit v2 on v1

--- a/solution.py
+++ b/solution.py
@@ -35,6 +35,7 @@
     layers_overall = layers * slabs
     knot_count = cmap_ref.shape[1]
     first_tile = lax.axis_index("region") == 0
+    me = lax.axis_index("depth")
     skew = skew_ref[0]
 
     order = []
@@ -42,7 +43,7 @@
         s = jnp.int32(0)
         for j in range(slabs):
             s = s + jnp.where(seq_ref[j] == k, j, 0)
-        order.append(s)
+        order.append((s - me + slabs) % slabs)
 
     for k in range(slabs):
         s = order[k]
@@ -112,7 +113,13 @@
     line = lax.broadcasted_iota(jnp.int32, (1, rows, 1), 1)
     marked = jnp.where(line < occupied_lines[0, 0], thermal_grid, EMPTY)
     blocks = marked.reshape(layers, slabs, share, width)
-    own = lax.all_to_all(blocks, "depth", split_axis=1, concat_axis=1, tiled=True)
+    me = lax.axis_index("depth")
+    held = [blocks[:, me]]
+    for m in range(1, slabs):
+        piece = lax.dynamic_index_in_dim(blocks, (me - m) % slabs, axis=1, keepdims=False)
+        route = [(i, (i - m) % slabs) for i in range(slabs)]
+        held.append(lax.ppermute(piece, "depth", route))
+    own = jnp.stack(held, axis=1)
     left = lax.ppermute(own, "region", [(i, i + 1) for i in range(regions - 1)])
     vmem = pltpu.VMEM
     smem = pltpu.SMEM

time: 39.9 us -> 35.3 us (0.88)
  the two profiles are of different devices: /device:TPU:4 before, /device:TPU:12 now
where the time goes in v2:
time: 35.3 us; the launch traced here: 35.1 us
  waiting for transfers between devices  18.7 us (53%)
  starting transfers between devices  6.59 us (19%)
  Pallas kernels  6.39 us (18%)
  between operations  1.36 us (4%)
  other arithmetic  1.19 us (3%)
  local copies, waits for them, and re-layouts  0.85 us (2%)
    ppermute x3, waiting for transfers between devices, shards(): held.append(lax.ppermute(piece, 'depth', route))  9.9 us
    ppermute x1, waiting for transfers between devices, shards(): left = lax.ppermute(own, 'region', [(i, i + 1) for i in range(regions - 1)])  8.82 us
    pallas_call x1, Pallas kernels, shards(): pl.pallas_call(render_kernel, out_shape=jax.ShapeDtypeStruct((4, share, w...  6.39 us
    ppermute x3, starting transfers between devices, shards(): held.append(lax.ppermute(piece, 'depth', route))  4.67 us
    ppermute x1, starting transfers between devices, shards(): left = lax.ppermute(own, 'region', [(i, i + 1) for i in range(regions - 1)])  1.92 us
    select_n x1, other arithmetic, shards(): marked = jnp.where(line < occupied_lines[0, 0], thermal_grid, EMPTY)  1.15 us
    unnamed x4, local copies, waits for them, and re-layouts  0.8 us
  transfers between devices with their start and end apart: 4, of which 4 were waited for; matrix products, arithmetic and copies ran while one was open for 0% of the time, Pallas kernels for 0%

profile of v2, /device:TPU:12, one launch (start us, length us, event | category | flops | bytes accessed | tf_op | source)
XLA Modules:
  0.0 35.1 jit_solution(1600945044184294469)
XLA Ops:
  0.7 1.2 %broadcast_select_fusion = f32[2,128,512]{2,1,0:T(8,128)S(1)} fusion(f32[2,128,512]{2,1,0:T(8,128)} %param.5, pred[128]{0:T(512)(128)(4,1)S(1)} %iota_compare_fusion), kind=kLoop, calls=%fused_computation.1 | loop fusion | flops 131072 | bytes 1048704 | tf_op jit(solution)/shard_map/jit(_where)/select_n | solution.py:114
  1.9 1.6 %collective-permute-start.2 = (f32[2,32,512]{2,1,0:T(8,128)S(1)}, f32[2,32,512]{2,1,0:T(8,128)S(1)}, u32[]{:S(2)}, u32[]{:S(2)}) collective-permute-start(f32[2,32,512]{2,1,0:T(8,128)S(1)} %get-tuple-element.6), channel_id=1, source_target_pairs={{0,8},{8,16},{16,24},{24,0},{1,9},{9,17},{17,25},{25,1},{2,10},{10... | collective-permute-start | bytes 393224 | tf_op jit(solution)/shard_map/ppermute | solution.py:121
  3.5 1.2 %collective-permute-start.1 = (f32[2,32,512]{2,1,0:T(8,128)S(1)}, f32[2,32,512]{2,1,0:T(8,128)S(1)}, u32[]{:S(2)}, u32[]{:S(2)}) collective-permute-start(f32[2,32,512]{2,1,0:T(8,128)S(1)} %get-tuple-element.7), channel_id=1, source_target_pairs={{0,16},{8,24},{16,0},{24,8},{1,17},{9,25},{17,1},{25,9},{2,18},{10... | collective-permute-start | bytes 393224 | tf_op jit(solution)/shard_map/ppermute | solution.py:121
  4.8 1.8 %collective-permute-start = (f32[2,32,512]{2,1,0:T(8,128)S(1)}, f32[2,32,512]{2,1,0:T(8,128)S(1)}, u32[]{:S(2)}, u32[]{:S(2)}) collective-permute-start(f32[2,32,512]{2,1,0:T(8,128)S(1)} %get-tuple-element.8), channel_id=1, source_target_pairs={{0,24},{8,0},{16,8},{24,16},{1,25},{9,1},{17,9},{25,17},{2,26},{10... | collective-permute-start | bytes 393224 | tf_op jit(solution)/shard_map/ppermute | solution.py:121
  6.6 6.5 %collective-permute-done.2 = f32[2,32,512]{2,1,0:T(8,128)S(1)} collective-permute-done((f32[2,32,512]{2,1,0:T(8,128)S(1)}, f32[2,32,512]{2,1,0:T(8,128)S(1)}, u32[]{:S(2)}, u32[]{:S(2)}) %collective-permute-start.2) | collective-permute-done | bytes 131104 | tf_op jit(solution)/shard_map/ppermute | solution.py:121
  13.0 1.7 %collective-permute-done.1 = f32[2,32,512]{2,1,0:T(8,128)S(1)} collective-permute-done((f32[2,32,512]{2,1,0:T(8,128)S(1)}, f32[2,32,512]{2,1,0:T(8,128)S(1)}, u32[]{:S(2)}, u32[]{:S(2)}) %collective-permute-start.1) | collective-permute-done | bytes 131104 | tf_op jit(solution)/shard_map/ppermute | solution.py:121
  14.7 1.8 %collective-permute-done = f32[2,32,512]{2,1,0:T(8,128)S(1)} collective-permute-done((f32[2,32,512]{2,1,0:T(8,128)S(1)}, f32[2,32,512]{2,1,0:T(8,128)S(1)}, u32[]{:S(2)}, u32[]{:S(2)}) %collective-permute-start) | collective-permute-done | bytes 131104 | tf_op jit(solution)/shard_map/ppermute | solution.py:121
  16.5 0.0 copy-start
  16.5 1.9 %collective-permute-start.3 = (f32[2,4,32,512]{3,2,1,0:T(8,128)S(1)}, f32[2,4,32,512]{3,2,1,0:T(8,128)S(1)}, u32[]{:S(2)}, u32[]{:S(2)}) collective-permute-start(f32[2,4,32,512]{3,2,1,0:T(8,128)S(1)} %pad_maximum_fusion.own_ref), channel_id=1, source_target_pairs={{0,1},{1,2},{2,3},{3,4},{4,5},{5,6},{6,7},{8,9},{9,10},{10,11},{11... | collective-permute-start | bytes 1572872 | tf_op jit(solution)/shard_map/ppermute | solution.py:123
  19.1 8.8 %collective-permute-done.3.left_ref = f32[2,4,32,512]{3,2,1,0:T(8,128)S(1)} collective-permute-done((f32[2,4,32,512]{3,2,1,0:T(8,128)S(1)}, f32[2,4,32,512]{3,2,1,0:T(8,128)S(1)}, u32[]{:S(2)}, u32[]{:S(2)}) %collective-permute-start.3) | collective-permute-done | bytes 524320 | tf_op jit(solution)/shard_map/ppermute | solution.py:123
  27.9 0.0 copy-done
  27.9 0.0 copy-start.1
  27.9 0.8 %copy-done.1 = f32[2,4,32,512]{3,2,1,0:T(8,128)} copy-done((f32[2,4,32,512]{3,2,1,0:T(8,128)}, f32[2,4,32,512]{3,2,1,0:T(8,128)S(1)}, u32[]{:S(2)}) %copy-start.1) | copy-done | bytes 524312
  28.7 6.4 %shard_map.55 = f32[4,32,512]{2,1,0:T(8,128)} custom-call(s32[4]{0:T(128)} %seq_ref.1, s32[1]{0:T(128)S(6)} %copy.7.skew_ref, f32[2,4,32,512]{3,2,1,0:T(8,128)} %copy-done, f32[2,4,32,512]{3,2,1,0:T(8,128)} %copy-done.1, f32[4,256]{1,0:T(4,128)} %cmap_ref.1), custom_call_target="tpu_custom_call" | custom-call | tf_op jit(solution)/shard_map/pallas_call | solution.py:126
  (3 shorter events, 0.1 us)
Async XLA Ops:
  1.9 11.1 %collective-permute-start.2 = (f32[2,32,512]{2,1,0:T(8,128)S(1)}, f32[2,32,512]{2,1,0:T(8,128)S(1)}, u32[]{:S(2)}, u32[]{:S(2)}) collective-permute-start(f32[2,32,512]{2,1,0:T(8,128)S(1)} %get-tuple-element.6), channel_id=1, source_target_pairs={{0,8},{8,16},{16,24},{24,0},{1,9},{9,17},{17,25},{25,1},{2,10},{10... | collective-permute-start | bytes 393224 | tf_op jit(solution)/shard_map/ppermute | solution.py:121
  3.5 11.2 %collective-permute-start.1 = (f32[2,32,512]{2,1,0:T(8,128)S(1)}, f32[2,32,512]{2,1,0:T(8,128)S(1)}, u32[]{:S(2)}, u32[]{:S(2)}) collective-permute-start(f32[2,32,512]{2,1,0:T(8,128)S(1)} %get-tuple-element.7), channel_id=1, source_target_pairs={{0,16},{8,24},{16,0},{24,8},{1,17},{9,25},{17,1},{25,9},{2,18},{10... | collective-permute-start | bytes 393224 | tf_op jit(solution)/shard_map/ppermute | solution.py:121
  4.8 11.7 %collective-permute-start = (f32[2,32,512]{2,1,0:T(8,128)S(1)}, f32[2,32,512]{2,1,0:T(8,128)S(1)}, u32[]{:S(2)}, u32[]{:S(2)}) collective-permute-start(f32[2,32,512]{2,1,0:T(8,128)S(1)} %get-tuple-element.8), channel_id=1, source_target_pairs={{0,24},{8,0},{16,8},{24,16},{1,25},{9,1},{17,9},{25,17},{2,26},{10... | collective-permute-start | bytes 393224 | tf_op jit(solution)/shard_map/ppermute | solution.py:121
  16.5 11.4 %copy-start = (f32[2,4,32,512]{3,2,1,0:T(8,128)}, f32[2,4,32,512]{3,2,1,0:T(8,128)S(1)}, u32[]{:S(2)}) copy-start(f32[2,4,32,512]{3,2,1,0:T(8,128)S(1)} %pad_maximum_fusion.own_ref) | copy-start | bytes 1572868
  16.5 11.4 %collective-permute-start.3 = (f32[2,4,32,512]{3,2,1,0:T(8,128)S(1)}, f32[2,4,32,512]{3,2,1,0:T(8,128)S(1)}, u32[]{:S(2)}, u32[]{:S(2)}) collective-permute-start(f32[2,4,32,512]{3,2,1,0:T(8,128)S(1)} %pad_maximum_fusion.own_ref), channel_id=1, source_target_pairs={{0,1},{1,2},{2,3},{3,4},{4,5},{5,6},{6,7},{8,9},{9,10},{10,11},{11... | collective-permute-start | bytes 1572872 | tf_op jit(solution)/shard_map/ppermute | solution.py:123
  27.9 0.8 %copy-start.1 = (f32[2,4,32,512]{3,2,1,0:T(8,128)}, f32[2,4,32,512]{3,2,1,0:T(8,128)S(1)}, u32[]{:S(2)}) copy-start(f32[2,4,32,512]{3,2,1,0:T(8,128)S(1)} %collective-permute-done.3.left_ref) | copy-start | bytes 1572868

commit v3 on v1

v3 whole, which is shorter than its diff:
```python
import functools

import jax
import jax.numpy as jnp
from jax import lax
from jax.experimental import pallas as pl
from jax.experimental.pallas import tpu as pltpu
from jax.sharding import PartitionSpec as P

EMPTY = 1.0e6
LANES = 128
SUBLANES = 8


def lookup(cells, tables, knot_count):
    scaled = jnp.clip((cells + 3.0) * ((knot_count - 1) / 6.0), 0.0, knot_count - 1.0)
    lower = jnp.minimum(jnp.floor(scaled), knot_count - 2.0)
    fraction = scaled - lower
    index = lower.astype(jnp.int32)
    upper_half = index >= LANES
    lane = jnp.where(upper_half, index - LANES, index)
    values = []
    for c in range(4):
        picked = []
        for base in (0, 8):
            low = jnp.take_along_axis(tables[base + 2 * c], lane, axis=1, mode="promise_in_bounds")
            high = jnp.take_along_axis(tables[base + 2 * c + 1], lane, axis=1, mode="promise_in_bounds")
            picked.append(jnp.where(upper_half, high, low))
        values.append(picked[0] + fraction * picked[1])
    return values


def slab_kernel(slot, seq_ref, skew_ref, own_ref, left_ref, cmap_ref, out_ref, shifted_ref):
    layers, rows, width = own_ref.shape
    slabs = seq_ref.shape[0]
    layers_overall = layers * slabs
    knot_count = cmap_ref.shape[1]
    first_tile = lax.axis_index("region") == 0
    rank = seq_ref[(lax.axis_index("depth") + slot) % slabs]
    skew = skew_ref[0]

    for l in range(layers):
        shift = ((rank * layers + l) * skew) // layers_overall
        for r in range(rows // SUBLANES):
            band = pl.ds(r * SUBLANES, SUBLANES)
            left = jnp.where(first_tile, EMPTY, left_ref[l, band, :])
            joined = jnp.concatenate([left, own_ref[l, band, :]], axis=1)
            shifted_ref[l, band, :] = pltpu.roll(joined, shift, 1)[:, width:]

    cmap = cmap_ref[...]
    following = pltpu.roll(cmap, knot_count - 1, 1)
    delta = following - cmap
    tables = []
    for src in (cmap, delta):
        for c in range(4):
            for h in range(knot_count // LANES):
                row = src[c : c + 1, h * LANES : (h + 1) * LANES]
                tables.append(jnp.broadcast_to(row, (SUBLANES, LANES)))

    pieces = width // LANES

    def block(i, carry):
        band = pl.ds(pl.multiple_of((i // pieces) * SUBLANES, SUBLANES), SUBLANES)
        cols = pl.ds(pl.multiple_of((i % pieces) * LANES, LANES), LANES)
        tau = None
        color = None
        for l in range(layers):
            cells = shifted_ref[l, band, cols]
            values = lookup(cells, tables, knot_count)
            absorb = jnp.where(cells < 100.0, values[3] * (6.0 / layers_overall), 0.0)
            opacity = 1.0 - jnp.exp(-absorb)
            emit = [values[c] * opacity for c in range(3)]
            if tau is None:
                color = emit
                tau = absorb
            else:
                fade = jnp.exp(-tau)
                color = [color[c] + fade * emit[c] for c in range(3)]
                tau = tau + absorb
        for c in range(3):
            out_ref[c, band, cols] = color[c]
        out_ref[3, band, cols] = tau
        return carry

    lax.fori_loop(0, (rows // SUBLANES) * pieces, block, 0)


def composite_kernel(seq_ref, *refs):
    parts, out_ref = refs[:-1], refs[-1]
    slabs = len(parts)
    me = lax.axis_index("depth")
    ranks = [seq_ref[(me + m) % slabs] for m in range(slabs)]
    _, rows, width = out_ref.shape
    pieces = width // LANES

    def block(i, carry):
        band = pl.ds(pl.multiple_of((i // pieces) * SUBLANES, SUBLANES), SUBLANES)
        cols = pl.ds(pl.multiple_of((i % pieces) * LANES, LANES), LANES)
        taus = [part[3, band, cols] for part in parts]
        image = [None] * 3
        total = None
        for m in range(slabs):
            prefix = None
            for j in range(slabs):
                if j == m:
                    continue
                term = jnp.where(ranks[j] < ranks[m], 1.0, 0.0) * taus[j]
                prefix = term if prefix is None else prefix + term
            fade = jnp.exp(-prefix) if prefix is not None else 1.0
            for c in range(3):
                shaded = fade * parts[m][c, band, cols]
                image[c] = shaded if image[c] is None else image[c] + shaded
            total = taus[m] if total is None else total + taus[m]
        for c in range(3):
            out_ref[c, band, cols] = image[c]
        out_ref[3, band, cols] = 1.0 - jnp.exp(-total)
        return carry

    lax.fori_loop(0, (rows // SUBLANES) * pieces, block, 0)


def shards(thermal_grid, colormap_samples, sheetgroup_viewer_sequence, occupied_lines, skew_offsets):
    layers, rows, width = thermal_grid.shape
    slabs = lax.axis_size("depth")
    regions = lax.axis_size("region")
    share = rows // slabs
    line = lax.broadcasted_iota(jnp.int32, (1, rows, 1), 1)
    marked = jnp.where(line < occupied_lines[0, 0], thermal_grid, EMPTY)
    blocks = marked.reshape(layers, slabs, share, width)
    me = lax.axis_index("depth")
    to_right = [(i, i + 1) for i in range(regions - 1)]
    smem = pl.BlockSpec(memory_space=pltpu.SMEM)
    vmem = pl.BlockSpec(memory_space=pltpu.VMEM)
    slab_parts = []
    for m in range(slabs):
        piece = lax.dynamic_index_in_dim(blocks, (me - m) % slabs, axis=1, keepdims=False)
        if m > 0:
            piece = lax.ppermute(piece, "depth", [(i, (i - m) % slabs) for i in range(slabs)])
        left = lax.ppermute(piece, "region", to_right)
        slab_parts.append(
            pl.pallas_call(
                functools.partial(slab_kernel, m),
                out_shape=jax.ShapeDtypeStruct((4, share, width), jnp.float32),
                in_specs=[smem, smem, vmem, vmem, vmem],
                out_specs=vmem,
                scratch_shapes=[pltpu.VMEM((layers, share, width), jnp.float32)],
            )(sheetgroup_viewer_sequence, skew_offsets, piece, left, colormap_samples)
        )
    return pl.pallas_call(
        composite_kernel,
        out_shape=jax.ShapeDtypeStruct((4, share, width), jnp.float32),
        in_specs=[smem] + [vmem] * slabs,
        out_specs=vmem,
    )(sheetgroup_viewer_sequence, *slab_parts)


def solution(mesh):
    in_specs = (P("depth", None, "region"), P(), P(), P("depth", "region"), P())
    out_specs = P(None, "depth", "region")
    return jax.shard_map(shards, mesh=mesh, in_specs=in_specs, out_specs=out_specs, check_vma=False)
```

time: 39.9 us -> 45.4 us (1.14)
  the two profiles are of different devices: /device:TPU:4 before, /device:TPU:17 now
where the time goes in v3:
time: 45.4 us; the launch traced here: 45.1 us
  starting transfers between devices  21.1 us (46%)
  Pallas kernels  18.6 us (41%)
  local copies, waits for them, and re-layouts  2.67 us (6%)
  between operations  1.48 us (3%)
  other arithmetic  1.16 us (3%)
    ppermute x4, starting transfers between devices, shards(): left = lax.ppermute(piece, 'region', to_right)  18.5 us
    pallas_call x4, Pallas kernels, shards(): pl.pallas_call(functools.partial(slab_kernel, m), out_shape=jax.ShapeDtyp...  16.2 us
    unnamed x16, local copies, waits for them, and re-layouts  2.62 us
    ppermute x3, starting transfers between devices, shards(): lax.ppermute(piece, 'depth', [(i, (i - m) % slabs) for i in range(slabs)])  2.61 us
    pallas_call x1, Pallas kernels, shards(): pl.pallas_call(composite_kernel, out_shape=jax.ShapeDtypeStruct((4, share...  2.42 us
    select_n x1, other arithmetic, shards(): marked = jnp.where(line < occupied_lines[0, 0], thermal_grid, EMPTY)  1.15 us
  transfers between devices with their start and end apart: 7, of which 0 were waited for; matrix products, arithmetic and copies ran while one was open for 0% of the time, Pallas kernels for 27%

profile of v3, /device:TPU:17, one launch (start us, length us, event | category | flops | bytes accessed | tf_op | source)
XLA Modules:
  0.0 45.1 jit_solution(14062024245504498056)
XLA Ops:
  0.7 1.2 %broadcast_select_fusion = f32[2,128,512]{2,1,0:T(8,128)S(1)} fusion(f32[2,128,512]{2,1,0:T(8,128)} %param.5, pred[128]{0:T(512)(128)(4,1)S(1)} %iota_compare_fusion), kind=kLoop, calls=%fused_computation | loop fusion | flops 131072 | bytes 1048704 | tf_op jit(solution)/shard_map/jit(_where)/select_n | solution.py:128
  1.9 0.0 copy-start
  1.9 1.3 %collective-permute-start.5 = (f32[2,32,512]{2,1,0:T(8,128)S(1)}, f32[2,32,512]{2,1,0:T(8,128)S(1)}, u32[]{:S(2)}, u32[]{:S(2)}) collective-permute-start(f32[2,32,512]{2,1,0:T(8,128)S(1)} %get-tuple-element.5), channel_id=1, source_target_pairs={{0,8},{8,16},{16,24},{24,0},{1,9},{9,17},{17,25},{25,1},{2,10},{10... | collective-permute-start | bytes 393224 | tf_op jit(solution)/shard_map/ppermute | solution.py:138
  3.3 0.1 collective-permute-start.3
  3.3 1.2 %collective-permute-start.1 = (f32[2,32,512]{2,1,0:T(8,128)S(1)}, f32[2,32,512]{2,1,0:T(8,128)S(1)}, u32[]{:S(2)}, u32[]{:S(2)}) collective-permute-start(f32[2,32,512]{2,1,0:T(8,128)S(1)} %get-tuple-element.7), channel_id=1, source_target_pairs={{0,24},{8,0},{16,8},{24,16},{1,25},{9,1},{17,9},{25,17},{2,26},{10... | collective-permute-start | bytes 393224 | tf_op jit(solution)/shard_map/ppermute | solution.py:138
  4.5 4.4 %collective-permute-start = (f32[2,32,512]{2,1,0:T(8,128)S(1)}, f32[2,32,512]{2,1,0:T(8,128)S(1)}, u32[]{:S(2)}, u32[]{:S(2)}) collective-permute-start(f32[2,32,512]{2,1,0:T(8,128)S(1)} %get-tuple-element.8.own_ref), channel_id=1, source_target_pairs={{0,1},{1,2},{2,3},{3,4},{4,5},{5,6},{6,7},{8,9},{9,10},{10,11},{11... | collective-permute-start | bytes 393224 | tf_op jit(solution)/shard_map/ppermute | solution.py:139
  8.9 0.0 collective-permute-done.5.own_ref
  8.9 0.0 copy-start.3
  8.9 8.7 %collective-permute-start.6 = (f32[2,32,512]{2,1,0:T(8,128)S(1)}, f32[2,32,512]{2,1,0:T(8,128)S(1)}, u32[]{:S(2)}, u32[]{:S(2)}) collective-permute-start(f32[2,32,512]{2,1,0:T(8,128)S(1)} %collective-permute-done.5.own_ref), channel_id=1, source_target_pairs={{0,1},{1,2},{2,3},{3,4},{4,5},{5,6},{6,7},{8,9},{9,10},{10,11},{11... | collective-permute-start | bytes 393224 | tf_op jit(solution)/shard_map/ppermute | solution.py:139
  17.6 0.0 collective-permute-done.3.own_ref
  17.7 0.0 copy-start.2
  17.7 1.9 %collective-permute-start.4 = (f32[2,32,512]{2,1,0:T(8,128)S(1)}, f32[2,32,512]{2,1,0:T(8,128)S(1)}, u32[]{:S(2)}, u32[]{:S(2)}) collective-permute-start(f32[2,32,512]{2,1,0:T(8,128)S(1)} %collective-permute-done.3.own_ref), channel_id=1, source_target_pairs={{0,1},{1,2},{2,3},{3,4},{4,5},{5,6},{6,7},{8,9},{9,10},{10,11},{11... | collective-permute-start | bytes 393224 | tf_op jit(solution)/shard_map/ppermute | solution.py:139
  19.6 0.0 collective-permute-done.1.own_ref
  19.6 0.0 copy-start.1
  19.6 3.5 %collective-permute-start.2 = (f32[2,32,512]{2,1,0:T(8,128)S(1)}, f32[2,32,512]{2,1,0:T(8,128)S(1)}, u32[]{:S(2)}, u32[]{:S(2)}) collective-permute-start(f32[2,32,512]{2,1,0:T(8,128)S(1)} %collective-permute-done.1.own_ref), channel_id=1, source_target_pairs={{0,1},{1,2},{2,3},{3,4},{4,5},{5,6},{6,7},{8,9},{9,10},{10,11},{11... | collective-permute-start | bytes 393224 | tf_op jit(solution)/shard_map/ppermute | solution.py:139
  23.8 0.0 collective-permute-done.left_ref
  23.8 0.0 copy-done
  23.8 0.0 copy-start.4
  23.8 0.6 %copy-done.4 = f32[2,32,512]{2,1,0:T(8,128)} copy-done((f32[2,32,512]{2,1,0:T(8,128)}, f32[2,32,512]{2,1,0:T(8,128)S(1)}, u32[]{:S(2)}) %copy-start.4) | copy-done | bytes 131096
  24.4 4.0 %shard_map.55.refs_0_ = f32[4,32,512]{2,1,0:T(8,128)} custom-call(s32[4]{0:T(128)} %seq_ref.9, s32[1]{0:T(128)S(6)} %copy.15.skew_ref, f32[2,32,512]{2,1,0:T(8,128)} %copy-done, f32[2,32,512]{2,1,0:T(8,128)} %copy-done.4, f32[4,256]{1,0:T(4,128)} %cmap_ref.7), custom_call_target="tpu_custom_call" | custom-call | tf_op jit(solution)/shard_map/pallas_call | solution.py:141
  28.5 0.0 copy-done.3
  28.5 0.0 copy-done.2
  28.5 0.0 copy-done.1
  28.5 0.0 collective-permute-done.6.left_ref
  28.5 0.0 copy-start.5
  28.5 0.6 %copy-done.5 = f32[2,32,512]{2,1,0:T(8,128)} copy-done((f32[2,32,512]{2,1,0:T(8,128)}, f32[2,32,512]{2,1,0:T(8,128)S(1)}, u32[]{:S(2)}) %copy-start.5) | copy-done | bytes 131096
  29.2 4.0 %shard_map.58.refs_3_ = f32[4,32,512]{2,1,0:T(8,128)} custom-call(s32[4]{0:T(128)} %seq_ref.9, s32[1]{0:T(128)S(6)} %copy.15.skew_ref, f32[2,32,512]{2,1,0:T(8,128)} %copy-done.3, f32[2,32,512]{2,1,0:T(8,128)} %copy-done.5, f32[4,256]{1,0:T(4,128)} %cmap_ref.7), custom_call_target="tpu_custom_call" | custom-call | tf_op jit(solution)/shard_map/pallas_call | solution.py:141
  33.2 0.0 collective-permute-done.4.left_ref
  33.2 0.0 copy-start.6
  33.2 0.7 %copy-done.6 = f32[2,32,512]{2,1,0:T(8,128)} copy-done((f32[2,32,512]{2,1,0:T(8,128)}, f32[2,32,512]{2,1,0:T(8,128)S(1)}, u32[]{:S(2)}) %copy-start.6) | copy-done | bytes 131096
  33.9 4.1 %shard_map.57.refs_2_ = f32[4,32,512]{2,1,0:T(8,128)} custom-call(s32[4]{0:T(128)} %seq_ref.9, s32[1]{0:T(128)S(6)} %copy.15.skew_ref, f32[2,32,512]{2,1,0:T(8,128)} %copy-done.2, f32[2,32,512]{2,1,0:T(8,128)} %copy-done.6, f32[4,256]{1,0:T(4,128)} %cmap_ref.7), custom_call_target="tpu_custom_call" | custom-call | tf_op jit(solution)/shard_map/pallas_call | solution.py:141
  37.9 0.0 collective-permute-done.2.left_ref
  37.9 0.0 copy-start.7
  37.9 0.7 %copy-done.7 = f32[2,32,512]{2,1,0:T(8,128)} copy-done((f32[2,32,512]{2,1,0:T(8,128)}, f32[2,32,512]{2,1,0:T(8,128)S(1)}, u32[]{:S(2)}) %copy-start.7) | copy-done | bytes 131096
  38.6 4.1 %shard_map.56.refs_1_ = f32[4,32,512]{2,1,0:T(8,128)} custom-call(s32[4]{0:T(128)} %seq_ref.9, s32[1]{0:T(128)S(6)} %copy.15.skew_ref, f32[2,32,512]{2,1,0:T(8,128)} %copy-done.1, f32[2,32,512]{2,1,0:T(8,128)} %copy-done.7, f32[4,256]{1,0:T(4,128)} %cmap_ref.7), custom_call_target="tpu_custom_call" | custom-call | tf_op jit(solution)/shard_map/pallas_call | solution.py:141
  42.7 2.4 %shard_map.59 = f32[4,32,512]{2,1,0:T(8,128)} custom-call(s32[4]{0:T(128)} %seq_ref.9, f32[4,32,512]{2,1,0:T(8,128)} %shard_map.55.refs_0_, f32[4,32,512]{2,1,0:T(8,128)} %shard_map.56.refs_1_, f32[4,32,512]{2,1,0:T(8,128)} %shard_map.57.refs_2_, f32[4,32,512]{2,1,0:T(8,128)} %shard_map.58.refs_3_), custom_call_target="tpu_custom_call" | custom-call | tf_op jit(solution)/shard_map/pallas_call | solution.py:149
  (2 shorter events, 0.1 us)
Async XLA Ops:
  1.9 21.9 %copy-start = (f32[2,32,512]{2,1,0:T(8,128)}, f32[2,32,512]{2,1,0:T(8,128)S(1)}, u32[]{:S(2)}) copy-start(f32[2,32,512]{2,1,0:T(8,128)S(1)} %get-tuple-element.8.own_ref) | copy-start | bytes 393220
  1.9 7.0 %collective-permute-start.5 = (f32[2,32,512]{2,1,0:T(8,128)S(1)}, f32[2,32,512]{2,1,0:T(8,128)S(1)}, u32[]{:S(2)}, u32[]{:S(2)}) collective-permute-start(f32[2,32,512]{2,1,0:T(8,128)S(1)} %get-tuple-element.5), channel_id=1, source_target_pairs={{0,8},{8,16},{16,24},{24,0},{1,9},{9,17},{17,25},{25,1},{2,10},{10... | collective-permute-start | bytes 393224 | tf_op jit(solution)/shard_map/ppermute | solution.py:138
  3.3 14.4 %collective-permute-start.3 = (f32[2,32,512]{2,1,0:T(8,128)S(1)}, f32[2,32,512]{2,1,0:T(8,128)S(1)}, u32[]{:S(2)}, u32[]{:S(2)}) collective-permute-start(f32[2,32,512]{2,1,0:T(8,128)S(1)} %get-tuple-element.6), channel_id=1, source_target_pairs={{0,16},{8,24},{16,0},{24,8},{1,17},{9,25},{17,1},{25,9},{2,18},{10... | collective-permute-start | bytes 393224 | tf_op jit(solution)/shard_map/ppermute | solution.py:138
  3.3 16.3 %collective-permute-start.1 = (f32[2,32,512]{2,1,0:T(8,128)S(1)}, f32[2,32,512]{2,1,0:T(8,128)S(1)}, u32[]{:S(2)}, u32[]{:S(2)}) collective-permute-start(f32[2,32,512]{2,1,0:T(8,128)S(1)} %get-tuple-element.7), channel_id=1, source_target_pairs={{0,24},{8,0},{16,8},{24,16},{1,25},{9,1},{17,9},{25,17},{2,26},{10... | collective-permute-start | bytes 393224 | tf_op jit(solution)/shard_map/ppermute | solution.py:138
  4.5 19.3 %collective-permute-start = (f32[2,32,512]{2,1,0:T(8,128)S(1)}, f32[2,32,512]{2,1,0:T(8,128)S(1)}, u32[]{:S(2)}, u32[]{:S(2)}) collective-permute-start(f32[2,32,512]{2,1,0:T(8,128)S(1)} %get-tuple-element.8.own_ref), channel_id=1, source_target_pairs={{0,1},{1,2},{2,3},{3,4},{4,5},{5,6},{6,7},{8,9},{9,10},{10,11},{11... | collective-permute-start | bytes 393224 | tf_op jit(solution)/shard_map/ppermute | solution.py:139
  8.9 19.6 %copy-start.3 = (f32[2,32,512]{2,1,0:T(8,128)}, f32[2,32,512]{2,1,0:T(8,128)S(1)}, u32[]{:S(2)}) copy-start(f32[2,32,512]{2,1,0:T(8,128)S(1)} %collective-permute-done.5.own_ref) | copy-start | bytes 393220
  8.9 19.6 %collective-permute-start.6 = (f32[2,32,512]{2,1,0:T(8,128)S(1)}, f32[2,32,512]{2,1,0:T(8,128)S(1)}, u32[]{:S(2)}, u32[]{:S(2)}) collective-permute-start(f32[2,32,512]{2,1,0:T(8,128)S(1)} %collective-permute-done.5.own_ref), channel_id=1, source_target_pairs={{0,1},{1,2},{2,3},{3,4},{4,5},{5,6},{6,7},{8,9},{9,10},{10,11},{11... | collective-permute-start | bytes 393224 | tf_op jit(solution)/shard_map/ppermute | solution.py:139
  17.7 10.8 %copy-start.2 = (f32[2,32,512]{2,1,0:T(8,128)}, f32[2,32,512]{2,1,0:T(8,128)S(1)}, u32[]{:S(2)}) copy-start(f32[2,32,512]{2,1,0:T(8,128)S(1)} %collective-permute-done.3.own_ref) | copy-start | bytes 393220
  17.7 15.5 %collective-permute-start.4 = (f32[2,32,512]{2,1,0:T(8,128)S(1)}, f32[2,32,512]{2,1,0:T(8,128)S(1)}, u32[]{:S(2)}, u32[]{:S(2)}) collective-permute-start(f32[2,32,512]{2,1,0:T(8,128)S(1)} %collective-permute-done.3.own_ref), channel_id=1, source_target_pairs={{0,1},{1,2},{2,3},{3,4},{4,5},{5,6},{6,7},{8,9},{9,10},{10,11},{11... | collective-permute-start | bytes 393224 | tf_op jit(solution)/shard_map/ppermute | solution.py:139
  19.6 8.9 %copy-start.1 = (f32[2,32,512]{2,1,0:T(8,128)}, f32[2,32,512]{2,1,0:T(8,128)S(1)}, u32[]{:S(2)}) copy-start(f32[2,32,512]{2,1,0:T(8,128)S(1)} %collective-permute-done.1.own_ref) | copy-start | bytes 393220
  19.6 18.3 %collective-permute-start.2 = (f32[2,32,512]{2,1,0:T(8,128)S(1)}, f32[2,32,512]{2,1,0:T(8,128)S(1)}, u32[]{:S(2)}, u32[]{:S(2)}) collective-permute-start(f32[2,32,512]{2,1,0:T(8,128)S(1)} %collective-permute-done.1.own_ref), channel_id=1, source_target_pairs={{0,1},{1,2},{2,3},{3,4},{4,5},{5,6},{6,7},{8,9},{9,10},{10,11},{11... | collective-permute-start | bytes 393224 | tf_op jit(solution)/shard_map/ppermute | solution.py:139
  23.8 0.7 %copy-start.4 = (f32[2,32,512]{2,1,0:T(8,128)}, f32[2,32,512]{2,1,0:T(8,128)S(1)}, u32[]{:S(2)}) copy-start(f32[2,32,512]{2,1,0:T(8,128)S(1)} %collective-permute-done.left_ref) | copy-start | bytes 393220
  28.5 0.7 %copy-start.5 = (f32[2,32,512]{2,1,0:T(8,128)}, f32[2,32,512]{2,1,0:T(8,128)S(1)}, u32[]{:S(2)}) copy-start(f32[2,32,512]{2,1,0:T(8,128)S(1)} %collective-permute-done.6.left_ref) | copy-start | bytes 393220
  33.2 0.7 %copy-start.6 = (f32[2,32,512]{2,1,0:T(8,128)}, f32[2,32,512]{2,1,0:T(8,128)S(1)}, u32[]{:S(2)}) copy-start(f32[2,32,512]{2,1,0:T(8,128)S(1)} %collective-permute-done.4.left_ref) | copy-start | bytes 393220
  37.9 0.7 %copy-start.7 = (f32[2,32,512]{2,1,0:T(8,128)}, f32[2,32,512]{2,1,0:T(8,128)S(1)}, u32[]{:S(2)}) copy-start(f32[2,32,512]{2,1,0:T(8,128)S(1)} %collective-permute-done.2.left_ref) | copy-start | bytes 393220

commit v4 on v2

--- a/solution.py
+++ b/solution.py
@@ -110,15 +110,16 @@
     slabs = lax.axis_size("depth")
     regions = lax.axis_size("region")
     share = rows // slabs
-    line = lax.broadcasted_iota(jnp.int32, (1, rows, 1), 1)
-    marked = jnp.where(line < occupied_lines[0, 0], thermal_grid, EMPTY)
-    blocks = marked.reshape(layers, slabs, share, width)
     me = lax.axis_index("depth")
-    held = [blocks[:, me]]
-    for m in range(1, slabs):
-        piece = lax.dynamic_index_in_dim(blocks, (me - m) % slabs, axis=1, keepdims=False)
-        route = [(i, (i - m) % slabs) for i in range(slabs)]
-        held.append(lax.ppermute(piece, "depth", route))
+    line = lax.broadcasted_iota(jnp.int32, (1, share, 1), 1)
+    held = []
+    for m in range(slabs):
+        start = ((me - m) % slabs) * share
+        piece = lax.dynamic_slice_in_dim(thermal_grid, start, share, axis=1)
+        piece = jnp.where(start + line < occupied_lines[0, 0], piece, EMPTY)
+        if m > 0:
+            piece = lax.ppermute(piece, "depth", [(i, (i - m) % slabs) for i in range(slabs)])
+        held.append(piece)
     own = jnp.stack(held, axis=1)
     left = lax.ppermute(own, "region", [(i, i + 1) for i in range(regions - 1)])
     vmem = pltpu.VMEM

time: 35.3 us -> 35.9 us (1.017)
  the two profiles are of different devices: /device:TPU:12 before, /device:TPU:4 now
where the time goes in v4:
time: 35.9 us; the launch traced here: 35.7 us
  waiting for transfers between devices  19.3 us (54%)
  starting transfers between devices  6.59 us (18%)
  Pallas kernels  6.39 us (18%)
  between operations  1.37 us (4%)
  other arithmetic  1.27 us (4%)
  local copies, waits for them, and re-layouts  0.8 us (2%)
    ppermute x3, waiting for transfers between devices, shards(): lax.ppermute(piece, 'depth', [(i, (i - m) % slabs) for i in range(slabs)])  10.5 us
    ppermute x1, waiting for transfers between devices, shards(): left = lax.ppermute(own, 'region', [(i, i + 1) for i in range(regions - 1)])  8.82 us
    pallas_call x1, Pallas kernels, shards(): pl.pallas_call(render_kernel, out_shape=jax.ShapeDtypeStruct((4, share, w...  6.39 us
    ppermute x3, starting transfers between devices, shards(): lax.ppermute(piece, 'depth', [(i, (i - m) % slabs) for i in range(slabs)])  4.67 us
    ppermute x1, starting transfers between devices, shards(): left = lax.ppermute(own, 'region', [(i, i + 1) for i in range(regions - 1)])  1.92 us
    another operation x2, other arithmetic, shards(): own = jnp.stack(held, axis=1)  1.26 us
    unnamed x4, local copies, waits for them, and re-layouts  0.8 us
  transfers between devices with their start and end apart: 4, of which 4 were waited for; matrix products, arithmetic and copies ran while one was open for 0% of the time, Pallas kernels for 0%

profile of v4, /device:TPU:4, one launch (start us, length us, event | category | flops | bytes accessed | tf_op | source)
XLA Modules:
  0.0 35.7 jit_solution(2103951896842165522)
XLA Ops:
  0.7 1.2 %select_bitcast_fusion = (f32[2,1,32,512]{3,2,1,0:T(8,128)S(1)}, f32[2,32,512]{2,1,0:T(8,128)S(1)}, f32[2,32,512]{2,1,0:T(8,128)S(1)}, f32[2,32,512]{2,1,0:T(8,128)S(1)}) fusion(f32[2,128,512]{2,1,0:T(8,128)} %param.5, s32[]{:T(128)S(6)} %select_n.45, pred[32]{0:T(512)(128)(4,1)S(1)} %get-tuple-element.12, s32[]{:T(128)S(6)} %select_n.48, ...), kind=kLoop, calls=%fused_computation.4 | loop fusion | flops 131072 | bytes 1048720 | tf_op jit(solution)/shard_map/stack | solution.py:123
  1.9 3.7 %collective-permute-start = (f32[2,32,512]{2,1,0:T(8,128)S(1)}, f32[2,32,512]{2,1,0:T(8,128)S(1)}, u32[]{:S(2)}, u32[]{:S(2)}) collective-permute-start(f32[2,32,512]{2,1,0:T(8,128)S(1)} %get-tuple-element.6), channel_id=1, source_target_pairs={{0,24},{8,0},{16,8},{24,16},{1,25},{9,1},{17,9},{25,17},{2,26},{10... | collective-permute-start | bytes 393224 | tf_op jit(solution)/shard_map/ppermute | solution.py:121
  5.6 0.0 collective-permute-start.2
  5.6 1.0 %collective-permute-start.1 = (f32[2,32,512]{2,1,0:T(8,128)S(1)}, f32[2,32,512]{2,1,0:T(8,128)S(1)}, u32[]{:S(2)}, u32[]{:S(2)}) collective-permute-start(f32[2,32,512]{2,1,0:T(8,128)S(1)} %get-tuple-element.8), channel_id=1, source_target_pairs={{0,16},{8,24},{16,0},{24,8},{1,17},{9,25},{17,1},{25,9},{2,18},{10... | collective-permute-start | bytes 393224 | tf_op jit(solution)/shard_map/ppermute | solution.py:121
  6.6 2.9 %collective-permute-done = f32[2,32,512]{2,1,0:T(8,128)S(1)} collective-permute-done((f32[2,32,512]{2,1,0:T(8,128)S(1)}, f32[2,32,512]{2,1,0:T(8,128)S(1)}, u32[]{:S(2)}, u32[]{:S(2)}) %collective-permute-start) | collective-permute-done | bytes 131104 | tf_op jit(solution)/shard_map/ppermute | solution.py:121
  9.5 4.4 %collective-permute-done.2 = f32[2,32,512]{2,1,0:T(8,128)S(1)} collective-permute-done((f32[2,32,512]{2,1,0:T(8,128)S(1)}, f32[2,32,512]{2,1,0:T(8,128)S(1)}, u32[]{:S(2)}, u32[]{:S(2)}) %collective-permute-start.2) | collective-permute-done | bytes 131104 | tf_op jit(solution)/shard_map/ppermute | solution.py:121
  13.9 3.2 %collective-permute-done.1 = f32[2,32,512]{2,1,0:T(8,128)S(1)} collective-permute-done((f32[2,32,512]{2,1,0:T(8,128)S(1)}, f32[2,32,512]{2,1,0:T(8,128)S(1)}, u32[]{:S(2)}, u32[]{:S(2)}) %collective-permute-start.1) | collective-permute-done | bytes 131104 | tf_op jit(solution)/shard_map/ppermute | solution.py:121
  17.1 0.0 copy-start
  17.1 1.9 %collective-permute-start.3 = (f32[2,4,32,512]{3,2,1,0:T(8,128)S(1)}, f32[2,4,32,512]{3,2,1,0:T(8,128)S(1)}, u32[]{:S(2)}, u32[]{:S(2)}) collective-permute-start(f32[2,4,32,512]{3,2,1,0:T(8,128)S(1)} %pad_maximum_fusion.own_ref), channel_id=1, source_target_pairs={{0,1},{1,2},{2,3},{3,4},{4,5},{5,6},{6,7},{8,9},{9,10},{10,11},{11... | collective-permute-start | bytes 1572872 | tf_op jit(solution)/shard_map/ppermute | solution.py:124
  19.7 8.8 %collective-permute-done.3.left_ref = f32[2,4,32,512]{3,2,1,0:T(8,128)S(1)} collective-permute-done((f32[2,4,32,512]{3,2,1,0:T(8,128)S(1)}, f32[2,4,32,512]{3,2,1,0:T(8,128)S(1)}, u32[]{:S(2)}, u32[]{:S(2)}) %collective-permute-start.3) | collective-permute-done | bytes 524320 | tf_op jit(solution)/shard_map/ppermute | solution.py:124
  28.5 0.0 copy-done
  28.5 0.0 copy-start.1
  28.5 0.8 %copy-done.1 = f32[2,4,32,512]{3,2,1,0:T(8,128)} copy-done((f32[2,4,32,512]{3,2,1,0:T(8,128)}, f32[2,4,32,512]{3,2,1,0:T(8,128)S(1)}, u32[]{:S(2)}) %copy-start.1) | copy-done | bytes 524312
  29.3 6.4 %shard_map.55 = f32[4,32,512]{2,1,0:T(8,128)} custom-call(s32[4]{0:T(128)} %seq_ref.1, s32[1]{0:T(128)S(6)} %copy.10.skew_ref, f32[2,4,32,512]{3,2,1,0:T(8,128)} %copy-done, f32[2,4,32,512]{3,2,1,0:T(8,128)} %copy-done.1, f32[4,256]{1,0:T(4,128)} %cmap_ref.1), custom_call_target="tpu_custom_call" | custom-call | tf_op jit(solution)/shard_map/pallas_call | solution.py:127
  (3 shorter events, 0.1 us)
Async XLA Ops:
  1.9 7.6 %collective-permute-start = (f32[2,32,512]{2,1,0:T(8,128)S(1)}, f32[2,32,512]{2,1,0:T(8,128)S(1)}, u32[]{:S(2)}, u32[]{:S(2)}) collective-permute-start(f32[2,32,512]{2,1,0:T(8,128)S(1)} %get-tuple-element.6), channel_id=1, source_target_pairs={{0,24},{8,0},{16,8},{24,16},{1,25},{9,1},{17,9},{25,17},{2,26},{10... | collective-permute-start | bytes 393224 | tf_op jit(solution)/shard_map/ppermute | solution.py:121
  5.6 8.3 %collective-permute-start.2 = (f32[2,32,512]{2,1,0:T(8,128)S(1)}, f32[2,32,512]{2,1,0:T(8,128)S(1)}, u32[]{:S(2)}, u32[]{:S(2)}) collective-permute-start(f32[2,32,512]{2,1,0:T(8,128)S(1)} %get-tuple-element.7), channel_id=1, source_target_pairs={{0,8},{8,16},{16,24},{24,0},{1,9},{9,17},{17,25},{25,1},{2,10},{10... | collective-permute-start | bytes 393224 | tf_op jit(solution)/shard_map/ppermute | solution.py:121
  5.6 11.5 %collective-permute-start.1 = (f32[2,32,512]{2,1,0:T(8,128)S(1)}, f32[2,32,512]{2,1,0:T(8,128)S(1)}, u32[]{:S(2)}, u32[]{:S(2)}) collective-permute-start(f32[2,32,512]{2,1,0:T(8,128)S(1)} %get-tuple-element.8), channel_id=1, source_target_pairs={{0,16},{8,24},{16,0},{24,8},{1,17},{9,25},{17,1},{25,9},{2,18},{10... | collective-permute-start | bytes 393224 | tf_op jit(solution)/shard_map/ppermute | solution.py:121
  17.1 11.4 %copy-start = (f32[2,4,32,512]{3,2,1,0:T(8,128)}, f32[2,4,32,512]{3,2,1,0:T(8,128)S(1)}, u32[]{:S(2)}) copy-start(f32[2,4,32,512]{3,2,1,0:T(8,128)S(1)} %pad_maximum_fusion.own_ref) | copy-start | bytes 1572868
  17.1 11.4 %collective-permute-start.3 = (f32[2,4,32,512]{3,2,1,0:T(8,128)S(1)}, f32[2,4,32,512]{3,2,1,0:T(8,128)S(1)}, u32[]{:S(2)}, u32[]{:S(2)}) collective-permute-start(f32[2,4,32,512]{3,2,1,0:T(8,128)S(1)} %pad_maximum_fusion.own_ref), channel_id=1, source_target_pairs={{0,1},{1,2},{2,3},{3,4},{4,5},{5,6},{6,7},{8,9},{9,10},{10,11},{11... | collective-permute-start | bytes 1572872 | tf_op jit(solution)/shard_map/ppermute | solution.py:124
  28.5 0.8 %copy-start.1 = (f32[2,4,32,512]{3,2,1,0:T(8,128)}, f32[2,4,32,512]{3,2,1,0:T(8,128)S(1)}, u32[]{:S(2)}) copy-start(f32[2,4,32,512]{3,2,1,0:T(8,128)S(1)} %collective-permute-done.3.left_ref) | copy-start | bytes 1572868

commit v5 on v1

--- a/solution.py
+++ b/solution.py
@@ -30,11 +30,16 @@
     return values
 
 
-def render_kernel(seq_ref, skew_ref, own_ref, left_ref, cmap_ref, out_ref, shifted_ref):
-    layers, slabs, rows, width = own_ref.shape
+def render_kernel(seq_ref, skew_ref, *refs):
+    halves = (len(refs) - 3) // 2
+    own_refs, left_refs = refs[:halves], refs[halves : 2 * halves]
+    cmap_ref, out_ref, shifted_ref = refs[2 * halves :]
+    layers, slabs, half_rows, width = own_refs[0].shape
+    rows = half_rows * halves
     layers_overall = layers * slabs
     knot_count = cmap_ref.shape[1]
     first_tile = lax.axis_index("region") == 0
+    me = lax.axis_index("depth")
     skew = skew_ref[0]
 
     order = []
@@ -42,7 +47,7 @@
         s = jnp.int32(0)
         for j in range(slabs):
             s = s + jnp.where(seq_ref[j] == k, j, 0)
-        order.append(s)
+        order.append((s - me + slabs) % slabs)
 
     for k in range(slabs):
         s = order[k]
@@ -50,8 +55,10 @@
             shift = ((k * layers + l) * skew) // layers_overall
             for r in range(rows // SUBLANES):
                 band = pl.ds(r * SUBLANES, SUBLANES)
-                left = jnp.where(first_tile, EMPTY, left_ref[l, s, band, :])
-                joined = jnp.concatenate([left, own_ref[l, s, band, :]], axis=1)
+                c, rest = divmod(r * SUBLANES, half_rows)
+                part = pl.ds(rest, SUBLANES)
+                left = jnp.where(first_tile, EMPTY, left_refs[c][l, s, part, :])
+                joined = jnp.concatenate([left, own_refs[c][l, s, part, :]], axis=1)
                 shifted_ref[l, k, band, :] = pltpu.roll(joined, shift, 1)[:, width:]
 
     cmap = cmap_ref[...]
@@ -109,11 +116,23 @@
     slabs = lax.axis_size("depth")
     regions = lax.axis_size("region")
     share = rows // slabs
-    line = lax.broadcasted_iota(jnp.int32, (1, rows, 1), 1)
-    marked = jnp.where(line < occupied_lines[0, 0], thermal_grid, EMPTY)
-    blocks = marked.reshape(layers, slabs, share, width)
-    own = lax.all_to_all(blocks, "depth", split_axis=1, concat_axis=1, tiled=True)
-    left = lax.ppermute(own, "region", [(i, i + 1) for i in range(regions - 1)])
+    me = lax.axis_index("depth")
+    halves = 2 if share % (2 * SUBLANES) == 0 else 1
+    half = share // halves
+    line = lax.broadcasted_iota(jnp.int32, (1, half, 1), 1)
+    owns, lefts = [], []
+    for c in range(halves):
+        held = []
+        for m in range(slabs):
+            start = ((me - m) % slabs) * share + c * half
+            piece = lax.dynamic_slice_in_dim(thermal_grid, start, half, axis=1)
+            piece = jnp.where(start + line < occupied_lines[0, 0], piece, EMPTY)
+            if m > 0:
+                piece = lax.ppermute(piece, "depth", [(i, (i - m) % slabs) for i in range(slabs)])
+            held.append(piece)
+        own = jnp.stack(held, axis=1)
+        owns.append(own)
+        lefts.append(lax.ppermute(own, "region", [(i, i + 1) for i in range(regions - 1)]))
     vmem = pltpu.VMEM
     smem = pltpu.SMEM
     return pl.pallas_call(
@@ -122,13 +141,11 @@
         in_specs=[
             pl.BlockSpec(memory_space=smem),
             pl.BlockSpec(memory_space=smem),
-            pl.BlockSpec(memory_space=vmem),
-            pl.BlockSpec(memory_space=vmem),
-            pl.BlockSpec(memory_space=vmem),
-        ],
+        ]
+        + [pl.BlockSpec(memory_space=vmem)] * (2 * halves + 1),
         out_specs=pl.BlockSpec(memory_space=vmem),
         scratch_shapes=[pltpu.VMEM((layers, slabs, share, width), jnp.float32)],
-    )(sheetgroup_viewer_sequence, skew_offsets, own, left, colormap_samples)
+    )(sheetgroup_viewer_sequence, skew_offsets, *owns, *lefts, colormap_samples)
 
 
 def solution(mesh):

time: 39.9 us -> 33.3 us (0.83)
  blocking collectives: 19.2 us -> 0 us
  starting transfers between devices: 1.92 us -> 15.7 us
  waiting for transfers between devices: 8.82 us -> 6.03 us
  local copies, waits for them, and re-layouts: 0.87 us -> 2.18 us
    all_to_all x1 -> x0, blocking collectives: 19.2 us -> none  [shards(): lax.all_to_all(blocks, 'depth', split_axis=1, concat_axis=1, tiled=True)]
    ppermute x1 -> x8, starting transfers between devices: 1.92 us -> 15.7 us  [the longest x6 10.4 us: shards(): lax.ppermute(piece, 'depth', [(i, (i - m) % slabs) for i in range(slabs)])]
    ppermute x1 -> x8, waiting for transfers between devices: 8.82 us -> 6.03 us  [the longest x2 3.78 us: shards(): lax.ppermute(own, 'region', [(i, i + 1) for i in range(regions - 1)])]
    another operation x0 -> x3, other arithmetic: none -> 1.24 us  [shards(): own = jnp.stack(held, axis=1)]
    select_n x1 -> x0, other arithmetic: 1.15 us -> none  [shards(): marked = jnp.where(line < occupied_lines[0, 0], thermal_grid, EMPTY)]
    ppermute x0 -> x1, local copies, waits for them, and re-layouts: none -> 0.73 us  [shards(): lax.ppermute(own, 'region', [(i, i + 1) for i in range(regions - 1)])]
    another operation x0 -> x1, local copies, waits for them, and re-layouts: none -> 0.72 us  [shards(): own = jnp.stack(held, axis=1)]
  transfers between devices with their start and end apart: 1 -> 8, of which waited for: 1 -> 4; matrix products, arithmetic and copies ran while one was open for 0% -> 5% of each run, Pallas kernels for 0% -> 0%
where the time goes in v5:
time: 33.3 us; the launch traced here: 33 us
  starting transfers between devices  15.7 us (47%)
  Pallas kernels  6.38 us (19%)
  waiting for transfers between devices  6.03 us (18%)
  local copies, waits for them, and re-layouts  2.18 us (7%)
  between operations  1.44 us (4%)
  other arithmetic  1.27 us (4%)
    ppermute x6, starting transfers between devices, shards(): lax.ppermute(piece, 'depth', [(i, (i - m) % slabs) for i in range(slabs)])  10.4 us
    pallas_call x1, Pallas kernels, shards(): pl.pallas_call(render_kernel, out_shape=jax.ShapeDtypeStruct((4, share, w...  6.38 us
    ppermute x2, starting transfers between devices, shards(): lax.ppermute(own, 'region', [(i, i + 1) for i in range(regions - 1)])  5.3 us
    ppermute x2, waiting for transfers between devices, shards(): lax.ppermute(own, 'region', [(i, i + 1) for i in range(regions - 1)])  3.78 us
    ppermute x6, waiting for transfers between devices, shards(): lax.ppermute(piece, 'depth', [(i, (i - m) % slabs) for i in range(slabs)])  2.25 us
    another operation x3, other arithmetic, shards(): own = jnp.stack(held, axis=1)  1.24 us
    ppermute x1, local copies, waits for them, and re-layouts, shards(): lax.ppermute(own, 'region', [(i, i + 1) for i in range(regions - 1)])  0.73 us
    unnamed x4, local copies, waits for them, and re-layouts  0.72 us
  transfers between devices with their start and end apart: 8, of which 4 were waited for; matrix products, arithmetic and copies ran while one was open for 5% of the time, Pallas kernels for 0%

profile of v5, /device:TPU:4, one launch (start us, length us, event | category | flops | bytes accessed | tf_op | source)
XLA Modules:
  0.0 33.0 jit_solution(3618813761188481493)
XLA Ops:
  0.8 1.2 %select_bitcast_fusion = (f32[2,1,16,512]{3,2,1,0:T(8,128)S(1)}, f32[2,16,512]{2,1,0:T(8,128)S(1)}, f32[2,16,512]{2,1,0:T(8,128)S(1)}, f32[2,16,512]{2,1,0:T(8,1...) fusion(f32[2,128,512]{2,1,0:T(8,128)} %param.5, ...), kind=kLoop, calls=%fused_computation.5 | loop fusion | flops 131072 | bytes 1048736 | tf_op jit(solution)/shard_map/stack | solution.py:133
  2.0 3.7 %collective-permute-start = (f32[2,16,512]{2,1,0:T(8,128)S(1)}, f32[2,16,512]{2,1,0:T(8,128)S(1)}, u32[]{:S(2)}, u32[]{:S(2)}) collective-permute-start(f32[2,16,512]{2,1,0:T(8,128)S(1)} %get-tuple-element.9), channel_id=1, source_target_pairs={{0,24},{8,0},{16,8},{24,16},{1,25},{9,1},{17,9},{25,17},{2,26},{10... | collective-permute-start | bytes 196616 | tf_op jit(solution)/shard_map/ppermute | solution.py:131
  5.6 0.0 collective-permute-start.1
  5.6 1.0 %collective-permute-start.2 = (f32[2,16,512]{2,1,0:T(8,128)S(1)}, f32[2,16,512]{2,1,0:T(8,128)S(1)}, u32[]{:S(2)}, u32[]{:S(2)}) collective-permute-start(f32[2,16,512]{2,1,0:T(8,128)S(1)} %get-tuple-element.7), channel_id=1, source_target_pairs={{0,8},{8,16},{16,24},{24,0},{1,9},{9,17},{17,25},{25,1},{2,10},{10... | collective-permute-start | bytes 196616 | tf_op jit(solution)/shard_map/ppermute | solution.py:131
  6.7 1.9 %collective-permute-start.4 = (f32[2,16,512]{2,1,0:T(8,128)S(1)}, f32[2,16,512]{2,1,0:T(8,128)S(1)}, u32[]{:S(2)}, u32[]{:S(2)}) collective-permute-start(f32[2,16,512]{2,1,0:T(8,128)S(1)} %get-tuple-element.12), channel_id=1, source_target_pairs={{0,16},{8,24},{16,0},{24,8},{1,17},{9,25},{17,1},{25,9},{2,18},{10... | collective-permute-start | bytes 196616 | tf_op jit(solution)/shard_map/ppermute | solution.py:131
  8.6 1.5 %collective-permute-start.5 = (f32[2,16,512]{2,1,0:T(8,128)S(1)}, f32[2,16,512]{2,1,0:T(8,128)S(1)}, u32[]{:S(2)}, u32[]{:S(2)}) collective-permute-start(f32[2,16,512]{2,1,0:T(8,128)S(1)} %get-tuple-element.11), channel_id=1, source_target_pairs={{0,8},{8,16},{16,24},{24,0},{1,9},{9,17},{17,25},{25,1},{2,10},{10... | collective-permute-start | bytes 196616 | tf_op jit(solution)/shard_map/ppermute | solution.py:131
  10.0 0.0 collective-permute-done
  10.0 2.4 %collective-permute-start.3 = (f32[2,16,512]{2,1,0:T(8,128)S(1)}, f32[2,16,512]{2,1,0:T(8,128)S(1)}, u32[]{:S(2)}, u32[]{:S(2)}) collective-permute-start(f32[2,16,512]{2,1,0:T(8,128)S(1)} %get-tuple-element.6), channel_id=1, source_target_pairs={{0,24},{8,0},{16,8},{24,16},{1,25},{9,1},{17,9},{25,17},{2,26},{10... | collective-permute-start | bytes 196616 | tf_op jit(solution)/shard_map/ppermute | solution.py:131
  12.4 2.1 %collective-permute-done.1 = f32[2,16,512]{2,1,0:T(8,128)S(1)} collective-permute-done((f32[2,16,512]{2,1,0:T(8,128)S(1)}, f32[2,16,512]{2,1,0:T(8,128)S(1)}, u32[]{:S(2)}, u32[]{:S(2)}) %collective-permute-start.1) | collective-permute-done | bytes 65568 | tf_op jit(solution)/shard_map/ppermute | solution.py:131
  14.5 0.0 collective-permute-done.2
  14.5 1.9 %collective-permute-start.6 = (f32[2,4,16,512]{3,2,0,1:T(8,128)S(1)}, f32[2,4,16,512]{3,2,0,1:T(8,128)S(1)}, u32[]{:S(2)}, u32[]{:S(2)}) collective-permute-start(f32[2,4,16,512]{3,2,0,1:T(8,128)S(1)} %pad_maximum_fusion), channel_id=1, source_target_pairs={{0,1},{1,2},{2,3},{3,4},{4,5},{5,6},{6,7},{8,9},{9,10},{10,11},{11... | collective-permute-start | bytes 786440 | tf_op jit(solution)/shard_map/ppermute | solution.py:135
  16.5 0.2 collective-permute-done.4
  16.6 0.0 collective-permute-done.5
  16.6 0.0 collective-permute-done.3
  16.6 0.0 copy-start
  16.6 3.4 %collective-permute-start.7 = (f32[2,4,16,512]{3,2,1,0:T(8,128)S(1)}, f32[2,4,16,512]{3,2,1,0:T(8,128)S(1)}, u32[]{:S(2)}, u32[]{:S(2)}) collective-permute-start(f32[2,4,16,512]{3,2,1,0:T(8,128)S(1)} %pad_maximum_fusion.1.refs_1_), channel_id=1, source_target_pairs={{0,1},{1,2},{2,3},{3,4},{4,5},{5,6},{6,7},{8,9},{9,10},{10,11},{11... | collective-permute-start | bytes 786440 | tf_op jit(solution)/shard_map/ppermute | solution.py:135
  20.7 0.7 %copy.9.refs_0_ = f32[2,4,16,512]{3,2,1,0:T(8,128)} copy(f32[2,4,16,512]{3,2,0,1:T(8,128)S(1)} %pad_maximum_fusion) | data formatting | bytes 524288 | tf_op jit(solution)/shard_map/stack | solution.py:133
  21.4 0.0 copy-done
  21.4 1.7 %collective-permute-done.6 = f32[2,4,16,512]{3,2,0,1:T(8,128)S(1)} collective-permute-done((f32[2,4,16,512]{3,2,0,1:T(8,128)S(1)}, f32[2,4,16,512]{3,2,0,1:T(8,128)S(1)}, u32[]{:S(2)}, u32[]{:S(2)}) %collective-permute-start.6) | collective-permute-done | bytes 262176 | tf_op jit(solution)/shard_map/ppermute | solution.py:135
  23.1 0.7 %copy.10.refs_2_ = f32[2,4,16,512]{3,2,1,0:T(8,128)} copy(f32[2,4,16,512]{3,2,0,1:T(8,128)S(1)} %collective-permute-done.6) | data formatting | bytes 524288 | tf_op jit(solution)/shard_map/ppermute | solution.py:135
  23.8 2.1 %collective-permute-done.7.refs_3_ = f32[2,4,16,512]{3,2,1,0:T(8,128)S(1)} collective-permute-done((f32[2,4,16,512]{3,2,1,0:T(8,128)S(1)}, f32[2,4,16,512]{3,2,1,0:T(8,128)S(1)}, u32[]{:S(2)}, u32[]{:S(2)}) %collective-permute-start.7) | collective-permute-done | bytes 262176 | tf_op jit(solution)/shard_map/ppermute | solution.py:135
  25.9 0.0 copy-start.1
  25.9 0.7 %copy-done.1 = f32[2,4,16,512]{3,2,1,0:T(8,128)} copy-done((f32[2,4,16,512]{3,2,1,0:T(8,128)}, f32[2,4,16,512]{3,2,1,0:T(8,128)S(1)}, u32[]{:S(2)}) %copy-start.1) | copy-done | bytes 262168
  26.6 6.4 %shard_map.55 = f32[4,32,512]{2,1,0:T(8,128)} custom-call(s32[4]{0:T(128)} %seq_ref.1, s32[1]{0:T(128)S(6)} %copy.12.skew_ref, f32[2,4,16,512]{3,2,1,0:T(8,128)} %copy.9.refs_0_, f32[2,4,16,512]{3,2,1,0:T(8,128)} %copy-done, f32[2,4,16,512]{3,2,1,0:T(8,128)} %copy.10.refs_2_, f32[2,4,16,512]{3,2,1,0:T(8,128)} %copy-done.1, f32[4,256]{1,0:T(4,128)} %refs_4_.1), custom_call_target="tpu_custom_call" | custom-call | tf_op jit(solution)/shard_map/pallas_call | solution.py:138
  (6 shorter events, 0.1 us)
Async XLA Ops:
  2.0 8.0 %collective-permute-start = (f32[2,16,512]{2,1,0:T(8,128)S(1)}, f32[2,16,512]{2,1,0:T(8,128)S(1)}, u32[]{:S(2)}, u32[]{:S(2)}) collective-permute-start(f32[2,16,512]{2,1,0:T(8,128)S(1)} %get-tuple-element.9), channel_id=1, source_target_pairs={{0,24},{8,0},{16,8},{24,16},{1,25},{9,1},{17,9},{25,17},{2,26},{10... | collective-permute-start | bytes 196616 | tf_op jit(solution)/shard_map/ppermute | solution.py:131
  5.6 8.9 %collective-permute-start.1 = (f32[2,16,512]{2,1,0:T(8,128)S(1)}, f32[2,16,512]{2,1,0:T(8,128)S(1)}, u32[]{:S(2)}, u32[]{:S(2)}) collective-permute-start(f32[2,16,512]{2,1,0:T(8,128)S(1)} %get-tuple-element.8), channel_id=1, source_target_pairs={{0,16},{8,24},{16,0},{24,8},{1,17},{9,25},{17,1},{25,9},{2,18},{10... | collective-permute-start | bytes 196616 | tf_op jit(solution)/shard_map/ppermute | solution.py:131
  5.6 8.9 %collective-permute-start.2 = (f32[2,16,512]{2,1,0:T(8,128)S(1)}, f32[2,16,512]{2,1,0:T(8,128)S(1)}, u32[]{:S(2)}, u32[]{:S(2)}) collective-permute-start(f32[2,16,512]{2,1,0:T(8,128)S(1)} %get-tuple-element.7), channel_id=1, source_target_pairs={{0,8},{8,16},{16,24},{24,0},{1,9},{9,17},{17,25},{25,1},{2,10},{10... | collective-permute-start | bytes 196616 | tf_op jit(solution)/shard_map/ppermute | solution.py:131
  6.7 10.0 %collective-permute-start.4 = (f32[2,16,512]{2,1,0:T(8,128)S(1)}, f32[2,16,512]{2,1,0:T(8,128)S(1)}, u32[]{:S(2)}, u32[]{:S(2)}) collective-permute-start(f32[2,16,512]{2,1,0:T(8,128)S(1)} %get-tuple-element.12), channel_id=1, source_target_pairs={{0,16},{8,24},{16,0},{24,8},{1,17},{9,25},{17,1},{25,9},{2,18},{10... | collective-permute-start | bytes 196616 | tf_op jit(solution)/shard_map/ppermute | solution.py:131
  8.6 8.0 %collective-permute-start.5 = (f32[2,16,512]{2,1,0:T(8,128)S(1)}, f32[2,16,512]{2,1,0:T(8,128)S(1)}, u32[]{:S(2)}, u32[]{:S(2)}) collective-permute-start(f32[2,16,512]{2,1,0:T(8,128)S(1)} %get-tuple-element.11), channel_id=1, source_target_pairs={{0,8},{8,16},{16,24},{24,0},{1,9},{9,17},{17,25},{25,1},{2,10},{10... | collective-permute-start | bytes 196616 | tf_op jit(solution)/shard_map/ppermute | solution.py:131
  10.0 6.6 %collective-permute-start.3 = (f32[2,16,512]{2,1,0:T(8,128)S(1)}, f32[2,16,512]{2,1,0:T(8,128)S(1)}, u32[]{:S(2)}, u32[]{:S(2)}) collective-permute-start(f32[2,16,512]{2,1,0:T(8,128)S(1)} %get-tuple-element.6), channel_id=1, source_target_pairs={{0,24},{8,0},{16,8},{24,16},{1,25},{9,1},{17,9},{25,17},{2,26},{10... | collective-permute-start | bytes 196616 | tf_op jit(solution)/shard_map/ppermute | solution.py:131
  14.5 8.6 %collective-permute-start.6 = (f32[2,4,16,512]{3,2,0,1:T(8,128)S(1)}, f32[2,4,16,512]{3,2,0,1:T(8,128)S(1)}, u32[]{:S(2)}, u32[]{:S(2)}) collective-permute-start(f32[2,4,16,512]{3,2,0,1:T(8,128)S(1)} %pad_maximum_fusion), channel_id=1, source_target_pairs={{0,1},{1,2},{2,3},{3,4},{4,5},{5,6},{6,7},{8,9},{9,10},{10,11},{11... | collective-permute-start | bytes 786440 | tf_op jit(solution)/shard_map/ppermute | solution.py:135
  16.6 4.8 %copy-start = (f32[2,4,16,512]{3,2,1,0:T(8,128)}, f32[2,4,16,512]{3,2,1,0:T(8,128)S(1)}, u32[]{:S(2)}) copy-start(f32[2,4,16,512]{3,2,1,0:T(8,128)S(1)} %pad_maximum_fusion.1.refs_1_) | copy-start | bytes 786436
  16.6 9.3 %collective-permute-start.7 = (f32[2,4,16,512]{3,2,1,0:T(8,128)S(1)}, f32[2,4,16,512]{3,2,1,0:T(8,128)S(1)}, u32[]{:S(2)}, u32[]{:S(2)}) collective-permute-start(f32[2,4,16,512]{3,2,1,0:T(8,128)S(1)} %pad_maximum_fusion.1.refs_1_), channel_id=1, source_target_pairs={{0,1},{1,2},{2,3},{3,4},{4,5},{5,6},{6,7},{8,9},{9,10},{10,11},{11... | collective-permute-start | bytes 786440 | tf_op jit(solution)/shard_map/ppermute | solution.py:135
  25.9 0.7 %copy-start.1 = (f32[2,4,16,512]{3,2,1,0:T(8,128)}, f32[2,4,16,512]{3,2,1,0:T(8,128)S(1)}, u32[]{:S(2)}) copy-start(f32[2,4,16,512]{3,2,1,0:T(8,128)S(1)} %collective-permute-done.7.refs_3_) | copy-start | bytes 786436

commit v6 on v5

--- a/solution.py
+++ b/solution.py
@@ -34,7 +34,7 @@
     halves = (len(refs) - 3) // 2
     own_refs, left_refs = refs[:halves], refs[halves : 2 * halves]
     cmap_ref, out_ref, shifted_ref = refs[2 * halves :]
-    layers, slabs, half_rows, width = own_refs[0].shape
+    slabs, layers, half_rows, width = own_refs[0].shape
     rows = half_rows * halves
     layers_overall = layers * slabs
     knot_count = cmap_ref.shape[1]
@@ -57,8 +57,8 @@
                 band = pl.ds(r * SUBLANES, SUBLANES)
                 c, rest = divmod(r * SUBLANES, half_rows)
                 part = pl.ds(rest, SUBLANES)
-                left = jnp.where(first_tile, EMPTY, left_refs[c][l, s, part, :])
-                joined = jnp.concatenate([left, own_refs[c][l, s, part, :]], axis=1)
+                left = jnp.where(first_tile, EMPTY, left_refs[c][s, l, part, :])
+                joined = jnp.concatenate([left, own_refs[c][s, l, part, :]], axis=1)
                 shifted_ref[l, k, band, :] = pltpu.roll(joined, shift, 1)[:, width:]
 
     cmap = cmap_ref[...]
@@ -130,11 +130,12 @@
             if m > 0:
                 piece = lax.ppermute(piece, "depth", [(i, (i - m) % slabs) for i in range(slabs)])
             held.append(piece)
-        own = jnp.stack(held, axis=1)
+        own = jnp.stack(held, axis=0)
         owns.append(own)
         lefts.append(lax.ppermute(own, "region", [(i, i + 1) for i in range(regions - 1)]))
     vmem = pltpu.VMEM
     smem = pltpu.SMEM
+    placed = [pltpu.with_memory_space_constraint(x, vmem) for x in owns + lefts]
     return pl.pallas_call(
         render_kernel,
         out_shape=jax.ShapeDtypeStruct((4, share, width), jnp.float32),
@@ -145,7 +146,7 @@
         + [pl.BlockSpec(memory_space=vmem)] * (2 * halves + 1),
         out_specs=pl.BlockSpec(memory_space=vmem),
         scratch_shapes=[pltpu.VMEM((layers, slabs, share, width), jnp.float32)],
-    )(sheetgroup_viewer_sequence, skew_offsets, *owns, *lefts, colormap_samples)
+    )(sheetgroup_viewer_sequence, skew_offsets, *placed, colormap_samples)
 
 
 def solution(mesh):

time: 33.3 us -> 34.1 us (1.024)
  waiting for transfers between devices: 6.03 us -> 9.4 us
  local copies, waits for them, and re-layouts: 2.18 us -> 0 us
  Pallas kernels: 6.38 us -> 5.88 us
    ppermute x6, waiting for transfers between devices: 2.25 us -> 4.14 us  [shards(): lax.ppermute(piece, 'depth', [(i, (i - m) % slabs) for i in range(slabs)])]
    ppermute x2, waiting for transfers between devices: 3.78 us -> 5.25 us  [shards(): lax.ppermute(own, 'region', [(i, i + 1) for i in range(regions - 1)])]
    ppermute x1 -> x0, local copies, waits for them, and re-layouts: 0.73 us -> none  [shards(): lax.ppermute(own, 'region', [(i, i + 1) for i in range(regions - 1)])]
    unnamed x4 -> x0, local copies, waits for them, and re-layouts: 0.72 us -> none
    another operation x1 -> x0, local copies, waits for them, and re-layouts: 0.72 us -> none  [shards(): own = jnp.stack(held, axis=1)]
    pallas_call x1, Pallas kernels: 6.38 us -> 5.88 us  [shards(): pl.pallas_call(render_kernel, out_shape=jax.ShapeDtypeStruct((4, share, w...]
  transfers between devices with their start and end apart: 8 -> 8, of which waited for: 4 -> 4; matrix products, arithmetic and copies ran while one was open for 5% -> 0% of each run, Pallas kernels for 0% -> 0%
where the time goes in v6:
time: 34.1 us; the launch traced here: 33.8 us
  starting transfers between devices  15.9 us (47%)
  waiting for transfers between devices  9.4 us (28%)
  Pallas kernels  5.88 us (17%)
  between operations  1.43 us (4%)
  other arithmetic  1.28 us (4%)
    ppermute x6, starting transfers between devices, shards(): lax.ppermute(piece, 'depth', [(i, (i - m) % slabs) for i in range(slabs)])  10.4 us
    pallas_call x1, Pallas kernels, shards(): pl.pallas_call(render_kernel, out_shape=jax.ShapeDtypeStruct((4, share, w...  5.88 us
    ppermute x2, starting transfers between devices, shards(): lax.ppermute(own, 'region', [(i, i + 1) for i in range(regions - 1)])  5.42 us
    ppermute x2, waiting for transfers between devices, shards(): lax.ppermute(own, 'region', [(i, i + 1) for i in range(regions - 1)])  5.25 us
    ppermute x6, waiting for transfers between devices, shards(): lax.ppermute(piece, 'depth', [(i, (i - m) % slabs) for i in range(slabs)])  4.14 us
    another operation x3, other arithmetic, shards(): own = jnp.stack(held, axis=0)  1.24 us
  transfers between devices with their start and end apart: 8, of which 4 were waited for; matrix products, arithmetic and copies ran while one was open for 0% of the time, Pallas kernels for 0%

profile of v6, /device:TPU:4, one launch (start us, length us, event | category | flops | bytes accessed | tf_op | source)
XLA Modules:
  0.0 33.8 jit_solution(11978569666098083031)
XLA Ops:
  0.8 1.2 %select_bitcast_fusion = (f32[1,2,16,512]{3,2,1,0:T(8,128)S(1)}, f32[2,16,512]{2,1,0:T(8,128)S(1)}, f32[2,16,512]{2,1,0:T(8,128)S(1)}, f32[2,16,512]{2,1,0:T(8,1...) fusion(f32[2,128,512]{2,1,0:T(8,128)} %param.5, ...), kind=kLoop, calls=%fused_computation.5 | loop fusion | flops 131072 | bytes 1048736 | tf_op jit(solution)/shard_map/stack | solution.py:133
  2.0 3.7 %collective-permute-start.3 = (f32[2,16,512]{2,1,0:T(8,128)S(1)}, f32[2,16,512]{2,1,0:T(8,128)S(1)}, u32[]{:S(2)}, u32[]{:S(2)}) collective-permute-start(f32[2,16,512]{2,1,0:T(8,128)S(1)} %get-tuple-element.6), channel_id=1, source_target_pairs={{0,24},{8,0},{16,8},{24,16},{1,25},{9,1},{17,9},{25,17},{2,26},{10... | collective-permute-start | bytes 196616 | tf_op jit(solution)/shard_map/ppermute | solution.py:131
  5.6 0.0 collective-permute-start.5
  5.6 1.0 %collective-permute-start.4 = (f32[2,16,512]{2,1,0:T(8,128)S(1)}, f32[2,16,512]{2,1,0:T(8,128)S(1)}, u32[]{:S(2)}, u32[]{:S(2)}) collective-permute-start(f32[2,16,512]{2,1,0:T(8,128)S(1)} %get-tuple-element.12), channel_id=1, source_target_pairs={{0,16},{8,24},{16,0},{24,8},{1,17},{9,25},{17,1},{25,9},{2,18},{10... | collective-permute-start | bytes 196616 | tf_op jit(solution)/shard_map/ppermute | solution.py:131
  6.6 3.4 %collective-permute-start.2 = (f32[2,16,512]{2,1,0:T(8,128)S(1)}, f32[2,16,512]{2,1,0:T(8,128)S(1)}, u32[]{:S(2)}, u32[]{:S(2)}) collective-permute-start(f32[2,16,512]{2,1,0:T(8,128)S(1)} %get-tuple-element.7), channel_id=1, source_target_pairs={{0,8},{8,16},{16,24},{24,0},{1,9},{9,17},{17,25},{25,1},{2,10},{10... | collective-permute-start | bytes 196616 | tf_op jit(solution)/shard_map/ppermute | solution.py:131
  10.0 0.0 collective-permute-start.1
  10.0 0.0 collective-permute-done.3
  10.0 2.4 %collective-permute-start = (f32[2,16,512]{2,1,0:T(8,128)S(1)}, f32[2,16,512]{2,1,0:T(8,128)S(1)}, u32[]{:S(2)}, u32[]{:S(2)}) collective-permute-start(f32[2,16,512]{2,1,0:T(8,128)S(1)} %get-tuple-element.9), channel_id=1, source_target_pairs={{0,24},{8,0},{16,8},{24,16},{1,25},{9,1},{17,9},{25,17},{2,26},{10... | collective-permute-start | bytes 196616 | tf_op jit(solution)/shard_map/ppermute | solution.py:131
  12.4 0.2 collective-permute-done.5
  12.6 4.0 %collective-permute-done.4 = f32[2,16,512]{2,1,0:T(8,128)S(1)} collective-permute-done((f32[2,16,512]{2,1,0:T(8,128)S(1)}, f32[2,16,512]{2,1,0:T(8,128)S(1)}, u32[]{:S(2)}, u32[]{:S(2)}) %collective-permute-start.4) | collective-permute-done | bytes 65568 | tf_op jit(solution)/shard_map/ppermute | solution.py:131
  16.6 1.9 %collective-permute-start.7 = (f32[4,2,16,512]{3,2,1,0:T(8,128)S(1)}, f32[4,2,16,512]{3,2,1,0:T(8,128)S(1)}, u32[]{:S(2)}, u32[]{:S(2)}) collective-permute-start(f32[4,2,16,512]{3,2,1,0:T(8,128)S(1)} %pad_maximum_fusion.1.refs_1_), channel_id=1, source_target_pairs={{0,1},{1,2},{2,3},{3,4},{4,5},{5,6},{6,7},{8,9},{9,10},{10,11},{11... | collective-permute-start | bytes 786440 | tf_op jit(solution)/shard_map/ppermute | solution.py:135
  18.5 0.0 collective-permute-done.2
  18.5 0.0 collective-permute-done.1
  18.5 0.0 collective-permute-done
  18.5 3.5 %collective-permute-start.6 = (f32[4,2,16,512]{3,2,1,0:T(8,128)S(1)}, f32[4,2,16,512]{3,2,1,0:T(8,128)S(1)}, u32[]{:S(2)}, u32[]{:S(2)}) collective-permute-start(f32[4,2,16,512]{3,2,1,0:T(8,128)S(1)} %pad_maximum_fusion.refs_0_), channel_id=1, source_target_pairs={{0,1},{1,2},{2,3},{3,4},{4,5},{5,6},{6,7},{8,9},{9,10},{10,11},{11... | collective-permute-start | bytes 786440 | tf_op jit(solution)/shard_map/ppermute | solution.py:135
  22.7 2.4 %collective-permute-done.7.refs_3_ = f32[4,2,16,512]{3,2,1,0:T(8,128)S(1)} collective-permute-done((f32[4,2,16,512]{3,2,1,0:T(8,128)S(1)}, f32[4,2,16,512]{3,2,1,0:T(8,128)S(1)}, u32[]{:S(2)}, u32[]{:S(2)}) %collective-permute-start.7) | collective-permute-done | bytes 262176 | tf_op jit(solution)/shard_map/ppermute | solution.py:135
  25.2 2.8 %collective-permute-done.6.refs_2_ = f32[4,2,16,512]{3,2,1,0:T(8,128)S(1)} collective-permute-done((f32[4,2,16,512]{3,2,1,0:T(8,128)S(1)}, f32[4,2,16,512]{3,2,1,0:T(8,128)S(1)}, u32[]{:S(2)}, u32[]{:S(2)}) %collective-permute-start.6) | collective-permute-done | bytes 262176 | tf_op jit(solution)/shard_map/ppermute | solution.py:135
  28.0 5.9 %shard_map.55 = f32[4,32,512]{2,1,0:T(8,128)} custom-call(s32[4]{0:T(128)} %seq_ref.1, s32[1]{0:T(128)S(6)} %copy.7.skew_ref, f32[4,2,16,512]{3,2,1,0:T(8,128)S(1)} %pad_maximum_fusion.refs_0_, f32[4,2,16,512]{3,2,1,0:T(8,128)S(1)} %pad_maximum_fusion.1.refs_1_, f32[4,2,16,512]{3,2,1,0:T(8,128)S(1)} %collective-permute-done.6.refs_2_, ...), custom_call_target="tpu_custom_call" | custom-call | tf_op jit(solution)/shard_map/pallas_call | solution.py:139
  (6 shorter events, 0.1 us)
Async XLA Ops:
  2.0 8.0 %collective-permute-start.3 = (f32[2,16,512]{2,1,0:T(8,128)S(1)}, f32[2,16,512]{2,1,0:T(8,128)S(1)}, u32[]{:S(2)}, u32[]{:S(2)}) collective-permute-start(f32[2,16,512]{2,1,0:T(8,128)S(1)} %get-tuple-element.6), channel_id=1, source_target_pairs={{0,24},{8,0},{16,8},{24,16},{1,25},{9,1},{17,9},{25,17},{2,26},{10... | collective-permute-start | bytes 196616 | tf_op jit(solution)/shard_map/ppermute | solution.py:131
  5.6 7.0 %collective-permute-start.5 = (f32[2,16,512]{2,1,0:T(8,128)S(1)}, f32[2,16,512]{2,1,0:T(8,128)S(1)}, u32[]{:S(2)}, u32[]{:S(2)}) collective-permute-start(f32[2,16,512]{2,1,0:T(8,128)S(1)} %get-tuple-element.11), channel_id=1, source_target_pairs={{0,8},{8,16},{16,24},{24,0},{1,9},{9,17},{17,25},{25,1},{2,10},{10... | collective-permute-start | bytes 196616 | tf_op jit(solution)/shard_map/ppermute | solution.py:131
  5.6 10.9 %collective-permute-start.4 = (f32[2,16,512]{2,1,0:T(8,128)S(1)}, f32[2,16,512]{2,1,0:T(8,128)S(1)}, u32[]{:S(2)}, u32[]{:S(2)}) collective-permute-start(f32[2,16,512]{2,1,0:T(8,128)S(1)} %get-tuple-element.12), channel_id=1, source_target_pairs={{0,16},{8,24},{16,0},{24,8},{1,17},{9,25},{17,1},{25,9},{2,18},{10... | collective-permute-start | bytes 196616 | tf_op jit(solution)/shard_map/ppermute | solution.py:131
  6.6 11.9 %collective-permute-start.2 = (f32[2,16,512]{2,1,0:T(8,128)S(1)}, f32[2,16,512]{2,1,0:T(8,128)S(1)}, u32[]{:S(2)}, u32[]{:S(2)}) collective-permute-start(f32[2,16,512]{2,1,0:T(8,128)S(1)} %get-tuple-element.7), channel_id=1, source_target_pairs={{0,8},{8,16},{16,24},{24,0},{1,9},{9,17},{17,25},{25,1},{2,10},{10... | collective-permute-start | bytes 196616 | tf_op jit(solution)/shard_map/ppermute | solution.py:131
  10.0 8.5 %collective-permute-start.1 = (f32[2,16,512]{2,1,0:T(8,128)S(1)}, f32[2,16,512]{2,1,0:T(8,128)S(1)}, u32[]{:S(2)}, u32[]{:S(2)}) collective-permute-start(f32[2,16,512]{2,1,0:T(8,128)S(1)} %get-tuple-element.8), channel_id=1, source_target_pairs={{0,16},{8,24},{16,0},{24,8},{1,17},{9,25},{17,1},{25,9},{2,18},{10... | collective-permute-start | bytes 196616 | tf_op jit(solution)/shard_map/ppermute | solution.py:131
  10.0 8.5 %collective-permute-start = (f32[2,16,512]{2,1,0:T(8,128)S(1)}, f32[2,16,512]{2,1,0:T(8,128)S(1)}, u32[]{:S(2)}, u32[]{:S(2)}) collective-permute-start(f32[2,16,512]{2,1,0:T(8,128)S(1)} %get-tuple-element.9), channel_id=1, source_target_pairs={{0,24},{8,0},{16,8},{24,16},{1,25},{9,1},{17,9},{25,17},{2,26},{10... | collective-permute-start | bytes 196616 | tf_op jit(solution)/shard_map/ppermute | solution.py:131
  16.6 8.6 %collective-permute-start.7 = (f32[4,2,16,512]{3,2,1,0:T(8,128)S(1)}, f32[4,2,16,512]{3,2,1,0:T(8,128)S(1)}, u32[]{:S(2)}, u32[]{:S(2)}) collective-permute-start(f32[4,2,16,512]{3,2,1,0:T(8,128)S(1)} %pad_maximum_fusion.1.refs_1_), channel_id=1, source_target_pairs={{0,1},{1,2},{2,3},{3,4},{4,5},{5,6},{6,7},{8,9},{9,10},{10,11},{11... | collective-permute-start | bytes 786440 | tf_op jit(solution)/shard_map/ppermute | solution.py:135
  18.5 9.4 %collective-permute-start.6 = (f32[4,2,16,512]{3,2,1,0:T(8,128)S(1)}, f32[4,2,16,512]{3,2,1,0:T(8,128)S(1)}, u32[]{:S(2)}, u32[]{:S(2)}) collective-permute-start(f32[4,2,16,512]{3,2,1,0:T(8,128)S(1)} %pad_maximum_fusion.refs_0_), channel_id=1, source_target_pairs={{0,1},{1,2},{2,3},{3,4},{4,5},{5,6},{6,7},{8,9},{9,10},{10,11},{11... | collective-permute-start | bytes 786440 | tf_op jit(solution)/shard_map/ppermute | solution.py:135

commit v7 on v6

--- a/solution.py
+++ b/solution.py
@@ -117,7 +117,7 @@
     regions = lax.axis_size("region")
     share = rows // slabs
     me = lax.axis_index("depth")
-    halves = 2 if share % (2 * SUBLANES) == 0 else 1
+    halves = max(1, min(4, share // SUBLANES))
     half = share // halves
     line = lax.broadcasted_iota(jnp.int32, (1, half, 1), 1)
     owns, lefts = [], []

time: 34.1 us -> 43.1 us (1.26); the launches traced: 33.8 us -> 42.4 us
  starting transfers between devices: 15.9 us -> 23.6 us
  waiting for transfers between devices: 9.4 us -> 10.1 us
    ppermute x6 -> x12, starting transfers between devices: 10.4 us -> 14.4 us  [shards(): lax.ppermute(piece, 'depth', [(i, (i - m) % slabs) for i in range(slabs)])]
    ppermute x2 -> x4, starting transfers between devices: 5.42 us -> 9.25 us  [shards(): lax.ppermute(own, 'region', [(i, i + 1) for i in range(regions - 1)])]
    ppermute x6 -> x12, waiting for transfers between devices: 4.14 us -> 5.51 us  [shards(): lax.ppermute(piece, 'depth', [(i, (i - m) % slabs) for i in range(slabs)])]
    another operation x3 -> x5, other arithmetic: 1.24 us -> 0.14 us  [shards(): own = jnp.stack(held, axis=0)]
    select_n x0 -> x1, other arithmetic: none -> 0.97 us  [shards(): piece = jnp.where(start + line < occupied_lines[0, 0], piece, EMPTY)]
    ppermute x2 -> x4, waiting for transfers between devices: 5.25 us -> 4.59 us  [shards(): lax.ppermute(own, 'region', [(i, i + 1) for i in range(regions - 1)])]
  transfers between devices with their start and end apart: 8 -> 16, of which waited for: 4 -> 7; matrix products, arithmetic and copies ran while one was open for 0% -> 0% of each run, Pallas kernels for 0% -> 0%
where the time goes in v7:
time: 43.1 us; the launch traced here: 42.4 us
  starting transfers between devices  23.6 us (55%)
  waiting for transfers between devices  10.1 us (23%)
  Pallas kernels  5.88 us (14%)
  between operations  1.62 us (4%)
  other arithmetic  1.17 us (3%)
    ppermute x12, starting transfers between devices, shards(): lax.ppermute(piece, 'depth', [(i, (i - m) % slabs) for i in range(slabs)])  14.4 us
    ppermute x4, starting transfers between devices, shards(): lax.ppermute(own, 'region', [(i, i + 1) for i in range(regions - 1)])  9.25 us
    pallas_call x1, Pallas kernels, shards(): pl.pallas_call(render_kernel, out_shape=jax.ShapeDtypeStruct((4, share, w...  5.88 us
    ppermute x12, waiting for transfers between devices, shards(): lax.ppermute(piece, 'depth', [(i, (i - m) % slabs) for i in range(slabs)])  5.51 us
    ppermute x4, waiting for transfers between devices, shards(): lax.ppermute(own, 'region', [(i, i + 1) for i in range(regions - 1)])  4.59 us
    select_n x1, other arithmetic, shards(): piece = jnp.where(start + line < occupied_lines[0, 0], piece, EMPTY)  0.97 us
  transfers between devices with their start and end apart: 16, of which 7 were waited for; matrix products, arithmetic and copies ran while one was open for 0% of the time, Pallas kernels for 0%

profile of v7, /device:TPU:4, one launch (start us, length us, event | category | flops | bytes accessed | tf_op | source)
XLA Modules:
  0.0 42.4 jit_solution(2769482164531866987)
XLA Ops:
  0.0 0.0 copy-start
  0.8 1.0 %dynamic-slice_select_fusion.1 = (f32[2,8,512]{2,1,0:T(8,128)S(1)}, f32[1,2,8,512]{3,2,1,0:T(8,128)S(1)}, f32[2,8,512]{2,1,0:T(8,128)S(1)}, f32[2,8,512]{2,1,0:T...) fusion(f32[2,128,512]{2,1,0:T(8,128)} %param.5, s32[]{:T(128)S(6)} %select_n.172, ...), kind=kLoop, calls=%fused_computation.5 | loop fusion | flops 57344 | bytes 458836 | tf_op jit(solution)/shard_map/jit(_where)/select_n | solution.py:129
  1.8 2.7 %collective-permute-start.10 = (f32[2,8,512]{2,1,0:T(8,128)S(1)}, f32[2,8,512]{2,1,0:T(8,128)S(1)}, u32[]{:S(2)}, u32[]{:S(2)}) collective-permute-start(f32[2,8,512]{2,1,0:T(8,128)S(1)} %get-tuple-element.14), channel_id=1, source_target_pairs={{0,16},{8,24},{16,0},{24,8},{1,17},{9,25},{17,1},{25,9},{2,18},{10... | collective-permute-start | bytes 98312 | tf_op jit(solution)/shard_map/ppermute | solution.py:131
  4.4 1.6 %collective-permute-start.2 = (f32[2,8,512]{2,1,0:T(8,128)S(1)}, f32[2,8,512]{2,1,0:T(8,128)S(1)}, u32[]{:S(2)}, u32[]{:S(2)}) collective-permute-start(f32[2,8,512]{2,1,0:T(8,128)S(1)} %get-tuple-element.16), channel_id=1, source_target_pairs={{0,8},{8,16},{16,24},{24,0},{1,9},{9,17},{17,25},{25,1},{2,10},{10... | collective-permute-start | bytes 98312 | tf_op jit(solution)/shard_map/ppermute | solution.py:131
  6.0 0.3 collective-permute-start.1
  6.3 2.0 %collective-permute-start = (f32[2,8,512]{2,1,0:T(8,128)S(1)}, f32[2,8,512]{2,1,0:T(8,128)S(1)}, u32[]{:S(2)}, u32[]{:S(2)}) collective-permute-start(f32[2,8,512]{2,1,0:T(8,128)S(1)} %get-tuple-element.18), channel_id=1, source_target_pairs={{0,24},{8,0},{16,8},{24,16},{1,25},{9,1},{17,9},{25,17},{2,26},{10... | collective-permute-start | bytes 98312 | tf_op jit(solution)/shard_map/ppermute | solution.py:131
  8.4 0.5 %collective-permute-start.11 = (f32[2,8,512]{2,1,0:T(8,128)S(1)}, f32[2,8,512]{2,1,0:T(8,128)S(1)}, u32[]{:S(2)}, u32[]{:S(2)}) collective-permute-start(f32[2,8,512]{2,1,0:T(8,128)S(1)} %get-tuple-element.20), channel_id=1, source_target_pairs={{0,8},{8,16},{16,24},{24,0},{1,9},{9,17},{17,25},{25,1},{2,10},{10... | collective-permute-start | bytes 98312 | tf_op jit(solution)/shard_map/ppermute | solution.py:131
  8.9 0.0 copy-done
  8.9 0.1 select_bitcast_fusion
  9.0 1.3 %collective-permute-done.2 = f32[2,8,512]{2,1,0:T(8,128)S(1)} collective-permute-done((f32[2,8,512]{2,1,0:T(8,128)S(1)}, f32[2,8,512]{2,1,0:T(8,128)S(1)}, u32[]{:S(2)}, u32[]{:S(2)}) %collective-permute-start.2) | collective-permute-done | bytes 32800 | tf_op jit(solution)/shard_map/ppermute | solution.py:131
  10.3 0.8 %collective-permute-start.5 = (f32[2,8,512]{2,1,0:T(8,128)S(1)}, f32[2,8,512]{2,1,0:T(8,128)S(1)}, u32[]{:S(2)}, u32[]{:S(2)}) collective-permute-start(f32[2,8,512]{2,1,0:T(8,128)S(1)} %get-tuple-element.11), channel_id=1, source_target_pairs={{0,8},{8,16},{16,24},{24,0},{1,9},{9,17},{17,25},{25,1},{2,10},{10... | collective-permute-start | bytes 98312 | tf_op jit(solution)/shard_map/ppermute | solution.py:131
  11.1 0.1 collective-permute-done.1
  11.2 1.9 %collective-permute-start.4 = (f32[2,8,512]{2,1,0:T(8,128)S(1)}, f32[2,8,512]{2,1,0:T(8,128)S(1)}, u32[]{:S(2)}, u32[]{:S(2)}) collective-permute-start(f32[2,8,512]{2,1,0:T(8,128)S(1)} %get-tuple-element.12), channel_id=1, source_target_pairs={{0,16},{8,24},{16,0},{24,8},{1,17},{9,25},{17,1},{25,9},{2,18},{10... | collective-permute-start | bytes 98312 | tf_op jit(solution)/shard_map/ppermute | solution.py:131
  13.0 0.0 collective-permute-done
  13.1 1.2 %collective-permute-start.3 = (f32[2,8,512]{2,1,0:T(8,128)S(1)}, f32[2,8,512]{2,1,0:T(8,128)S(1)}, u32[]{:S(2)}, u32[]{:S(2)}) collective-permute-start(f32[2,8,512]{2,1,0:T(8,128)S(1)} %get-tuple-element.13), channel_id=1, source_target_pairs={{0,24},{8,0},{16,8},{24,16},{1,25},{9,1},{17,9},{25,17},{2,26},{10... | collective-permute-start | bytes 98312 | tf_op jit(solution)/shard_map/ppermute | solution.py:131
  14.2 1.9 %collective-permute-done.5 = f32[2,8,512]{2,1,0:T(8,128)S(1)} collective-permute-done((f32[2,8,512]{2,1,0:T(8,128)S(1)}, f32[2,8,512]{2,1,0:T(8,128)S(1)}, u32[]{:S(2)}, u32[]{:S(2)}) %collective-permute-start.5) | collective-permute-done | bytes 32800 | tf_op jit(solution)/shard_map/ppermute | solution.py:131
  16.1 0.0 collective-permute-start.8
  16.1 0.6 %collective-permute-done.4 = f32[2,8,512]{2,1,0:T(8,128)S(1)} collective-permute-done((f32[2,8,512]{2,1,0:T(8,128)S(1)}, f32[2,8,512]{2,1,0:T(8,128)S(1)}, u32[]{:S(2)}, u32[]{:S(2)}) %collective-permute-start.4) | collective-permute-done | bytes 32800 | tf_op jit(solution)/shard_map/ppermute | solution.py:131
  16.7 1.2 %collective-permute-start.7 = (f32[2,8,512]{2,1,0:T(8,128)S(1)}, f32[2,8,512]{2,1,0:T(8,128)S(1)}, u32[]{:S(2)}, u32[]{:S(2)}) collective-permute-start(f32[2,8,512]{2,1,0:T(8,128)S(1)} %get-tuple-element.8), channel_id=1, source_target_pairs={{0,16},{8,24},{16,0},{24,8},{1,17},{9,25},{17,1},{25,9},{2,18},{10... | collective-permute-start | bytes 98312 | tf_op jit(solution)/shard_map/ppermute | solution.py:131
  17.9 0.0 collective-permute-done.3
  17.9 2.3 %collective-permute-start.6 = (f32[2,8,512]{2,1,0:T(8,128)S(1)}, f32[2,8,512]{2,1,0:T(8,128)S(1)}, u32[]{:S(2)}, u32[]{:S(2)}) collective-permute-start(f32[2,8,512]{2,1,0:T(8,128)S(1)} %get-tuple-element.9), channel_id=1, source_target_pairs={{0,24},{8,0},{16,8},{24,16},{1,25},{9,1},{17,9},{25,17},{2,26},{10... | collective-permute-start | bytes 98312 | tf_op jit(solution)/shard_map/ppermute | solution.py:131
  20.2 1.7 %collective-permute-done.8 = f32[2,8,512]{2,1,0:T(8,128)S(1)} collective-permute-done((f32[2,8,512]{2,1,0:T(8,128)S(1)}, f32[2,8,512]{2,1,0:T(8,128)S(1)}, u32[]{:S(2)}, u32[]{:S(2)}) %collective-permute-start.8) | collective-permute-done | bytes 32800 | tf_op jit(solution)/shard_map/ppermute | solution.py:131
  21.9 0.0 collective-permute-start.9
  21.9 0.0 collective-permute-done.7
  21.9 1.9 %collective-permute-start.12 = (f32[4,2,8,512]{3,2,1,0:T(8,128)S(1)}, f32[4,2,8,512]{3,2,1,0:T(8,128)S(1)}, u32[]{:S(2)}, u32[]{:S(2)}) collective-permute-start(f32[4,2,8,512]{3,2,1,0:T(8,128)S(1)} %pad_maximum_fusion.refs_0_), channel_id=1, source_target_pairs={{0,1},{1,2},{2,3},{3,4},{4,5},{5,6},{6,7},{8,9},{9,10},{10,11},{11... | collective-permute-start | bytes 393224 | tf_op jit(solution)/shard_map/ppermute | solution.py:135
  23.8 0.0 collective-permute-done.6
  23.8 3.5 %collective-permute-start.13 = (f32[4,2,8,512]{3,2,1,0:T(8,128)S(1)}, f32[4,2,8,512]{3,2,1,0:T(8,128)S(1)}, u32[]{:S(2)}, u32[]{:S(2)}) collective-permute-start(f32[4,2,8,512]{3,2,1,0:T(8,128)S(1)} %pad_maximum_fusion.1.refs_1_), channel_id=1, source_target_pairs={{0,1},{1,2},{2,3},{3,4},{4,5},{5,6},{6,7},{8,9},{9,10},{10,11},{11... | collective-permute-start | bytes 393224 | tf_op jit(solution)/shard_map/ppermute | solution.py:135
  27.4 0.0 collective-permute-done.10
  27.4 1.9 %collective-permute-start.14 = (f32[4,2,8,512]{3,2,1,0:T(8,128)S(1)}, f32[4,2,8,512]{3,2,1,0:T(8,128)S(1)}, u32[]{:S(2)}, u32[]{:S(2)}) collective-permute-start(f32[4,2,8,512]{3,2,1,0:T(8,128)S(1)} %pad_maximum_fusion.2.refs_2_), channel_id=1, source_target_pairs={{0,1},{1,2},{2,3},{3,4},{4,5},{5,6},{6,7},{8,9},{9,10},{10,11},{11... | collective-permute-start | bytes 393224 | tf_op jit(solution)/shard_map/ppermute | solution.py:135
  29.3 0.0 collective-permute-done.11
  29.3 0.0 collective-permute-done.9
  29.3 1.9 %collective-permute-start.15 = (f32[4,2,8,512]{3,2,1,0:T(8,128)S(1)}, f32[4,2,8,512]{3,2,1,0:T(8,128)S(1)}, u32[]{:S(2)}, u32[]{:S(2)}) collective-permute-start(f32[4,2,8,512]{3,2,1,0:T(8,128)S(1)} %pad_maximum_fusion.3.refs_3_), channel_id=1, source_target_pairs={{0,1},{1,2},{2,3},{3,4},{4,5},{5,6},{6,7},{8,9},{9,10},{10,11},{11... | collective-permute-start | bytes 393224 | tf_op jit(solution)/shard_map/ppermute | solution.py:135
  31.9 0.0 collective-permute-done.12.refs_4_
  31.9 0.0 collective-permute-done.13.refs_5_
  31.9 2.6 %collective-permute-done.14.refs_6_ = f32[4,2,8,512]{3,2,1,0:T(8,128)S(1)} collective-permute-done((f32[4,2,8,512]{3,2,1,0:T(8,128)S(1)}, f32[4,2,8,512]{3,2,1,0:T(8,128)S(1)}, u32[]{:S(2)}, u32[]{:S(2)}) %collective-permute-start.14) | collective-permute-done | bytes 131104 | tf_op jit(solution)/shard_map/ppermute | solution.py:135
  34.5 2.0 %collective-permute-done.15.refs_7_ = f32[4,2,8,512]{3,2,1,0:T(8,128)S(1)} collective-permute-done((f32[4,2,8,512]{3,2,1,0:T(8,128)S(1)}, f32[4,2,8,512]{3,2,1,0:T(8,128)S(1)}, u32[]{:S(2)}, u32[]{:S(2)}) %collective-permute-start.15) | collective-permute-done | bytes 131104 | tf_op jit(solution)/shard_map/ppermute | solution.py:135
  36.5 5.9 %shard_map.55 = f32[4,32,512]{2,1,0:T(8,128)} custom-call(s32[4]{0:T(128)} %seq_ref.1, s32[1]{0:T(128)S(6)} %copy.7.skew_ref, f32[4,2,8,512]{3,2,1,0:T(8,128)S(1)} %pad_maximum_fusion.refs_0_, f32[4,2,8,512]{3,2,1,0:T(8,128)S(1)} %pad_maximum_fusion.1.refs_1_, f32[4,2,8,512]{3,2,1,0:T(8,128)S(1)} %pad_maximum_fusion.2.refs_2_, ...), custom_call_target="tpu_custom_call" | custom-call | tf_op jit(solution)/shard_map/pallas_call | solution.py:139
  (13 shorter events, 0.1 us)
Async XLA Ops:
  0.0 8.9 %copy-start = (f32[2,128,512]{2,1,0:T(8,128)S(1)}, f32[2,128,512]{2,1,0:T(8,128)}, u32[]{:S(2)}) copy-start(f32[2,128,512]{2,1,0:T(8,128)} %param.5) | copy-start | bytes 1572868
  1.8 25.6 %collective-permute-start.10 = (f32[2,8,512]{2,1,0:T(8,128)S(1)}, f32[2,8,512]{2,1,0:T(8,128)S(1)}, u32[]{:S(2)}, u32[]{:S(2)}) collective-permute-start(f32[2,8,512]{2,1,0:T(8,128)S(1)} %get-tuple-element.14), channel_id=1, source_target_pairs={{0,16},{8,24},{16,0},{24,8},{1,17},{9,25},{17,1},{25,9},{2,18},{10... | collective-permute-start | bytes 98312 | tf_op jit(solution)/shard_map/ppermute | solution.py:131
  4.4 5.9 %collective-permute-start.2 = (f32[2,8,512]{2,1,0:T(8,128)S(1)}, f32[2,8,512]{2,1,0:T(8,128)S(1)}, u32[]{:S(2)}, u32[]{:S(2)}) collective-permute-start(f32[2,8,512]{2,1,0:T(8,128)S(1)} %get-tuple-element.16), channel_id=1, source_target_pairs={{0,8},{8,16},{16,24},{24,0},{1,9},{9,17},{17,25},{25,1},{2,10},{10... | collective-permute-start | bytes 98312 | tf_op jit(solution)/shard_map/ppermute | solution.py:131
  6.0 5.2 %collective-permute-start.1 = (f32[2,8,512]{2,1,0:T(8,128)S(1)}, f32[2,8,512]{2,1,0:T(8,128)S(1)}, u32[]{:S(2)}, u32[]{:S(2)}) collective-permute-start(f32[2,8,512]{2,1,0:T(8,128)S(1)} %get-tuple-element.17), channel_id=1, source_target_pairs={{0,16},{8,24},{16,0},{24,8},{1,17},{9,25},{17,1},{25,9},{2,18},{10... | collective-permute-start | bytes 98312 | tf_op jit(solution)/shard_map/ppermute | solution.py:131
  6.3 6.7 %collective-permute-start = (f32[2,8,512]{2,1,0:T(8,128)S(1)}, f32[2,8,512]{2,1,0:T(8,128)S(1)}, u32[]{:S(2)}, u32[]{:S(2)}) collective-permute-start(f32[2,8,512]{2,1,0:T(8,128)S(1)} %get-tuple-element.18), channel_id=1, source_target_pairs={{0,24},{8,0},{16,8},{24,16},{1,25},{9,1},{17,9},{25,17},{2,26},{10... | collective-permute-start | bytes 98312 | tf_op jit(solution)/shard_map/ppermute | solution.py:131
  8.4 20.9 %collective-permute-start.11 = (f32[2,8,512]{2,1,0:T(8,128)S(1)}, f32[2,8,512]{2,1,0:T(8,128)S(1)}, u32[]{:S(2)}, u32[]{:S(2)}) collective-permute-start(f32[2,8,512]{2,1,0:T(8,128)S(1)} %get-tuple-element.20), channel_id=1, source_target_pairs={{0,8},{8,16},{16,24},{24,0},{1,9},{9,17},{17,25},{25,1},{2,10},{10... | collective-permute-start | bytes 98312 | tf_op jit(solution)/shard_map/ppermute | solution.py:131
  10.3 5.8 %collective-permute-start.5 = (f32[2,8,512]{2,1,0:T(8,128)S(1)}, f32[2,8,512]{2,1,0:T(8,128)S(1)}, u32[]{:S(2)}, u32[]{:S(2)}) collective-permute-start(f32[2,8,512]{2,1,0:T(8,128)S(1)} %get-tuple-element.11), channel_id=1, source_target_pairs={{0,8},{8,16},{16,24},{24,0},{1,9},{9,17},{17,25},{25,1},{2,10},{10... | collective-permute-start | bytes 98312 | tf_op jit(solution)/shard_map/ppermute | solution.py:131
  11.2 5.5 %collective-permute-start.4 = (f32[2,8,512]{2,1,0:T(8,128)S(1)}, f32[2,8,512]{2,1,0:T(8,128)S(1)}, u32[]{:S(2)}, u32[]{:S(2)}) collective-permute-start(f32[2,8,512]{2,1,0:T(8,128)S(1)} %get-tuple-element.12), channel_id=1, source_target_pairs={{0,16},{8,24},{16,0},{24,8},{1,17},{9,25},{17,1},{25,9},{2,18},{10... | collective-permute-start | bytes 98312 | tf_op jit(solution)/shard_map/ppermute | solution.py:131
  13.1 4.8 %collective-permute-start.3 = (f32[2,8,512]{2,1,0:T(8,128)S(1)}, f32[2,8,512]{2,1,0:T(8,128)S(1)}, u32[]{:S(2)}, u32[]{:S(2)}) collective-permute-start(f32[2,8,512]{2,1,0:T(8,128)S(1)} %get-tuple-element.13), channel_id=1, source_target_pairs={{0,24},{8,0},{16,8},{24,16},{1,25},{9,1},{17,9},{25,17},{2,26},{10... | collective-permute-start | bytes 98312 | tf_op jit(solution)/shard_map/ppermute | solution.py:131
  16.1 5.7 %collective-permute-start.8 = (f32[2,8,512]{2,1,0:T(8,128)S(1)}, f32[2,8,512]{2,1,0:T(8,128)S(1)}, u32[]{:S(2)}, u32[]{:S(2)}) collective-permute-start(f32[2,8,512]{2,1,0:T(8,128)S(1)} %get-tuple-element.7), channel_id=1, source_target_pairs={{0,8},{8,16},{16,24},{24,0},{1,9},{9,17},{17,25},{25,1},{2,10},{10... | collective-permute-start | bytes 98312 | tf_op jit(solution)/shard_map/ppermute | solution.py:131
  16.7 5.2 %collective-permute-start.7 = (f32[2,8,512]{2,1,0:T(8,128)S(1)}, f32[2,8,512]{2,1,0:T(8,128)S(1)}, u32[]{:S(2)}, u32[]{:S(2)}) collective-permute-start(f32[2,8,512]{2,1,0:T(8,128)S(1)} %get-tuple-element.8), channel_id=1, source_target_pairs={{0,16},{8,24},{16,0},{24,8},{1,17},{9,25},{17,1},{25,9},{2,18},{10... | collective-permute-start | bytes 98312 | tf_op jit(solution)/shard_map/ppermute | solution.py:131
  17.9 5.9 %collective-permute-start.6 = (f32[2,8,512]{2,1,0:T(8,128)S(1)}, f32[2,8,512]{2,1,0:T(8,128)S(1)}, u32[]{:S(2)}, u32[]{:S(2)}) collective-permute-start(f32[2,8,512]{2,1,0:T(8,128)S(1)} %get-tuple-element.9), channel_id=1, source_target_pairs={{0,24},{8,0},{16,8},{24,16},{1,25},{9,1},{17,9},{25,17},{2,26},{10... | collective-permute-start | bytes 98312 | tf_op jit(solution)/shard_map/ppermute | solution.py:131
  21.9 7.4 %collective-permute-start.9 = (f32[2,8,512]{2,1,0:T(8,128)S(1)}, f32[2,8,512]{2,1,0:T(8,128)S(1)}, u32[]{:S(2)}, u32[]{:S(2)}) collective-permute-start(f32[2,8,512]{2,1,0:T(8,128)S(1)} %get-tuple-element.6), channel_id=1, source_target_pairs={{0,24},{8,0},{16,8},{24,16},{1,25},{9,1},{17,9},{25,17},{2,26},{10... | collective-permute-start | bytes 98312 | tf_op jit(solution)/shard_map/ppermute | solution.py:131
  21.9 10.0 %collective-permute-start.12 = (f32[4,2,8,512]{3,2,1,0:T(8,128)S(1)}, f32[4,2,8,512]{3,2,1,0:T(8,128)S(1)}, u32[]{:S(2)}, u32[]{:S(2)}) collective-permute-start(f32[4,2,8,512]{3,2,1,0:T(8,128)S(1)} %pad_maximum_fusion.refs_0_), channel_id=1, source_target_pairs={{0,1},{1,2},{2,3},{3,4},{4,5},{5,6},{6,7},{8,9},{9,10},{10,11},{11... | collective-permute-start | bytes 393224 | tf_op jit(solution)/shard_map/ppermute | solution.py:135
  23.8 8.1 %collective-permute-start.13 = (f32[4,2,8,512]{3,2,1,0:T(8,128)S(1)}, f32[4,2,8,512]{3,2,1,0:T(8,128)S(1)}, u32[]{:S(2)}, u32[]{:S(2)}) collective-permute-start(f32[4,2,8,512]{3,2,1,0:T(8,128)S(1)} %pad_maximum_fusion.1.refs_1_), channel_id=1, source_target_pairs={{0,1},{1,2},{2,3},{3,4},{4,5},{5,6},{6,7},{8,9},{9,10},{10,11},{11... | collective-permute-start | bytes 393224 | tf_op jit(solution)/shard_map/ppermute | solution.py:135
  27.4 7.2 %collective-permute-start.14 = (f32[4,2,8,512]{3,2,1,0:T(8,128)S(1)}, f32[4,2,8,512]{3,2,1,0:T(8,128)S(1)}, u32[]{:S(2)}, u32[]{:S(2)}) collective-permute-start(f32[4,2,8,512]{3,2,1,0:T(8,128)S(1)} %pad_maximum_fusion.2.refs_2_), channel_id=1, source_target_pairs={{0,1},{1,2},{2,3},{3,4},{4,5},{5,6},{6,7},{8,9},{9,10},{10,11},{11... | collective-permute-start | bytes 393224 | tf_op jit(solution)/shard_map/ppermute | solution.py:135
  29.3 7.2 %collective-permute-start.15 = (f32[4,2,8,512]{3,2,1,0:T(8,128)S(1)}, f32[4,2,8,512]{3,2,1,0:T(8,128)S(1)}, u32[]{:S(2)}, u32[]{:S(2)}) collective-permute-start(f32[4,2,8,512]{3,2,1,0:T(8,128)S(1)} %pad_maximum_fusion.3.refs_3_), channel_id=1, source_target_pairs={{0,1},{1,2},{2,3},{3,4},{4,5},{5,6},{6,7},{8,9},{9,10},{10,11},{11... | collective-permute-start | bytes 393224 | tf_op jit(solution)/shard_map/ppermute | solution.py:135

commit v8 on v6

--- a/solution.py
+++ b/solution.py
@@ -121,17 +121,21 @@
     half = share // halves
     line = lax.broadcasted_iota(jnp.int32, (1, half, 1), 1)
     owns, lefts = [], []
+    gate = None
     for c in range(halves):
         held = []
         for m in range(slabs):
             start = ((me - m) % slabs) * share + c * half
             piece = lax.dynamic_slice_in_dim(thermal_grid, start, half, axis=1)
             piece = jnp.where(start + line < occupied_lines[0, 0], piece, EMPTY)
+            if gate is not None:
+                piece = piece + gate
             if m > 0:
                 piece = lax.ppermute(piece, "depth", [(i, (i - m) % slabs) for i in range(slabs)])
             held.append(piece)
         own = jnp.stack(held, axis=0)
         owns.append(own)
+        gate = 0.0 * own[1:, 0, 0, 0].sum()
         lefts.append(lax.ppermute(own, "region", [(i, i + 1) for i in range(regions - 1)]))
     vmem = pltpu.VMEM
     smem = pltpu.SMEM

time: 34.1 us -> 37.6 us (1.10)
  waiting for transfers between devices: 9.4 us -> 16.7 us
  starting transfers between devices: 15.9 us -> 10.9 us
  between operations: 1.43 us -> 2.13 us
  other arithmetic: 1.28 us -> 1.78 us
    ppermute x6, waiting for transfers between devices: 4.14 us -> 10.7 us  [shards(): lax.ppermute(piece, 'depth', [(i, (i - m) % slabs) for i in range(slabs)])]
    ppermute x6, starting transfers between devices: 10.4 us -> 7.03 us  [shards(): lax.ppermute(piece, 'depth', [(i, (i - m) % slabs) for i in range(slabs)])]
    ppermute x2, starting transfers between devices: 5.42 us -> 3.84 us  [shards(): lax.ppermute(own, 'region', [(i, i + 1) for i in range(regions - 1)])]
    another operation x3, other arithmetic: 1.24 us -> 0.14 us  [shards(): own = jnp.stack(held, axis=0)]
    select_n x0 -> x1, other arithmetic: none -> 1.01 us  [shards(): piece = jnp.where(start + line < occupied_lines[0, 0], piece, EMPTY)]
    ppermute x2, waiting for transfers between devices: 5.25 us -> 6.01 us  [shards(): lax.ppermute(own, 'region', [(i, i + 1) for i in range(regions - 1)])]
    reduce_sum x0 -> x1, other arithmetic: none -> 0.6 us  [shards(): gate = 0.0 * own[1:, 0, 0, 0].sum()]
  transfers between devices with their start and end apart: 8 -> 8, of which waited for: 4 -> 7; matrix products, arithmetic and copies ran while one was open for 0% -> 0% of each run, Pallas kernels for 0% -> 0%
where the time goes in v8:
time: 37.6 us; the launch traced here: 37.4 us
  waiting for transfers between devices  16.7 us (44%)
  starting transfers between devices  10.9 us (29%)
  Pallas kernels  5.88 us (16%)
  between operations  2.13 us (6%)
  other arithmetic  1.78 us (5%)
    ppermute x6, waiting for transfers between devices, shards(): lax.ppermute(piece, 'depth', [(i, (i - m) % slabs) for i in range(slabs)])  10.7 us
    ppermute x6, starting transfers between devices, shards(): lax.ppermute(piece, 'depth', [(i, (i - m) % slabs) for i in range(slabs)])  7.03 us
    ppermute x2, waiting for transfers between devices, shards(): lax.ppermute(own, 'region', [(i, i + 1) for i in range(regions - 1)])  6.01 us
    pallas_call x1, Pallas kernels, shards(): pl.pallas_call(render_kernel, out_shape=jax.ShapeDtypeStruct((4, share, w...  5.88 us
    ppermute x2, starting transfers between devices, shards(): lax.ppermute(own, 'region', [(i, i + 1) for i in range(regions - 1)])  3.84 us
    select_n x1, other arithmetic, shards(): piece = jnp.where(start + line < occupied_lines[0, 0], piece, EMPTY)  1.01 us
  transfers between devices with their start and end apart: 8, of which 7 were waited for; matrix products, arithmetic and copies ran while one was open for 0% of the time, Pallas kernels for 0%

profile of v8, /device:TPU:4, one launch (start us, length us, event | category | flops | bytes accessed | tf_op | source)
XLA Modules:
  0.0 37.4 jit_solution(4732445998703148461)
XLA Ops:
  0.0 0.0 copy-start
  0.8 1.0 %dynamic-slice_select_fusion.2 = (f32[2,16,512]{2,1,0:T(8,128)S(1)}, f32[2,16,512]{2,1,0:T(8,128)S(1)}, f32[2,16,512]{2,1,0:T(8,128)S(1)}) fusion(f32[2,128,512]{2,1,0:T(8,128)} %param.5, s32[]{:T(128)S(6)} %select_n.80, pred[16]{0:T(512)(128)(4,1)S(1)} %get-tuple-element.18, s32[]{:T(128)S(6)} %select_n.86, pred[16]{0:T(512)(128)(4,1)S(1)} %get-tuple-element.16, ...), kind=kLoop, calls=%fused_computation.8 | loop fusion | flops 49152 | bytes 393276 | tf_op jit(solution)/shard_map/jit(_where)/select_n | solution.py:130
  1.8 3.7 %collective-permute-start = (f32[2,16,512]{2,1,0:T(8,128)S(1)}, f32[2,16,512]{2,1,0:T(8,128)S(1)}, u32[]{:S(2)}, u32[]{:S(2)}) collective-permute-start(f32[2,16,512]{2,1,0:T(8,128)S(1)} %get-tuple-element.10), channel_id=1, source_target_pairs={{0,24},{8,0},{16,8},{24,16},{1,25},{9,1},{17,9},{25,17},{2,26},{10... | collective-permute-start | bytes 196616 | tf_op jit(solution)/shard_map/ppermute | solution.py:134
  5.4 0.0 collective-permute-start.2
  5.4 1.0 %collective-permute-start.1 = (f32[2,16,512]{2,1,0:T(8,128)S(1)}, f32[2,16,512]{2,1,0:T(8,128)S(1)}, u32[]{:S(2)}, u32[]{:S(2)}) collective-permute-start(f32[2,16,512]{2,1,0:T(8,128)S(1)} %get-tuple-element.12), channel_id=1, source_target_pairs={{0,16},{8,24},{16,0},{24,8},{1,17},{9,25},{17,1},{25,9},{2,18},{10... | collective-permute-start | bytes 196616 | tf_op jit(solution)/shard_map/ppermute | solution.py:134
  6.5 1.4 %collective-permute-done = f32[2,16,512]{2,1,0:T(8,128)S(1)} collective-permute-done((f32[2,16,512]{2,1,0:T(8,128)S(1)}, f32[2,16,512]{2,1,0:T(8,128)S(1)}, u32[]{:S(2)}, u32[]{:S(2)}) %collective-permute-start) | collective-permute-done | bytes 65568 | tf_op jit(solution)/shard_map/ppermute | solution.py:134
  7.9 3.7 %collective-permute-done.2 = f32[2,16,512]{2,1,0:T(8,128)S(1)} collective-permute-done((f32[2,16,512]{2,1,0:T(8,128)S(1)}, f32[2,16,512]{2,1,0:T(8,128)S(1)}, u32[]{:S(2)}, u32[]{:S(2)}) %collective-permute-start.2) | collective-permute-done | bytes 65568 | tf_op jit(solution)/shard_map/ppermute | solution.py:134
  11.6 1.3 %collective-permute-done.1 = f32[2,16,512]{2,1,0:T(8,128)S(1)} collective-permute-done((f32[2,16,512]{2,1,0:T(8,128)S(1)}, f32[2,16,512]{2,1,0:T(8,128)S(1)}, u32[]{:S(2)}, u32[]{:S(2)}) %collective-permute-start.1) | collective-permute-done | bytes 65568 | tf_op jit(solution)/shard_map/ppermute | solution.py:134
  12.9 0.6 %fusion = f32[]{:T(128)} fusion(f32[1,2,16,512]{3,2,1,0:T(8,128)S(1)} %bitcast.18, f32[1,2,16,512]{3,2,1,0:T(8,128)S(1)} %bitcast.20, f32[1,2,16,512]{3,2,1,0:T(8,128)S(1)} %bitcast.16), kind=kLoop, calls=%fused_computation.12 | loop fusion | flops 8 | bytes 196612 | tf_op jit(solution)/shard_map/reduce_sum | solution.py:138
  14.1 0.0 copy-done
  14.1 0.1 add_bitcast_fusion
  14.3 1.7 %collective-permute-start.3 = (f32[2,16,512]{2,1,0:T(8,128)S(1)}, f32[2,16,512]{2,1,0:T(8,128)S(1)}, u32[]{:S(2)}, u32[]{:S(2)}) collective-permute-start(f32[2,16,512]{2,1,0:T(8,128)S(1)} %get-tuple-element.6), channel_id=1, source_target_pairs={{0,24},{8,0},{16,8},{24,16},{1,25},{9,1},{17,9},{25,17},{2,26},{10... | collective-permute-start | bytes 196616 | tf_op jit(solution)/shard_map/ppermute | solution.py:134
  16.0 0.3 collective-permute-start.5
  16.3 0.3 collective-permute-start.4
  16.6 1.9 %collective-permute-start.6 = (f32[4,2,16,512]{3,2,1,0:T(8,128)S(1)}, f32[4,2,16,512]{3,2,1,0:T(8,128)S(1)}, u32[]{:S(2)}, u32[]{:S(2)}) collective-permute-start(f32[4,2,16,512]{3,2,1,0:T(8,128)S(1)} %pad_maximum_fusion.refs_0_), channel_id=1, source_target_pairs={{0,1},{1,2},{2,3},{3,4},{4,5},{5,6},{6,7},{8,9},{9,10},{10,11},{11... | collective-permute-start | bytes 786440 | tf_op jit(solution)/shard_map/ppermute | solution.py:139
  18.6 1.2 %collective-permute-done.3 = f32[2,16,512]{2,1,0:T(8,128)S(1)} collective-permute-done((f32[2,16,512]{2,1,0:T(8,128)S(1)}, f32[2,16,512]{2,1,0:T(8,128)S(1)}, u32[]{:S(2)}, u32[]{:S(2)}) %collective-permute-start.3) | collective-permute-done | bytes 65568 | tf_op jit(solution)/shard_map/ppermute | solution.py:134
  19.8 2.4 %collective-permute-done.5 = f32[2,16,512]{2,1,0:T(8,128)S(1)} collective-permute-done((f32[2,16,512]{2,1,0:T(8,128)S(1)}, f32[2,16,512]{2,1,0:T(8,128)S(1)}, u32[]{:S(2)}, u32[]{:S(2)}) %collective-permute-start.5) | collective-permute-done | bytes 65568 | tf_op jit(solution)/shard_map/ppermute | solution.py:134
  22.2 0.7 %collective-permute-done.4 = f32[2,16,512]{2,1,0:T(8,128)S(1)} collective-permute-done((f32[2,16,512]{2,1,0:T(8,128)S(1)}, f32[2,16,512]{2,1,0:T(8,128)S(1)}, u32[]{:S(2)}, u32[]{:S(2)}) %collective-permute-start.4) | collective-permute-done | bytes 65568 | tf_op jit(solution)/shard_map/ppermute | solution.py:134
  22.9 1.9 %collective-permute-start.7 = (f32[4,2,16,512]{3,2,1,0:T(8,128)S(1)}, f32[4,2,16,512]{3,2,1,0:T(8,128)S(1)}, u32[]{:S(2)}, u32[]{:S(2)}) collective-permute-start(f32[4,2,16,512]{3,2,1,0:T(8,128)S(1)} %pad_maximum_fusion.1.refs_1_), channel_id=1, source_target_pairs={{0,1},{1,2},{2,3},{3,4},{4,5},{5,6},{6,7},{8,9},{9,10},{10,11},{11... | collective-permute-start | bytes 786440 | tf_op jit(solution)/shard_map/ppermute | solution.py:139
  25.5 0.0 collective-permute-done.6.refs_2_
  25.5 6.0 %collective-permute-done.7.refs_3_ = f32[4,2,16,512]{3,2,1,0:T(8,128)S(1)} collective-permute-done((f32[4,2,16,512]{3,2,1,0:T(8,128)S(1)}, f32[4,2,16,512]{3,2,1,0:T(8,128)S(1)}, u32[]{:S(2)}, u32[]{:S(2)}) %collective-permute-start.7) | collective-permute-done | bytes 262176 | tf_op jit(solution)/shard_map/ppermute | solution.py:139
  31.5 5.9 %shard_map.55 = f32[4,32,512]{2,1,0:T(8,128)} custom-call(s32[4]{0:T(128)} %seq_ref.1, s32[1]{0:T(128)S(6)} %copy.7.skew_ref, f32[4,2,16,512]{3,2,1,0:T(8,128)S(1)} %pad_maximum_fusion.refs_0_, f32[4,2,16,512]{3,2,1,0:T(8,128)S(1)} %pad_maximum_fusion.1.refs_1_, f32[4,2,16,512]{3,2,1,0:T(8,128)S(1)} %collective-permute-done.6.refs_2_, ...), custom_call_target="tpu_custom_call" | custom-call | tf_op jit(solution)/shard_map/pallas_call | solution.py:143
  (7 shorter events, 0.1 us)
Async XLA Ops:
  0.0 14.1 %copy-start = (f32[2,128,512]{2,1,0:T(8,128)S(1)}, f32[2,128,512]{2,1,0:T(8,128)}, u32[]{:S(2)}) copy-start(f32[2,128,512]{2,1,0:T(8,128)} %param.5) | copy-start | bytes 1572868
  1.8 6.2 %collective-permute-start = (f32[2,16,512]{2,1,0:T(8,128)S(1)}, f32[2,16,512]{2,1,0:T(8,128)S(1)}, u32[]{:S(2)}, u32[]{:S(2)}) collective-permute-start(f32[2,16,512]{2,1,0:T(8,128)S(1)} %get-tuple-element.10), channel_id=1, source_target_pairs={{0,24},{8,0},{16,8},{24,16},{1,25},{9,1},{17,9},{25,17},{2,26},{10... | collective-permute-start | bytes 196616 | tf_op jit(solution)/shard_map/ppermute | solution.py:134
  5.4 6.2 %collective-permute-start.2 = (f32[2,16,512]{2,1,0:T(8,128)S(1)}, f32[2,16,512]{2,1,0:T(8,128)S(1)}, u32[]{:S(2)}, u32[]{:S(2)}) collective-permute-start(f32[2,16,512]{2,1,0:T(8,128)S(1)} %get-tuple-element.11), channel_id=1, source_target_pairs={{0,8},{8,16},{16,24},{24,0},{1,9},{9,17},{17,25},{25,1},{2,10},{10... | collective-permute-start | bytes 196616 | tf_op jit(solution)/shard_map/ppermute | solution.py:134
  5.4 7.5 %collective-permute-start.1 = (f32[2,16,512]{2,1,0:T(8,128)S(1)}, f32[2,16,512]{2,1,0:T(8,128)S(1)}, u32[]{:S(2)}, u32[]{:S(2)}) collective-permute-start(f32[2,16,512]{2,1,0:T(8,128)S(1)} %get-tuple-element.12), channel_id=1, source_target_pairs={{0,16},{8,24},{16,0},{24,8},{1,17},{9,25},{17,1},{25,9},{2,18},{10... | collective-permute-start | bytes 196616 | tf_op jit(solution)/shard_map/ppermute | solution.py:134
  14.3 5.5 %collective-permute-start.3 = (f32[2,16,512]{2,1,0:T(8,128)S(1)}, f32[2,16,512]{2,1,0:T(8,128)S(1)}, u32[]{:S(2)}, u32[]{:S(2)}) collective-permute-start(f32[2,16,512]{2,1,0:T(8,128)S(1)} %get-tuple-element.6), channel_id=1, source_target_pairs={{0,24},{8,0},{16,8},{24,16},{1,25},{9,1},{17,9},{25,17},{2,26},{10... | collective-permute-start | bytes 196616 | tf_op jit(solution)/shard_map/ppermute | solution.py:134
  16.0 6.2 %collective-permute-start.5 = (f32[2,16,512]{2,1,0:T(8,128)S(1)}, f32[2,16,512]{2,1,0:T(8,128)S(1)}, u32[]{:S(2)}, u32[]{:S(2)}) collective-permute-start(f32[2,16,512]{2,1,0:T(8,128)S(1)} %get-tuple-element.8), channel_id=1, source_target_pairs={{0,8},{8,16},{16,24},{24,0},{1,9},{9,17},{17,25},{25,1},{2,10},{10... | collective-permute-start | bytes 196616 | tf_op jit(solution)/shard_map/ppermute | solution.py:134
  16.3 6.6 %collective-permute-start.4 = (f32[2,16,512]{2,1,0:T(8,128)S(1)}, f32[2,16,512]{2,1,0:T(8,128)S(1)}, u32[]{:S(2)}, u32[]{:S(2)}) collective-permute-start(f32[2,16,512]{2,1,0:T(8,128)S(1)} %get-tuple-element.9), channel_id=1, source_target_pairs={{0,16},{8,24},{16,0},{24,8},{1,17},{9,25},{17,1},{25,9},{2,18},{10... | collective-permute-start | bytes 196616 | tf_op jit(solution)/shard_map/ppermute | solution.py:134
  16.6 8.9 %collective-permute-start.6 = (f32[4,2,16,512]{3,2,1,0:T(8,128)S(1)}, f32[4,2,16,512]{3,2,1,0:T(8,128)S(1)}, u32[]{:S(2)}, u32[]{:S(2)}) collective-permute-start(f32[4,2,16,512]{3,2,1,0:T(8,128)S(1)} %pad_maximum_fusion.refs_0_), channel_id=1, source_target_pairs={{0,1},{1,2},{2,3},{3,4},{4,5},{5,6},{6,7},{8,9},{9,10},{10,11},{11... | collective-permute-start | bytes 786440 | tf_op jit(solution)/shard_map/ppermute | solution.py:139
  22.9 8.6 %collective-permute-start.7 = (f32[4,2,16,512]{3,2,1,0:T(8,128)S(1)}, f32[4,2,16,512]{3,2,1,0:T(8,128)S(1)}, u32[]{:S(2)}, u32[]{:S(2)}) collective-permute-start(f32[4,2,16,512]{3,2,1,0:T(8,128)S(1)} %pad_maximum_fusion.1.refs_1_), channel_id=1, source_target_pairs={{0,1},{1,2},{2,3},{3,4},{4,5},{5,6},{6,7},{8,9},{9,10},{10,11},{11... | collective-permute-start | bytes 786440 | tf_op jit(solution)/shard_map/ppermute | solution.py:139

commit v9 on v6

--- a/solution.py
+++ b/solution.py
@@ -10,6 +10,18 @@
 EMPTY = 1.0e6
 LANES = 128
 SUBLANES = 8
+
+
+def partner(i, m, n, sign=1):
+    if n & (n - 1) == 0:
+        return i ^ m
+    return (i + sign * m) % n
+
+
+def slot_of(s, me, n):
+    if n & (n - 1) == 0:
+        return s ^ me
+    return (s - me + n) % n
 
 
 def lookup(cells, tables, knot_count):
@@ -47,7 +59,7 @@
         s = jnp.int32(0)
         for j in range(slabs):
             s = s + jnp.where(seq_ref[j] == k, j, 0)
-        order.append((s - me + slabs) % slabs)
+        order.append(slot_of(s, me, slabs))
 
     for k in range(slabs):
         s = order[k]
@@ -124,11 +136,12 @@
     for c in range(halves):
         held = []
         for m in range(slabs):
-            start = ((me - m) % slabs) * share + c * half
+            start = partner(me, m, slabs, -1) * share + c * half
             piece = lax.dynamic_slice_in_dim(thermal_grid, start, half, axis=1)
             piece = jnp.where(start + line < occupied_lines[0, 0], piece, EMPTY)
             if m > 0:
-                piece = lax.ppermute(piece, "depth", [(i, (i - m) % slabs) for i in range(slabs)])
+                route = [(i, partner(i, m, slabs, -1)) for i in range(slabs)]
+                piece = lax.ppermute(piece, "depth", route)
             held.append(piece)
         own = jnp.stack(held, axis=0)
         owns.append(own)

time: 34.1 us -> 33 us (0.968)
  starting transfers between devices: 15.9 us -> 13.4 us
  waiting for transfers between devices: 9.4 us -> 10.9 us
    ppermute x6, starting transfers between devices: 10.4 us -> 8.62 us  [shards(): piece = lax.ppermute(piece, 'depth', route)]
    ppermute x6, waiting for transfers between devices: 4.14 us -> 5.6 us  [shards(): piece = lax.ppermute(piece, 'depth', route)]
    ppermute x2, starting transfers between devices: 5.42 us -> 4.73 us  [shards(): lax.ppermute(own, 'region', [(i, i + 1) for i in range(regions - 1)])]
where the time goes in v9:
time: 33 us; the launch traced here: 32.8 us
  starting transfers between devices  13.4 us (41%)
  waiting for transfers between devices  10.9 us (33%)
  Pallas kernels  5.88 us (18%)
  between operations  1.4 us (4%)
  other arithmetic  1.28 us (4%)
    ppermute x6, starting transfers between devices, shards(): piece = lax.ppermute(piece, 'depth', route)  8.62 us
    pallas_call x1, Pallas kernels, shards(): pl.pallas_call(render_kernel, out_shape=jax.ShapeDtypeStruct((4, share, w...  5.88 us
    ppermute x6, waiting for transfers between devices, shards(): piece = lax.ppermute(piece, 'depth', route)  5.6 us
    ppermute x2, waiting for transfers between devices, shards(): lax.ppermute(own, 'region', [(i, i + 1) for i in range(regions - 1)])  5.25 us
    ppermute x2, starting transfers between devices, shards(): lax.ppermute(own, 'region', [(i, i + 1) for i in range(regions - 1)])  4.73 us
    another operation x3, other arithmetic, shards(): own = jnp.stack(held, axis=0)  1.24 us
  transfers between devices with their start and end apart: 8, of which 4 were waited for; matrix products, arithmetic and copies ran while one was open for 0% of the time, Pallas kernels for 0%

profile of v9, /device:TPU:4, one launch (start us, length us, event | category | flops | bytes accessed | tf_op | source)
XLA Modules:
  0.0 32.8 jit_solution(7975746372385537050)
XLA Ops:
  0.7 1.2 %select_bitcast_fusion = (f32[1,2,16,512]{3,2,1,0:T(8,128)S(1)}, f32[2,16,512]{2,1,0:T(8,128)S(1)}, f32[2,16,512]{2,1,0:T(8,128)S(1)}, f32[2,16,512]{2,1,0:T(8,1...) fusion(f32[2,128,512]{2,1,0:T(8,128)} %param.5, ...), kind=kLoop, calls=%fused_computation.5 | loop fusion | flops 131072 | bytes 1048736 | tf_op jit(solution)/shard_map/stack | solution.py:146
  2.0 1.6 %collective-permute-start.3 = (f32[2,16,512]{2,1,0:T(8,128)S(1)}, f32[2,16,512]{2,1,0:T(8,128)S(1)}, u32[]{:S(2)}, u32[]{:S(2)}) collective-permute-start(f32[2,16,512]{2,1,0:T(8,128)S(1)} %get-tuple-element.6), channel_id=1, source_target_pairs={{0,8},{8,0},{16,24},{24,16},{1,9},{9,1},{17,25},{25,17},{2,10},{10... | collective-permute-start | bytes 196616 | tf_op jit(solution)/shard_map/ppermute | solution.py:144
  3.6 2.5 %collective-permute-start.5 = (f32[2,16,512]{2,1,0:T(8,128)S(1)}, f32[2,16,512]{2,1,0:T(8,128)S(1)}, u32[]{:S(2)}, u32[]{:S(2)}) collective-permute-start(f32[2,16,512]{2,1,0:T(8,128)S(1)} %get-tuple-element.11), channel_id=1, source_target_pairs={{0,24},{8,16},{16,8},{24,0},{1,25},{9,17},{17,9},{25,1},{2,26},{10... | collective-permute-start | bytes 196616 | tf_op jit(solution)/shard_map/ppermute | solution.py:144
  6.1 0.1 collective-permute-start.4
  6.2 2.9 %collective-permute-start.2 = (f32[2,16,512]{2,1,0:T(8,128)S(1)}, f32[2,16,512]{2,1,0:T(8,128)S(1)}, u32[]{:S(2)}, u32[]{:S(2)}) collective-permute-start(f32[2,16,512]{2,1,0:T(8,128)S(1)} %get-tuple-element.7), channel_id=1, source_target_pairs={{0,24},{8,16},{16,8},{24,0},{1,25},{9,17},{17,9},{25,1},{2,26},{10... | collective-permute-start | bytes 196616 | tf_op jit(solution)/shard_map/ppermute | solution.py:144
  9.1 0.3 %collective-permute-start.1 = (f32[2,16,512]{2,1,0:T(8,128)S(1)}, f32[2,16,512]{2,1,0:T(8,128)S(1)}, u32[]{:S(2)}, u32[]{:S(2)}) collective-permute-start(f32[2,16,512]{2,1,0:T(8,128)S(1)} %get-tuple-element.8), channel_id=1, source_target_pairs={{0,16},{8,24},{16,0},{24,8},{1,17},{9,25},{17,1},{25,9},{2,18},{10... | collective-permute-start | bytes 196616 | tf_op jit(solution)/shard_map/ppermute | solution.py:144
  9.5 0.0 collective-permute-done.3
  9.5 1.1 %collective-permute-start = (f32[2,16,512]{2,1,0:T(8,128)S(1)}, f32[2,16,512]{2,1,0:T(8,128)S(1)}, u32[]{:S(2)}, u32[]{:S(2)}) collective-permute-start(f32[2,16,512]{2,1,0:T(8,128)S(1)} %get-tuple-element.9), channel_id=1, source_target_pairs={{0,8},{8,0},{16,24},{24,16},{1,9},{9,1},{17,25},{25,17},{2,10},{10... | collective-permute-start | bytes 196616 | tf_op jit(solution)/shard_map/ppermute | solution.py:144
  10.6 0.0 collective-permute-done.5
  10.6 4.9 %collective-permute-done.4 = f32[2,16,512]{2,1,0:T(8,128)S(1)} collective-permute-done((f32[2,16,512]{2,1,0:T(8,128)S(1)}, f32[2,16,512]{2,1,0:T(8,128)S(1)}, u32[]{:S(2)}, u32[]{:S(2)}) %collective-permute-start.4) | collective-permute-done | bytes 65568 | tf_op jit(solution)/shard_map/ppermute | solution.py:144
  15.5 1.9 %collective-permute-start.7 = (f32[4,2,16,512]{3,2,1,0:T(8,128)S(1)}, f32[4,2,16,512]{3,2,1,0:T(8,128)S(1)}, u32[]{:S(2)}, u32[]{:S(2)}) collective-permute-start(f32[4,2,16,512]{3,2,1,0:T(8,128)S(1)} %pad_maximum_fusion.1.refs_1_), channel_id=1, source_target_pairs={{0,1},{1,2},{2,3},{3,4},{4,5},{5,6},{6,7},{8,9},{9,10},{10,11},{11... | collective-permute-start | bytes 786440 | tf_op jit(solution)/shard_map/ppermute | solution.py:148
  17.4 0.0 collective-permute-done.2
  17.4 0.7 %collective-permute-done.1 = f32[2,16,512]{2,1,0:T(8,128)S(1)} collective-permute-done((f32[2,16,512]{2,1,0:T(8,128)S(1)}, f32[2,16,512]{2,1,0:T(8,128)S(1)}, u32[]{:S(2)}, u32[]{:S(2)}) %collective-permute-start.1) | collective-permute-done | bytes 65568 | tf_op jit(solution)/shard_map/ppermute | solution.py:144
  18.1 0.0 collective-permute-done
  18.2 2.8 %collective-permute-start.6 = (f32[4,2,16,512]{3,2,1,0:T(8,128)S(1)}, f32[4,2,16,512]{3,2,1,0:T(8,128)S(1)}, u32[]{:S(2)}, u32[]{:S(2)}) collective-permute-start(f32[4,2,16,512]{3,2,1,0:T(8,128)S(1)} %pad_maximum_fusion.refs_0_), channel_id=1, source_target_pairs={{0,1},{1,2},{2,3},{3,4},{4,5},{5,6},{6,7},{8,9},{9,10},{10,11},{11... | collective-permute-start | bytes 786440 | tf_op jit(solution)/shard_map/ppermute | solution.py:148
  21.6 2.4 %collective-permute-done.7.refs_3_ = f32[4,2,16,512]{3,2,1,0:T(8,128)S(1)} collective-permute-done((f32[4,2,16,512]{3,2,1,0:T(8,128)S(1)}, f32[4,2,16,512]{3,2,1,0:T(8,128)S(1)}, u32[]{:S(2)}, u32[]{:S(2)}) %collective-permute-start.7) | collective-permute-done | bytes 262176 | tf_op jit(solution)/shard_map/ppermute | solution.py:148
  24.1 2.8 %collective-permute-done.6.refs_2_ = f32[4,2,16,512]{3,2,1,0:T(8,128)S(1)} collective-permute-done((f32[4,2,16,512]{3,2,1,0:T(8,128)S(1)}, f32[4,2,16,512]{3,2,1,0:T(8,128)S(1)}, u32[]{:S(2)}, u32[]{:S(2)}) %collective-permute-start.6) | collective-permute-done | bytes 262176 | tf_op jit(solution)/shard_map/ppermute | solution.py:148
  26.9 5.9 %shard_map.55 = f32[4,32,512]{2,1,0:T(8,128)} custom-call(s32[4]{0:T(128)} %seq_ref.1, s32[1]{0:T(128)S(6)} %copy.7.skew_ref, f32[4,2,16,512]{3,2,1,0:T(8,128)S(1)} %pad_maximum_fusion.refs_0_, f32[4,2,16,512]{3,2,1,0:T(8,128)S(1)} %pad_maximum_fusion.1.refs_1_, f32[4,2,16,512]{3,2,1,0:T(8,128)S(1)} %collective-permute-done.6.refs_2_, ...), custom_call_target="tpu_custom_call" | custom-call | tf_op jit(solution)/shard_map/pallas_call | solution.py:152
  (6 shorter events, 0.1 us)
Async XLA Ops:
  2.0 7.5 %collective-permute-start.3 = (f32[2,16,512]{2,1,0:T(8,128)S(1)}, f32[2,16,512]{2,1,0:T(8,128)S(1)}, u32[]{:S(2)}, u32[]{:S(2)}) collective-permute-start(f32[2,16,512]{2,1,0:T(8,128)S(1)} %get-tuple-element.6), channel_id=1, source_target_pairs={{0,8},{8,0},{16,24},{24,16},{1,9},{9,1},{17,25},{25,17},{2,10},{10... | collective-permute-start | bytes 196616 | tf_op jit(solution)/shard_map/ppermute | solution.py:144
  3.6 7.0 %collective-permute-start.5 = (f32[2,16,512]{2,1,0:T(8,128)S(1)}, f32[2,16,512]{2,1,0:T(8,128)S(1)}, u32[]{:S(2)}, u32[]{:S(2)}) collective-permute-start(f32[2,16,512]{2,1,0:T(8,128)S(1)} %get-tuple-element.11), channel_id=1, source_target_pairs={{0,24},{8,16},{16,8},{24,0},{1,25},{9,17},{17,9},{25,1},{2,26},{10... | collective-permute-start | bytes 196616 | tf_op jit(solution)/shard_map/ppermute | solution.py:144
  6.1 9.4 %collective-permute-start.4 = (f32[2,16,512]{2,1,0:T(8,128)S(1)}, f32[2,16,512]{2,1,0:T(8,128)S(1)}, u32[]{:S(2)}, u32[]{:S(2)}) collective-permute-start(f32[2,16,512]{2,1,0:T(8,128)S(1)} %get-tuple-element.12), channel_id=1, source_target_pairs={{0,16},{8,24},{16,0},{24,8},{1,17},{9,25},{17,1},{25,9},{2,18},{10... | collective-permute-start | bytes 196616 | tf_op jit(solution)/shard_map/ppermute | solution.py:144
  6.2 11.2 %collective-permute-start.2 = (f32[2,16,512]{2,1,0:T(8,128)S(1)}, f32[2,16,512]{2,1,0:T(8,128)S(1)}, u32[]{:S(2)}, u32[]{:S(2)}) collective-permute-start(f32[2,16,512]{2,1,0:T(8,128)S(1)} %get-tuple-element.7), channel_id=1, source_target_pairs={{0,24},{8,16},{16,8},{24,0},{1,25},{9,17},{17,9},{25,1},{2,26},{10... | collective-permute-start | bytes 196616 | tf_op jit(solution)/shard_map/ppermute | solution.py:144
  9.1 9.0 %collective-permute-start.1 = (f32[2,16,512]{2,1,0:T(8,128)S(1)}, f32[2,16,512]{2,1,0:T(8,128)S(1)}, u32[]{:S(2)}, u32[]{:S(2)}) collective-permute-start(f32[2,16,512]{2,1,0:T(8,128)S(1)} %get-tuple-element.8), channel_id=1, source_target_pairs={{0,16},{8,24},{16,0},{24,8},{1,17},{9,25},{17,1},{25,9},{2,18},{10... | collective-permute-start | bytes 196616 | tf_op jit(solution)/shard_map/ppermute | solution.py:144
  9.5 8.7 %collective-permute-start = (f32[2,16,512]{2,1,0:T(8,128)S(1)}, f32[2,16,512]{2,1,0:T(8,128)S(1)}, u32[]{:S(2)}, u32[]{:S(2)}) collective-permute-start(f32[2,16,512]{2,1,0:T(8,128)S(1)} %get-tuple-element.9), channel_id=1, source_target_pairs={{0,8},{8,0},{16,24},{24,16},{1,9},{9,1},{17,25},{25,17},{2,10},{10... | collective-permute-start | bytes 196616 | tf_op jit(solution)/shard_map/ppermute | solution.py:144
  15.5 8.6 %collective-permute-start.7 = (f32[4,2,16,512]{3,2,1,0:T(8,128)S(1)}, f32[4,2,16,512]{3,2,1,0:T(8,128)S(1)}, u32[]{:S(2)}, u32[]{:S(2)}) collective-permute-start(f32[4,2,16,512]{3,2,1,0:T(8,128)S(1)} %pad_maximum_fusion.1.refs_1_), channel_id=1, source_target_pairs={{0,1},{1,2},{2,3},{3,4},{4,5},{5,6},{6,7},{8,9},{9,10},{10,11},{11... | collective-permute-start | bytes 786440 | tf_op jit(solution)/shard_map/ppermute | solution.py:148
  18.2 8.7 %collective-permute-start.6 = (f32[4,2,16,512]{3,2,1,0:T(8,128)S(1)}, f32[4,2,16,512]{3,2,1,0:T(8,128)S(1)}, u32[]{:S(2)}, u32[]{:S(2)}) collective-permute-start(f32[4,2,16,512]{3,2,1,0:T(8,128)S(1)} %pad_maximum_fusion.refs_0_), channel_id=1, source_target_pairs={{0,1},{1,2},{2,3},{3,4},{4,5},{5,6},{6,7},{8,9},{9,10},{10,11},{11... | collective-permute-start | bytes 786440 | tf_op jit(solution)/shard_map/ppermute | solution.py:148

commit v10 on v9

--- a/solution.py
+++ b/solution.py
@@ -43,9 +43,9 @@
 
 
 def render_kernel(seq_ref, skew_ref, *refs):
-    halves = (len(refs) - 3) // 2
+    halves = (len(refs) - 4) // 2
     own_refs, left_refs = refs[:halves], refs[halves : 2 * halves]
-    cmap_ref, out_ref, shifted_ref = refs[2 * halves :]
+    left_first_ref, cmap_ref, out_ref, shifted_ref = refs[2 * halves :]
     slabs, layers, half_rows, width = own_refs[0].shape
     rows = half_rows * halves
     layers_overall = layers * slabs
@@ -69,7 +69,12 @@
                 band = pl.ds(r * SUBLANES, SUBLANES)
                 c, rest = divmod(r * SUBLANES, half_rows)
                 part = pl.ds(rest, SUBLANES)
-                left = jnp.where(first_tile, EMPTY, left_refs[c][s, l, part, :])
+                left = jnp.where(
+                    s == 0,
+                    left_first_ref[l, band, :],
+                    left_refs[c][jnp.maximum(s - 1, 0), l, part, :],
+                )
+                left = jnp.where(first_tile, EMPTY, left)
                 joined = jnp.concatenate([left, own_refs[c][s, l, part, :]], axis=1)
                 shifted_ref[l, k, band, :] = pltpu.roll(joined, shift, 1)[:, width:]
 
@@ -132,23 +137,26 @@
     halves = 2 if share % (2 * SUBLANES) == 0 else 1
     half = share // halves
     line = lax.broadcasted_iota(jnp.int32, (1, half, 1), 1)
+    to_right = [(i, i + 1) for i in range(regions - 1)]
+    own_rows = me * share
+    first = lax.dynamic_slice_in_dim(thermal_grid, own_rows, share, axis=1)
+    first = jnp.where(own_rows + lax.broadcasted_iota(jnp.int32, (1, share, 1), 1) < occupied_lines[0, 0], first, EMPTY)
+    left_first = lax.ppermute(first, "region", to_right)
+    gate = 0.0 * left_first[0, 0, 0]
     owns, lefts = [], []
     for c in range(halves):
-        held = []
-        for m in range(slabs):
+        held = [first[:, c * half : (c + 1) * half]]
+        for m in range(1, slabs):
             start = partner(me, m, slabs, -1) * share + c * half
             piece = lax.dynamic_slice_in_dim(thermal_grid, start, half, axis=1)
             piece = jnp.where(start + line < occupied_lines[0, 0], piece, EMPTY)
-            if m > 0:
-                route = [(i, partner(i, m, slabs, -1)) for i in range(slabs)]
-                piece = lax.ppermute(piece, "depth", route)
-            held.append(piece)
-        own = jnp.stack(held, axis=0)
-        owns.append(own)
-        lefts.append(lax.ppermute(own, "region", [(i, i + 1) for i in range(regions - 1)]))
+            route = [(i, partner(i, m, slabs, -1)) for i in range(slabs)]
+            held.append(lax.ppermute(piece, "depth", route))
+        owns.append(jnp.stack(held, axis=0))
+        lefts.append(lax.ppermute(jnp.stack(held[1:], axis=0) + gate, "region", to_right))
     vmem = pltpu.VMEM
     smem = pltpu.SMEM
-    placed = [pltpu.with_memory_space_constraint(x, vmem) for x in owns + lefts]
+    placed = [pltpu.with_memory_space_constraint(x, vmem) for x in owns + lefts + [left_first]]
     return pl.pallas_call(
         render_kernel,
         out_shape=jax.ShapeDtypeStruct((4, share, width), jnp.float32),
@@ -156,7 +164,7 @@
             pl.BlockSpec(memory_space=smem),
             pl.BlockSpec(memory_space=smem),
         ]
-        + [pl.BlockSpec(memory_space=vmem)] * (2 * halves + 1),
+        + [pl.BlockSpec(memory_space=vmem)] * (2 * halves + 2),
         out_specs=pl.BlockSpec(memory_space=vmem),
         scratch_shapes=[pltpu.VMEM((layers, slabs, share, width), jnp.float32)],
     )(sheetgroup_viewer_sequence, skew_offsets, *placed, colormap_samples)

time: 33 us -> 35.9 us (1.088)
  starting transfers between devices: 13.4 us -> 15.9 us
  waiting for transfers between devices: 10.9 us -> 8.9 us
  other arithmetic: 1.28 us -> 2.22 us
  between operations: 1.4 us -> 2.14 us
  local copies, waits for them, and re-layouts: 0 us -> 0.52 us
    ppermute x8 -> x9, starting transfers between devices: 13.4 us -> 15.9 us  [the longest x6 9.69 us: shards(): held.append(lax.ppermute(piece, 'depth', route))]
    select_n x0 -> x2, other arithmetic: none -> 2.12 us  [the longest x1 1.13 us: shards(): piece = jnp.where(start + line < occupied_lines[0, 0], piece, EMPTY)]
    ppermute x8 -> x9, waiting for transfers between devices: 10.9 us -> 8.9 us  [the longest x2 5.8 us: shards(): lax.ppermute(jnp.stack(held[1:], axis=0) + gate, 'region', to_right)]
    another operation x3 -> x2, other arithmetic: 1.24 us -> 0.04 us  [shards(): owns.append(jnp.stack(held, axis=0))]
    slice x0 -> x1, local copies, waits for them, and re-layouts: none -> 0.51 us  [shards(): gate = 0.0 * left_first[0, 0, 0]]
  transfers between devices with their start and end apart: 8 -> 9, of which waited for: 4 -> 3; matrix products, arithmetic and copies ran while one was open for 0% -> 5% of each run, Pallas kernels for 0% -> 0%
where the time goes in v10:
time: 35.9 us; the launch traced here: 35.6 us
  starting transfers between devices  15.9 us (44%)
  waiting for transfers between devices  8.9 us (25%)
  Pallas kernels  5.88 us (16%)
  other arithmetic  2.22 us (6%)
  between operations  2.14 us (6%)
  local copies, waits for them, and re-layouts  0.52 us (1%)
    ppermute x6, starting transfers between devices, shards(): held.append(lax.ppermute(piece, 'depth', route))  9.69 us
    pallas_call x1, Pallas kernels, shards(): pl.pallas_call(render_kernel, out_shape=jax.ShapeDtypeStruct((4, share, w...  5.88 us
    ppermute x2, waiting for transfers between devices, shards(): lax.ppermute(jnp.stack(held[1:], axis=0) + gate, 'region', to_right)  5.8 us
    ppermute x2, starting transfers between devices, shards(): lax.ppermute(jnp.stack(held[1:], axis=0) + gate, 'region', to_right)  4.28 us
    ppermute x6, waiting for transfers between devices, shards(): held.append(lax.ppermute(piece, 'depth', route))  3.1 us
    ppermute x1, starting transfers between devices, shards(): left_first = lax.ppermute(first, 'region', to_right)  1.92 us
    select_n x1, other arithmetic, shards(): piece = jnp.where(start + line < occupied_lines[0, 0], piece, EMPTY)  1.13 us
    select_n x1, other arithmetic, shards(): jnp.where(own_rows + lax.broadcasted_iota(jnp.int32, (1, share, 1), 1) <...  1 us
  transfers between devices with their start and end apart: 9, of which 3 were waited for; matrix products, arithmetic and copies ran while one was open for 5% of the time, Pallas kernels for 0%

profile of v10, /device:TPU:4, one launch (start us, length us, event | category | flops | bytes accessed | tf_op | source)
XLA Modules:
  0.0 35.6 jit_solution(4612763433359500213)
XLA Ops:
  0.7 1.0 %dynamic-slice_select_fusion = f32[2,32,512]{2,1,0:T(8,128)S(1)} fusion(f32[2,128,512]{2,1,0:T(8,128)} %param.5, s32[]{:T(128)S(6)} %select_n.44, pred[32]{0:T(512)(128)(4,1)S(1)} %add_compare_fusion.6), kind=kLoop, calls=%fused_computation.4 | loop fusion | flops 32768 | bytes 262180 | tf_op jit(solution)/shard_map/jit(_where)/select_n | solution.py:143
  1.7 1.9 %collective-permute-start.6 = (f32[2,32,512]{2,1,0:T(8,128)S(1)}, f32[2,32,512]{2,1,0:T(8,128)S(1)}, u32[]{:S(2)}, u32[]{:S(2)}) collective-permute-start(f32[2,32,512]{2,1,0:T(8,128)S(1)} %dynamic-slice_select_fusion), channel_id=1, source_target_pairs={{0,1},{1,2},{2,3},{3,4},{4,5},{5,6},{6,7},{8,9},{9,10},{10,11},{11... | collective-permute-start | bytes 393224 | tf_op jit(solution)/shard_map/ppermute | solution.py:144
  3.7 1.1 %dynamic-slice_select_fusion.3 = (f32[2,16,512]{2,1,0:T(8,128)S(1)}, f32[2,16,512]{2,1,0:T(8,128)S(1)}, f32[2,16,512]{2,1,0:T(8,128)S(1)}, f32[2,16,512]{2,1,0:T...) fusion(f32[2,128,512]{2,1,0:T(8,128)} %param.5, s32[]{:T(128)S(6)} %select_n.52, ...), kind=kLoop, calls=%fused_computation.9 | loop fusion | flops 98304 | bytes 786552 | tf_op jit(solution)/shard_map/jit(_where)/select_n | solution.py:152
  4.8 1.6 %collective-permute-start.3 = (f32[2,16,512]{2,1,0:T(8,128)S(1)}, f32[2,16,512]{2,1,0:T(8,128)S(1)}, u32[]{:S(2)}, u32[]{:S(2)}) collective-permute-start(f32[2,16,512]{2,1,0:T(8,128)S(1)} %get-tuple-element.5), channel_id=1, source_target_pairs={{0,8},{8,0},{16,24},{24,16},{1,9},{9,1},{17,25},{25,17},{2,10},{10... | collective-permute-start | bytes 196616 | tf_op jit(solution)/shard_map/ppermute | solution.py:154
  6.5 2.5 %collective-permute-start.2 = (f32[2,16,512]{2,1,0:T(8,128)S(1)}, f32[2,16,512]{2,1,0:T(8,128)S(1)}, u32[]{:S(2)}, u32[]{:S(2)}) collective-permute-start(f32[2,16,512]{2,1,0:T(8,128)S(1)} %get-tuple-element.6), channel_id=1, source_target_pairs={{0,24},{8,16},{16,8},{24,0},{1,25},{9,17},{17,9},{25,1},{2,26},{10... | collective-permute-start | bytes 196616 | tf_op jit(solution)/shard_map/ppermute | solution.py:154
  8.9 0.1 collective-permute-start.1
  9.1 1.8 %collective-permute-start = (f32[2,16,512]{2,1,0:T(8,128)S(1)}, f32[2,16,512]{2,1,0:T(8,128)S(1)}, u32[]{:S(2)}, u32[]{:S(2)}) collective-permute-start(f32[2,16,512]{2,1,0:T(8,128)S(1)} %get-tuple-element.8), channel_id=1, source_target_pairs={{0,8},{8,0},{16,24},{24,16},{1,9},{9,1},{17,25},{25,17},{2,10},{10... | collective-permute-start | bytes 196616 | tf_op jit(solution)/shard_map/ppermute | solution.py:154
  11.5 0.0 collective-permute-done.6.refs_4_
  11.5 2.5 %collective-permute-start.5 = (f32[2,16,512]{2,1,0:T(8,128)S(1)}, f32[2,16,512]{2,1,0:T(8,128)S(1)}, u32[]{:S(2)}, u32[]{:S(2)}) collective-permute-start(f32[2,16,512]{2,1,0:T(8,128)S(1)} %get-tuple-element.9), channel_id=1, source_target_pairs={{0,24},{8,16},{16,8},{24,0},{1,25},{9,17},{17,9},{25,1},{2,26},{10... | collective-permute-start | bytes 196616 | tf_op jit(solution)/shard_map/ppermute | solution.py:154
  14.1 0.5 %slice.14 = f32[1,1,1]{2,1,0:T(1,128)} slice(f32[2,32,512]{2,1,0:T(8,128)S(1)} %collective-permute-done.6.refs_4_), slice={[0:1], [0:1], [0:1]} | slice | bytes 8 | tf_op jit(solution)/shard_map/slice | solution.py:145
  15.2 0.0 collective-permute-done.2
  15.2 1.1 %collective-permute-start.4 = (f32[2,16,512]{2,1,0:T(8,128)S(1)}, f32[2,16,512]{2,1,0:T(8,128)S(1)}, u32[]{:S(2)}, u32[]{:S(2)}) collective-permute-start(f32[2,16,512]{2,1,0:T(8,128)S(1)} %get-tuple-element.10), channel_id=1, source_target_pairs={{0,16},{8,24},{16,0},{24,8},{1,17},{9,25},{17,1},{25,9},{2,18},{10... | collective-permute-start | bytes 196616 | tf_op jit(solution)/shard_map/ppermute | solution.py:154
  16.4 0.0 collective-permute-done.1
  16.4 0.0 collective-permute-done
  16.4 2.3 %collective-permute-start.7 = (f32[3,2,16,512]{3,2,1,0:T(8,128)S(1)}, f32[3,2,16,512]{3,2,1,0:T(8,128)S(1)}, u32[]{:S(2)}, u32[]{:S(2)}) collective-permute-start(f32[3,2,16,512]{3,2,1,0:T(8,128)S(1)} %maximum_add_fusion), channel_id=1, source_target_pairs={{0,1},{1,2},{2,3},{3,4},{4,5},{5,6},{6,7},{8,9},{9,10},{10,11},{11... | collective-permute-start | bytes 589832 | tf_op jit(solution)/shard_map/ppermute | solution.py:156
  18.7 0.0 collective-permute-done.3
  18.7 0.0 collective-permute-done.5
  18.7 3.1 %collective-permute-done.4 = f32[2,16,512]{2,1,0:T(8,128)S(1)} collective-permute-done((f32[2,16,512]{2,1,0:T(8,128)S(1)}, f32[2,16,512]{2,1,0:T(8,128)S(1)}, u32[]{:S(2)}, u32[]{:S(2)}) %collective-permute-start.4) | collective-permute-done | bytes 65568 | tf_op jit(solution)/shard_map/ppermute | solution.py:154
  21.8 2.0 %collective-permute-start.8 = (f32[3,2,16,512]{3,2,1,0:T(8,128)S(1)}, f32[3,2,16,512]{3,2,1,0:T(8,128)S(1)}, u32[]{:S(2)}, u32[]{:S(2)}) collective-permute-start(f32[3,2,16,512]{3,2,1,0:T(8,128)S(1)} %maximum_add_fusion.1), channel_id=1, source_target_pairs={{0,1},{1,2},{2,3},{3,4},{4,5},{5,6},{6,7},{8,9},{9,10},{10,11},{11... | collective-permute-start | bytes 589832 | tf_op jit(solution)/shard_map/ppermute | solution.py:156
  23.9 0.4 %collective-permute-done.7.refs_2_ = f32[3,2,16,512]{3,2,1,0:T(8,128)S(1)} collective-permute-done((f32[3,2,16,512]{3,2,1,0:T(8,128)S(1)}, f32[3,2,16,512]{3,2,1,0:T(8,128)S(1)}, u32[]{:S(2)}, u32[]{:S(2)}) %collective-permute-start.7) | collective-permute-done | bytes 196640 | tf_op jit(solution)/shard_map/ppermute | solution.py:156
  24.3 5.4 %collective-permute-done.8.refs_3_ = f32[3,2,16,512]{3,2,1,0:T(8,128)S(1)} collective-permute-done((f32[3,2,16,512]{3,2,1,0:T(8,128)S(1)}, f32[3,2,16,512]{3,2,1,0:T(8,128)S(1)}, u32[]{:S(2)}, u32[]{:S(2)}) %collective-permute-start.8) | collective-permute-done | bytes 196640 | tf_op jit(solution)/shard_map/ppermute | solution.py:156
  29.7 5.9 %shard_map.55 = f32[4,32,512]{2,1,0:T(8,128)} custom-call(s32[4]{0:T(128)} %seq_ref.1, s32[1]{0:T(128)S(6)} %copy.7.skew_ref, f32[4,2,16,512]{3,2,1,0:T(8,128)S(1)} %pad_maximum_fusion.refs_0_, f32[4,2,16,512]{3,2,1,0:T(8,128)S(1)} %pad_maximum_fusion.1.refs_1_, f32[3,2,16,512]{3,2,1,0:T(8,128)S(1)} %collective-permute-done.7.refs_2_, ...), custom_call_target="tpu_custom_call" | custom-call | tf_op jit(solution)/shard_map/pallas_call | solution.py:160
  (9 shorter events, 0.1 us)
Async XLA Ops:
  1.7 9.9 %collective-permute-start.6 = (f32[2,32,512]{2,1,0:T(8,128)S(1)}, f32[2,32,512]{2,1,0:T(8,128)S(1)}, u32[]{:S(2)}, u32[]{:S(2)}) collective-permute-start(f32[2,32,512]{2,1,0:T(8,128)S(1)} %dynamic-slice_select_fusion), channel_id=1, source_target_pairs={{0,1},{1,2},{2,3},{3,4},{4,5},{5,6},{6,7},{8,9},{9,10},{10,11},{11... | collective-permute-start | bytes 393224 | tf_op jit(solution)/shard_map/ppermute | solution.py:144
  4.8 13.8 %collective-permute-start.3 = (f32[2,16,512]{2,1,0:T(8,128)S(1)}, f32[2,16,512]{2,1,0:T(8,128)S(1)}, u32[]{:S(2)}, u32[]{:S(2)}) collective-permute-start(f32[2,16,512]{2,1,0:T(8,128)S(1)} %get-tuple-element.5), channel_id=1, source_target_pairs={{0,8},{8,0},{16,24},{24,16},{1,9},{9,1},{17,25},{25,17},{2,10},{10... | collective-permute-start | bytes 196616 | tf_op jit(solution)/shard_map/ppermute | solution.py:154
  6.5 8.8 %collective-permute-start.2 = (f32[2,16,512]{2,1,0:T(8,128)S(1)}, f32[2,16,512]{2,1,0:T(8,128)S(1)}, u32[]{:S(2)}, u32[]{:S(2)}) collective-permute-start(f32[2,16,512]{2,1,0:T(8,128)S(1)} %get-tuple-element.6), channel_id=1, source_target_pairs={{0,24},{8,16},{16,8},{24,0},{1,25},{9,17},{17,9},{25,1},{2,26},{10... | collective-permute-start | bytes 196616 | tf_op jit(solution)/shard_map/ppermute | solution.py:154
  8.9 7.4 %collective-permute-start.1 = (f32[2,16,512]{2,1,0:T(8,128)S(1)}, f32[2,16,512]{2,1,0:T(8,128)S(1)}, u32[]{:S(2)}, u32[]{:S(2)}) collective-permute-start(f32[2,16,512]{2,1,0:T(8,128)S(1)} %get-tuple-element.7), channel_id=1, source_target_pairs={{0,16},{8,24},{16,0},{24,8},{1,17},{9,25},{17,1},{25,9},{2,18},{10... | collective-permute-start | bytes 196616 | tf_op jit(solution)/shard_map/ppermute | solution.py:154
  9.1 7.3 %collective-permute-start = (f32[2,16,512]{2,1,0:T(8,128)S(1)}, f32[2,16,512]{2,1,0:T(8,128)S(1)}, u32[]{:S(2)}, u32[]{:S(2)}) collective-permute-start(f32[2,16,512]{2,1,0:T(8,128)S(1)} %get-tuple-element.8), channel_id=1, source_target_pairs={{0,8},{8,0},{16,24},{24,16},{1,9},{9,1},{17,25},{25,17},{2,10},{10... | collective-permute-start | bytes 196616 | tf_op jit(solution)/shard_map/ppermute | solution.py:154
  11.5 7.1 %collective-permute-start.5 = (f32[2,16,512]{2,1,0:T(8,128)S(1)}, f32[2,16,512]{2,1,0:T(8,128)S(1)}, u32[]{:S(2)}, u32[]{:S(2)}) collective-permute-start(f32[2,16,512]{2,1,0:T(8,128)S(1)} %get-tuple-element.9), channel_id=1, source_target_pairs={{0,24},{8,16},{16,8},{24,0},{1,25},{9,17},{17,9},{25,1},{2,26},{10... | collective-permute-start | bytes 196616 | tf_op jit(solution)/shard_map/ppermute | solution.py:154
  15.2 6.5 %collective-permute-start.4 = (f32[2,16,512]{2,1,0:T(8,128)S(1)}, f32[2,16,512]{2,1,0:T(8,128)S(1)}, u32[]{:S(2)}, u32[]{:S(2)}) collective-permute-start(f32[2,16,512]{2,1,0:T(8,128)S(1)} %get-tuple-element.10), channel_id=1, source_target_pairs={{0,16},{8,24},{16,0},{24,8},{1,17},{9,25},{17,1},{25,9},{2,18},{10... | collective-permute-start | bytes 196616 | tf_op jit(solution)/shard_map/ppermute | solution.py:154
  16.4 7.9 %collective-permute-start.7 = (f32[3,2,16,512]{3,2,1,0:T(8,128)S(1)}, f32[3,2,16,512]{3,2,1,0:T(8,128)S(1)}, u32[]{:S(2)}, u32[]{:S(2)}) collective-permute-start(f32[3,2,16,512]{3,2,1,0:T(8,128)S(1)} %maximum_add_fusion), channel_id=1, source_target_pairs={{0,1},{1,2},{2,3},{3,4},{4,5},{5,6},{6,7},{8,9},{9,10},{10,11},{11... | collective-permute-start | bytes 589832 | tf_op jit(solution)/shard_map/ppermute | solution.py:156
  21.8 7.9 %collective-permute-start.8 = (f32[3,2,16,512]{3,2,1,0:T(8,128)S(1)}, f32[3,2,16,512]{3,2,1,0:T(8,128)S(1)}, u32[]{:S(2)}, u32[]{:S(2)}) collective-permute-start(f32[3,2,16,512]{3,2,1,0:T(8,128)S(1)} %maximum_add_fusion.1), channel_id=1, source_target_pairs={{0,1},{1,2},{2,3},{3,4},{4,5},{5,6},{6,7},{8,9},{9,10},{10,11},{11... | collective-permute-start | bytes 589832 | tf_op jit(solution)/shard_map/ppermute | solution.py:156

commit v11 on v9

--- a/solution.py
+++ b/solution.py
@@ -46,8 +46,11 @@
     halves = (len(refs) - 3) // 2
     own_refs, left_refs = refs[:halves], refs[halves : 2 * halves]
     cmap_ref, out_ref, shifted_ref = refs[2 * halves :]
-    slabs, layers, half_rows, width = own_refs[0].shape
-    rows = half_rows * halves
+    slabs, layers, _, width = own_refs[0].shape
+    bounds = [0]
+    for ref in own_refs:
+        bounds.append(bounds[-1] + ref.shape[2])
+    rows = bounds[-1]
     layers_overall = layers * slabs
     knot_count = cmap_ref.shape[1]
     first_tile = lax.axis_index("region") == 0
@@ -67,7 +70,8 @@
             shift = ((k * layers + l) * skew) // layers_overall
             for r in range(rows // SUBLANES):
                 band = pl.ds(r * SUBLANES, SUBLANES)
-                c, rest = divmod(r * SUBLANES, half_rows)
+                c = max(i for i in range(halves) if bounds[i] <= r * SUBLANES)
+                rest = r * SUBLANES - bounds[c]
                 part = pl.ds(rest, SUBLANES)
                 left = jnp.where(first_tile, EMPTY, left_refs[c][s, l, part, :])
                 joined = jnp.concatenate([left, own_refs[c][s, l, part, :]], axis=1)
@@ -129,14 +133,16 @@
     regions = lax.axis_size("region")
     share = rows // slabs
     me = lax.axis_index("depth")
-    halves = 2 if share % (2 * SUBLANES) == 0 else 1
-    half = share // halves
-    line = lax.broadcasted_iota(jnp.int32, (1, half, 1), 1)
+    if share % (4 * SUBLANES) == 0:
+        chunks = [share * 3 // 4, share // 4]
+    else:
+        chunks = [share]
     owns, lefts = [], []
-    for c in range(halves):
+    for c, half in enumerate(chunks):
+        line = lax.broadcasted_iota(jnp.int32, (1, half, 1), 1)
         held = []
         for m in range(slabs):
-            start = partner(me, m, slabs, -1) * share + c * half
+            start = partner(me, m, slabs, -1) * share + sum(chunks[:c])
             piece = lax.dynamic_slice_in_dim(thermal_grid, start, half, axis=1)
             piece = jnp.where(start + line < occupied_lines[0, 0], piece, EMPTY)
             if m > 0:
@@ -156,7 +162,7 @@
             pl.BlockSpec(memory_space=smem),
             pl.BlockSpec(memory_space=smem),
         ]
-        + [pl.BlockSpec(memory_space=vmem)] * (2 * halves + 1),
+        + [pl.BlockSpec(memory_space=vmem)] * (2 * len(chunks) + 1),
         out_specs=pl.BlockSpec(memory_space=vmem),
         scratch_shapes=[pltpu.VMEM((layers, slabs, share, width), jnp.float32)],
     )(sheetgroup_viewer_sequence, skew_offsets, *placed, colormap_samples)

time: 33 us -> 37.5 us (1.14)
  waiting for transfers between devices: 10.9 us -> 15.1 us
  other arithmetic: 1.28 us -> 2.13 us
  starting transfers between devices: 13.4 us -> 12.7 us
    ppermute x6, waiting for transfers between devices: 5.6 us -> 11.4 us  [shards(): piece = lax.ppermute(piece, 'depth', route)]
    ppermute x2, waiting for transfers between devices: 5.25 us -> 3.76 us  [shards(): lax.ppermute(own, 'region', [(i, i + 1) for i in range(regions - 1)])]
    another operation x3 -> x4, other arithmetic: 1.24 us -> 2.09 us  [shards(): own = jnp.stack(held, axis=0)]
    ppermute x6, starting transfers between devices: 8.62 us -> 8.01 us  [shards(): piece = lax.ppermute(piece, 'depth', route)]
  transfers between devices with their start and end apart: 8 -> 8, of which waited for: 4 -> 6; matrix products, arithmetic and copies ran while one was open for 0% -> 3% of each run, Pallas kernels for 0% -> 0%
where the time goes in v11:
time: 37.5 us; the launch traced here: 37.2 us
  waiting for transfers between devices  15.1 us (40%)
  starting transfers between devices  12.7 us (34%)
  Pallas kernels  5.88 us (16%)
  other arithmetic  2.13 us (6%)
  between operations  1.39 us (4%)
    ppermute x6, waiting for transfers between devices, shards(): piece = lax.ppermute(piece, 'depth', route)  11.4 us
    ppermute x6, starting transfers between devices, shards(): piece = lax.ppermute(piece, 'depth', route)  8.01 us
    pallas_call x1, Pallas kernels, shards(): pl.pallas_call(render_kernel, out_shape=jax.ShapeDtypeStruct((4, share, w...  5.88 us
    ppermute x2, starting transfers between devices, shards(): lax.ppermute(own, 'region', [(i, i + 1) for i in range(regions - 1)])  4.7 us
    ppermute x2, waiting for transfers between devices, shards(): lax.ppermute(own, 'region', [(i, i + 1) for i in range(regions - 1)])  3.76 us
    another operation x4, other arithmetic, shards(): own = jnp.stack(held, axis=0)  2.09 us
  transfers between devices with their start and end apart: 8, of which 6 were waited for; matrix products, arithmetic and copies ran while one was open for 3% of the time, Pallas kernels for 0%

profile of v11, /device:TPU:4, one launch (start us, length us, event | category | flops | bytes accessed | tf_op | source)
XLA Modules:
  0.0 37.2 jit_solution(16872560492997669280)
XLA Ops:
  0.7 1.2 %select_bitcast_fusion = (f32[1,2,24,512]{3,2,1,0:T(8,128)S(1)}, f32[2,24,512]{2,1,0:T(8,128)S(1)}, f32[2,24,512]{2,1,0:T(8,128)S(1)}, f32[2,24,512]{2,1,0:T(8,128)S(1)}) fusion(f32[2,128,512]{2,1,0:T(8,128)} %param.5, s32[]{:T(128)S(6)} %select_n.50, pred[24]{0:T(512)(128)(4,1)S(1)} %get-tuple-element.18, s32[]{:T(128)S(6)} %select_n.56, ...), kind=kLoop, calls=%fused_computation.5 | loop fusion | flops 98304 | bytes 786544 | tf_op jit(solution)/shard_map/stack | solution.py:152
  1.9 3.7 %collective-permute-start.2 = (f32[2,24,512]{2,1,0:T(8,128)S(1)}, f32[2,24,512]{2,1,0:T(8,128)S(1)}, u32[]{:S(2)}, u32[]{:S(2)}) collective-permute-start(f32[2,24,512]{2,1,0:T(8,128)S(1)} %get-tuple-element.10), channel_id=1, source_target_pairs={{0,24},{8,16},{16,8},{24,0},{1,25},{9,17},{17,9},{25,1},{2,26},{10... | collective-permute-start | bytes 294920 | tf_op jit(solution)/shard_map/ppermute | solution.py:150
  5.5 0.0 collective-permute-start.1
  5.5 0.8 %collective-permute-start = (f32[2,24,512]{2,1,0:T(8,128)S(1)}, f32[2,24,512]{2,1,0:T(8,128)S(1)}, u32[]{:S(2)}, u32[]{:S(2)}) collective-permute-start(f32[2,24,512]{2,1,0:T(8,128)S(1)} %get-tuple-element.12), channel_id=1, source_target_pairs={{0,8},{8,0},{16,24},{24,16},{1,9},{9,1},{17,25},{25,17},{2,10},{10... | collective-permute-start | bytes 294920 | tf_op jit(solution)/shard_map/ppermute | solution.py:150
  6.4 2.9 %collective-permute-done.2 = f32[2,24,512]{2,1,0:T(8,128)S(1)} collective-permute-done((f32[2,24,512]{2,1,0:T(8,128)S(1)}, f32[2,24,512]{2,1,0:T(8,128)S(1)}, u32[]{:S(2)}, u32[]{:S(2)}) %collective-permute-start.2) | collective-permute-done | bytes 98336 | tf_op jit(solution)/shard_map/ppermute | solution.py:150
  9.2 4.6 %collective-permute-done.1 = f32[2,24,512]{2,1,0:T(8,128)S(1)} collective-permute-done((f32[2,24,512]{2,1,0:T(8,128)S(1)}, f32[2,24,512]{2,1,0:T(8,128)S(1)}, u32[]{:S(2)}, u32[]{:S(2)}) %collective-permute-start.1) | collective-permute-done | bytes 98336 | tf_op jit(solution)/shard_map/ppermute | solution.py:150
  13.8 0.0 collective-permute-done
  13.8 1.9 %collective-permute-start.6 = (f32[4,2,24,512]{3,2,1,0:T(8,128)S(1)}, f32[4,2,24,512]{3,2,1,0:T(8,128)S(1)}, u32[]{:S(2)}, u32[]{:S(2)}) collective-permute-start(f32[4,2,24,512]{3,2,1,0:T(8,128)S(1)} %pad_maximum_fusion.refs_0_), channel_id=1, source_target_pairs={{0,1},{1,2},{2,3},{3,4},{4,5},{5,6},{6,7},{8,9},{9,10},{10,11},{11... | collective-permute-start | bytes 1179656 | tf_op jit(solution)/shard_map/ppermute | solution.py:154
  15.8 0.9 %select_bitcast_fusion.1 = (f32[1,2,8,512]{3,2,1,0:T(8,128)S(1)}, f32[2,8,512]{2,1,0:T(8,128)S(1)}, f32[2,8,512]{2,1,0:T(8,128)S(1)}, f32[2,8,512]{2,1,0:T(8,128)S(1)}) fusion(f32[2,128,512]{2,1,0:T(8,128)} %param.5, s32[]{:T(128)S(6)} %select_n.58, pred[8]{0:T(512)(128)(4,1)S(1)} %add_compare_fusion.3, s32[]{:T(128)S(6)} %select_n.60, ...), kind=kLoop, calls=%fused_computation.9 | loop fusion | flops 32768 | bytes 262192 | tf_op jit(solution)/shard_map/stack | solution.py:152
  16.7 0.6 %collective-permute-start.3 = (f32[2,8,512]{2,1,0:T(8,128)S(1)}, f32[2,8,512]{2,1,0:T(8,128)S(1)}, u32[]{:S(2)}, u32[]{:S(2)}) collective-permute-start(f32[2,8,512]{2,1,0:T(8,128)S(1)} %get-tuple-element.6), channel_id=1, source_target_pairs={{0,8},{8,0},{16,24},{24,16},{1,9},{9,1},{17,25},{25,17},{2,10},{10... | collective-permute-start | bytes 98312 | tf_op jit(solution)/shard_map/ppermute | solution.py:150
  17.2 2.1 %collective-permute-start.5 = (f32[2,8,512]{2,1,0:T(8,128)S(1)}, f32[2,8,512]{2,1,0:T(8,128)S(1)}, u32[]{:S(2)}, u32[]{:S(2)}) collective-permute-start(f32[2,8,512]{2,1,0:T(8,128)S(1)} %get-tuple-element.7), channel_id=1, source_target_pairs={{0,24},{8,16},{16,8},{24,0},{1,25},{9,17},{17,9},{25,1},{2,26},{10... | collective-permute-start | bytes 98312 | tf_op jit(solution)/shard_map/ppermute | solution.py:150
  19.3 0.9 %collective-permute-start.4 = (f32[2,8,512]{2,1,0:T(8,128)S(1)}, f32[2,8,512]{2,1,0:T(8,128)S(1)}, u32[]{:S(2)}, u32[]{:S(2)}) collective-permute-start(f32[2,8,512]{2,1,0:T(8,128)S(1)} %get-tuple-element.8), channel_id=1, source_target_pairs={{0,16},{8,24},{16,0},{24,8},{1,17},{9,25},{17,1},{25,9},{2,18},{10... | collective-permute-start | bytes 98312 | tf_op jit(solution)/shard_map/ppermute | solution.py:150
  20.2 0.4 %collective-permute-done.3 = f32[2,8,512]{2,1,0:T(8,128)S(1)} collective-permute-done((f32[2,8,512]{2,1,0:T(8,128)S(1)}, f32[2,8,512]{2,1,0:T(8,128)S(1)}, u32[]{:S(2)}, u32[]{:S(2)}) %collective-permute-start.3) | collective-permute-done | bytes 32800 | tf_op jit(solution)/shard_map/ppermute | solution.py:150
  20.6 2.3 %collective-permute-done.5 = f32[2,8,512]{2,1,0:T(8,128)S(1)} collective-permute-done((f32[2,8,512]{2,1,0:T(8,128)S(1)}, f32[2,8,512]{2,1,0:T(8,128)S(1)}, u32[]{:S(2)}, u32[]{:S(2)}) %collective-permute-start.5) | collective-permute-done | bytes 32800 | tf_op jit(solution)/shard_map/ppermute | solution.py:150
  23.0 1.2 %collective-permute-done.4 = f32[2,8,512]{2,1,0:T(8,128)S(1)} collective-permute-done((f32[2,8,512]{2,1,0:T(8,128)S(1)}, f32[2,8,512]{2,1,0:T(8,128)S(1)}, u32[]{:S(2)}, u32[]{:S(2)}) %collective-permute-start.4) | collective-permute-done | bytes 32800 | tf_op jit(solution)/shard_map/ppermute | solution.py:150
  24.2 2.8 %collective-permute-start.7 = (f32[4,2,8,512]{3,2,1,0:T(8,128)S(1)}, f32[4,2,8,512]{3,2,1,0:T(8,128)S(1)}, u32[]{:S(2)}, u32[]{:S(2)}) collective-permute-start(f32[4,2,8,512]{3,2,1,0:T(8,128)S(1)} %pad_maximum_fusion.1.refs_1_), channel_id=1, source_target_pairs={{0,1},{1,2},{2,3},{3,4},{4,5},{5,6},{6,7},{8,9},{9,10},{10,11},{11... | collective-permute-start | bytes 393224 | tf_op jit(solution)/shard_map/ppermute | solution.py:154
  27.6 3.8 %collective-permute-done.7.refs_3_ = f32[4,2,8,512]{3,2,1,0:T(8,128)S(1)} collective-permute-done((f32[4,2,8,512]{3,2,1,0:T(8,128)S(1)}, f32[4,2,8,512]{3,2,1,0:T(8,128)S(1)}, u32[]{:S(2)}, u32[]{:S(2)}) %collective-permute-start.7) | collective-permute-done | bytes 131104 | tf_op jit(solution)/shard_map/ppermute | solution.py:154
  31.3 0.0 collective-permute-done.6.refs_2_
  31.3 5.9 %shard_map.55 = f32[4,32,512]{2,1,0:T(8,128)} custom-call(s32[4]{0:T(128)} %seq_ref.1, s32[1]{0:T(128)S(6)} %copy.7.skew_ref, f32[4,2,24,512]{3,2,1,0:T(8,128)S(1)} %pad_maximum_fusion.refs_0_, f32[4,2,8,512]{3,2,1,0:T(8,128)S(1)} %pad_maximum_fusion.1.refs_1_, f32[4,2,24,512]{3,2,1,0:T(8,128)S(1)} %collective-permute-done.6.refs_2_, ...), custom_call_target="tpu_custom_call" | custom-call | tf_op jit(solution)/shard_map/pallas_call | solution.py:158
  (7 shorter events, 0.1 us)
Async XLA Ops:
  1.9 7.4 %collective-permute-start.2 = (f32[2,24,512]{2,1,0:T(8,128)S(1)}, f32[2,24,512]{2,1,0:T(8,128)S(1)}, u32[]{:S(2)}, u32[]{:S(2)}) collective-permute-start(f32[2,24,512]{2,1,0:T(8,128)S(1)} %get-tuple-element.10), channel_id=1, source_target_pairs={{0,24},{8,16},{16,8},{24,0},{1,25},{9,17},{17,9},{25,1},{2,26},{10... | collective-permute-start | bytes 294920 | tf_op jit(solution)/shard_map/ppermute | solution.py:150
  5.5 8.3 %collective-permute-start.1 = (f32[2,24,512]{2,1,0:T(8,128)S(1)}, f32[2,24,512]{2,1,0:T(8,128)S(1)}, u32[]{:S(2)}, u32[]{:S(2)}) collective-permute-start(f32[2,24,512]{2,1,0:T(8,128)S(1)} %get-tuple-element.11), channel_id=1, source_target_pairs={{0,16},{8,24},{16,0},{24,8},{1,17},{9,25},{17,1},{25,9},{2,18},{10... | collective-permute-start | bytes 294920 | tf_op jit(solution)/shard_map/ppermute | solution.py:150
  5.5 8.3 %collective-permute-start = (f32[2,24,512]{2,1,0:T(8,128)S(1)}, f32[2,24,512]{2,1,0:T(8,128)S(1)}, u32[]{:S(2)}, u32[]{:S(2)}) collective-permute-start(f32[2,24,512]{2,1,0:T(8,128)S(1)} %get-tuple-element.12), channel_id=1, source_target_pairs={{0,8},{8,0},{16,24},{24,16},{1,9},{9,1},{17,25},{25,17},{2,10},{10... | collective-permute-start | bytes 294920 | tf_op jit(solution)/shard_map/ppermute | solution.py:150
  13.8 17.5 %collective-permute-start.6 = (f32[4,2,24,512]{3,2,1,0:T(8,128)S(1)}, f32[4,2,24,512]{3,2,1,0:T(8,128)S(1)}, u32[]{:S(2)}, u32[]{:S(2)}) collective-permute-start(f32[4,2,24,512]{3,2,1,0:T(8,128)S(1)} %pad_maximum_fusion.refs_0_), channel_id=1, source_target_pairs={{0,1},{1,2},{2,3},{3,4},{4,5},{5,6},{6,7},{8,9},{9,10},{10,11},{11... | collective-permute-start | bytes 1179656 | tf_op jit(solution)/shard_map/ppermute | solution.py:154
  16.7 4.0 %collective-permute-start.3 = (f32[2,8,512]{2,1,0:T(8,128)S(1)}, f32[2,8,512]{2,1,0:T(8,128)S(1)}, u32[]{:S(2)}, u32[]{:S(2)}) collective-permute-start(f32[2,8,512]{2,1,0:T(8,128)S(1)} %get-tuple-element.6), channel_id=1, source_target_pairs={{0,8},{8,0},{16,24},{24,16},{1,9},{9,1},{17,25},{25,17},{2,10},{10... | collective-permute-start | bytes 98312 | tf_op jit(solution)/shard_map/ppermute | solution.py:150
  17.2 5.7 %collective-permute-start.5 = (f32[2,8,512]{2,1,0:T(8,128)S(1)}, f32[2,8,512]{2,1,0:T(8,128)S(1)}, u32[]{:S(2)}, u32[]{:S(2)}) collective-permute-start(f32[2,8,512]{2,1,0:T(8,128)S(1)} %get-tuple-element.7), channel_id=1, source_target_pairs={{0,24},{8,16},{16,8},{24,0},{1,25},{9,17},{17,9},{25,1},{2,26},{10... | collective-permute-start | bytes 98312 | tf_op jit(solution)/shard_map/ppermute | solution.py:150
  19.3 4.8 %collective-permute-start.4 = (f32[2,8,512]{2,1,0:T(8,128)S(1)}, f32[2,8,512]{2,1,0:T(8,128)S(1)}, u32[]{:S(2)}, u32[]{:S(2)}) collective-permute-start(f32[2,8,512]{2,1,0:T(8,128)S(1)} %get-tuple-element.8), channel_id=1, source_target_pairs={{0,16},{8,24},{16,0},{24,8},{1,17},{9,25},{17,1},{25,9},{2,18},{10... | collective-permute-start | bytes 98312 | tf_op jit(solution)/shard_map/ppermute | solution.py:150
  24.2 7.2 %collective-permute-start.7 = (f32[4,2,8,512]{3,2,1,0:T(8,128)S(1)}, f32[4,2,8,512]{3,2,1,0:T(8,128)S(1)}, u32[]{:S(2)}, u32[]{:S(2)}) collective-permute-start(f32[4,2,8,512]{3,2,1,0:T(8,128)S(1)} %pad_maximum_fusion.1.refs_1_), channel_id=1, source_target_pairs={{0,1},{1,2},{2,3},{3,4},{4,5},{5,6},{6,7},{8,9},{9,10},{10,11},{11... | collective-permute-start | bytes 393224 | tf_op jit(solution)/shard_map/ppermute | solution.py:154

commit v12 on v9

--- a/solution.py
+++ b/solution.py
@@ -148,18 +148,19 @@
         lefts.append(lax.ppermute(own, "region", [(i, i + 1) for i in range(regions - 1)]))
     vmem = pltpu.VMEM
     smem = pltpu.SMEM
-    placed = [pltpu.with_memory_space_constraint(x, vmem) for x in owns + lefts]
-    return pl.pallas_call(
-        render_kernel,
-        out_shape=jax.ShapeDtypeStruct((4, share, width), jnp.float32),
-        in_specs=[
-            pl.BlockSpec(memory_space=smem),
-            pl.BlockSpec(memory_space=smem),
-        ]
-        + [pl.BlockSpec(memory_space=vmem)] * (2 * halves + 1),
-        out_specs=pl.BlockSpec(memory_space=vmem),
-        scratch_shapes=[pltpu.VMEM((layers, slabs, share, width), jnp.float32)],
-    )(sheetgroup_viewer_sequence, skew_offsets, *placed, colormap_samples)
+    images = []
+    for own, left in zip(owns, lefts):
+        placed = [pltpu.with_memory_space_constraint(x, vmem) for x in (own, left)]
+        images.append(
+            pl.pallas_call(
+                render_kernel,
+                out_shape=jax.ShapeDtypeStruct((4, half, width), jnp.float32),
+                in_specs=[pl.BlockSpec(memory_space=smem)] * 2 + [pl.BlockSpec(memory_space=vmem)] * 3,
+                out_specs=pl.BlockSpec(memory_space=vmem),
+                scratch_shapes=[pltpu.VMEM((layers, slabs, half, width), jnp.float32)],
+            )(sheetgroup_viewer_sequence, skew_offsets, *placed, colormap_samples)
+        )
+    return jnp.concatenate(images, axis=1) if len(images) > 1 else images[0]
 
 
 def solution(mesh):

time: 33 us -> 33.4 us (1.012)
  waiting for transfers between devices: 10.9 us -> 8.05 us
  other arithmetic: 1.28 us -> 2.9 us
  Pallas kernels: 5.88 us -> 7.37 us
    ppermute x2, waiting for transfers between devices: 5.25 us -> 2.45 us  [shards(): lax.ppermute(own, 'region', [(i, i + 1) for i in range(regions - 1)])]
    concatenate x0 -> x1, other arithmetic: none -> 1.62 us  [shards(): return jnp.concatenate(images, axis=1) if len(images) > 1 else images[0]]
    pallas_call x1 -> x2, Pallas kernels: 5.88 us -> 7.37 us  [shards(): pl.pallas_call(render_kernel, out_shape=jax.ShapeDtypeStruct((4, half, wi...]
  transfers between devices with their start and end apart: 8 -> 8, of which waited for: 4 -> 3; matrix products, arithmetic and copies ran while one was open for 0% -> 0% of each run, Pallas kernels for 0% -> 11%
where the time goes in v12:
time: 33.4 us; the launch traced here: 33.1 us
  starting transfers between devices  13.4 us (40%)
  waiting for transfers between devices  8.05 us (24%)
  Pallas kernels  7.37 us (22%)
  other arithmetic  2.9 us (9%)
  between operations  1.41 us (4%)
    ppermute x6, starting transfers between devices, shards(): piece = lax.ppermute(piece, 'depth', route)  8.62 us
    pallas_call x2, Pallas kernels, shards(): pl.pallas_call(render_kernel, out_shape=jax.ShapeDtypeStruct((4, half, wi...  7.37 us
    ppermute x6, waiting for transfers between devices, shards(): piece = lax.ppermute(piece, 'depth', route)  5.6 us
    ppermute x2, starting transfers between devices, shards(): lax.ppermute(own, 'region', [(i, i + 1) for i in range(regions - 1)])  4.73 us
    ppermute x2, waiting for transfers between devices, shards(): lax.ppermute(own, 'region', [(i, i + 1) for i in range(regions - 1)])  2.45 us
    concatenate x1, other arithmetic, shards(): return jnp.concatenate(images, axis=1) if len(images) > 1 else images[0]  1.62 us
    another operation x3, other arithmetic, shards(): own = jnp.stack(held, axis=0)  1.24 us
  transfers between devices with their start and end apart: 8, of which 3 were waited for; matrix products, arithmetic and copies ran while one was open for 0% of the time, Pallas kernels for 11%

profile of v12, /device:TPU:4, one launch (start us, length us, event | category | flops | bytes accessed | tf_op | source)
XLA Modules:
  0.0 33.1 jit_solution(7745763578646920741)
XLA Ops:
  0.7 1.2 %select_bitcast_fusion.1 = (f32[1,2,16,512]{3,2,1,0:T(8,128)S(1)}, f32[2,16,512]{2,1,0:T(8,128)S(1)}, f32[1,2,16,512]{3,2,1,0:T(8,128)S(1)}, f32[2,16,512]{2,1,0...) fusion(f32[2,128,512]{2,1,0:T(8,128)} %param.5, ...), kind=kLoop, calls=%fused_computation.10 | loop fusion | flops 131072 | bytes 1048736 | tf_op jit(solution)/shard_map/stack | solution.py:146
  2.0 1.6 %collective-permute-start.4 = (f32[2,16,512]{2,1,0:T(8,128)S(1)}, f32[2,16,512]{2,1,0:T(8,128)S(1)}, u32[]{:S(2)}, u32[]{:S(2)}) collective-permute-start(f32[2,16,512]{2,1,0:T(8,128)S(1)} %get-tuple-element.6), channel_id=1, source_target_pairs={{0,8},{8,0},{16,24},{24,16},{1,9},{9,1},{17,25},{25,17},{2,10},{10... | collective-permute-start | bytes 196616 | tf_op jit(solution)/shard_map/ppermute | solution.py:144
  3.6 2.5 %collective-permute-start.6 = (f32[2,16,512]{2,1,0:T(8,128)S(1)}, f32[2,16,512]{2,1,0:T(8,128)S(1)}, u32[]{:S(2)}, u32[]{:S(2)}) collective-permute-start(f32[2,16,512]{2,1,0:T(8,128)S(1)} %get-tuple-element.11), channel_id=1, source_target_pairs={{0,24},{8,16},{16,8},{24,0},{1,25},{9,17},{17,9},{25,1},{2,26},{10... | collective-permute-start | bytes 196616 | tf_op jit(solution)/shard_map/ppermute | solution.py:144
  6.1 0.1 collective-permute-start.5
  6.2 2.9 %collective-permute-start.2 = (f32[2,16,512]{2,1,0:T(8,128)S(1)}, f32[2,16,512]{2,1,0:T(8,128)S(1)}, u32[]{:S(2)}, u32[]{:S(2)}) collective-permute-start(f32[2,16,512]{2,1,0:T(8,128)S(1)} %get-tuple-element.8), channel_id=1, source_target_pairs={{0,24},{8,16},{16,8},{24,0},{1,25},{9,17},{17,9},{25,1},{2,26},{10... | collective-permute-start | bytes 196616 | tf_op jit(solution)/shard_map/ppermute | solution.py:144
  9.1 0.3 %collective-permute-start.1 = (f32[2,16,512]{2,1,0:T(8,128)S(1)}, f32[2,16,512]{2,1,0:T(8,128)S(1)}, u32[]{:S(2)}, u32[]{:S(2)}) collective-permute-start(f32[2,16,512]{2,1,0:T(8,128)S(1)} %get-tuple-element.9), channel_id=1, source_target_pairs={{0,16},{8,24},{16,0},{24,8},{1,17},{9,25},{17,1},{25,9},{2,18},{10... | collective-permute-start | bytes 196616 | tf_op jit(solution)/shard_map/ppermute | solution.py:144
  9.5 0.0 collective-permute-done.4
  9.5 1.1 %collective-permute-start = (f32[2,16,512]{2,1,0:T(8,128)S(1)}, f32[2,16,512]{2,1,0:T(8,128)S(1)}, u32[]{:S(2)}, u32[]{:S(2)}) collective-permute-start(f32[2,16,512]{2,1,0:T(8,128)S(1)} %get-tuple-element.10), channel_id=1, source_target_pairs={{0,8},{8,0},{16,24},{24,16},{1,9},{9,1},{17,25},{25,17},{2,10},{10... | collective-permute-start | bytes 196616 | tf_op jit(solution)/shard_map/ppermute | solution.py:144
  10.6 0.0 collective-permute-done.6
  10.6 4.9 %collective-permute-done.5 = f32[2,16,512]{2,1,0:T(8,128)S(1)} collective-permute-done((f32[2,16,512]{2,1,0:T(8,128)S(1)}, f32[2,16,512]{2,1,0:T(8,128)S(1)}, u32[]{:S(2)}, u32[]{:S(2)}) %collective-permute-start.5) | collective-permute-done | bytes 65568 | tf_op jit(solution)/shard_map/ppermute | solution.py:144
  15.5 1.9 %collective-permute-start.7 = (f32[4,2,16,512]{3,2,1,0:T(8,128)S(1)}, f32[4,2,16,512]{3,2,1,0:T(8,128)S(1)}, u32[]{:S(2)}, u32[]{:S(2)}) collective-permute-start(f32[4,2,16,512]{3,2,1,0:T(8,128)S(1)} %pad_maximum_fusion.1.refs_0_), channel_id=1, source_target_pairs={{0,1},{1,2},{2,3},{3,4},{4,5},{5,6},{6,7},{8,9},{9,10},{10,11},{11... | collective-permute-start | bytes 786440 | tf_op jit(solution)/shard_map/ppermute | solution.py:148
  17.4 0.0 collective-permute-done.2
  17.4 0.7 %collective-permute-done.1 = f32[2,16,512]{2,1,0:T(8,128)S(1)} collective-permute-done((f32[2,16,512]{2,1,0:T(8,128)S(1)}, f32[2,16,512]{2,1,0:T(8,128)S(1)}, u32[]{:S(2)}, u32[]{:S(2)}) %collective-permute-start.1) | collective-permute-done | bytes 65568 | tf_op jit(solution)/shard_map/ppermute | solution.py:144
  18.1 0.0 collective-permute-done
  18.2 2.8 %collective-permute-start.3 = (f32[4,2,16,512]{3,2,1,0:T(8,128)S(1)}, f32[4,2,16,512]{3,2,1,0:T(8,128)S(1)}, u32[]{:S(2)}, u32[]{:S(2)}) collective-permute-start(f32[4,2,16,512]{3,2,1,0:T(8,128)S(1)} %pad_maximum_fusion.refs_0_), channel_id=1, source_target_pairs={{0,1},{1,2},{2,3},{3,4},{4,5},{5,6},{6,7},{8,9},{9,10},{10,11},{11... | collective-permute-start | bytes 786440 | tf_op jit(solution)/shard_map/ppermute | solution.py:148
  21.6 2.4 %collective-permute-done.7.refs_1_ = f32[4,2,16,512]{3,2,1,0:T(8,128)S(1)} collective-permute-done((f32[4,2,16,512]{3,2,1,0:T(8,128)S(1)}, f32[4,2,16,512]{3,2,1,0:T(8,128)S(1)}, u32[]{:S(2)}, u32[]{:S(2)}) %collective-permute-start.7) | collective-permute-done | bytes 262176 | tf_op jit(solution)/shard_map/ppermute | solution.py:148
  24.1 3.6 %shard_map.56 = f32[4,16,512]{2,1,0:T(8,128)} custom-call(s32[4]{0:T(128)} %seq_ref.3, s32[1]{0:T(128)S(6)} %copy.7.skew_ref, f32[4,2,16,512]{3,2,1,0:T(8,128)S(1)} %pad_maximum_fusion.1.refs_0_, f32[4,2,16,512]{3,2,1,0:T(8,128)S(1)} %collective-permute-done.7.refs_1_, f32[4,256]{1,0:T(4,128)} %refs_2_.3), custom_call_target="tpu_custom_call" | custom-call | tf_op jit(solution)/shard_map/pallas_call | solution.py:155
  27.7 0.0 copy-start
  27.7 0.0 collective-permute-done.3.refs_1_
  27.7 3.7 %shard_map.55 = f32[4,16,512]{2,1,0:T(8,128)} custom-call(s32[4]{0:T(128)} %seq_ref.3, s32[1]{0:T(128)S(6)} %copy.7.skew_ref, f32[4,2,16,512]{3,2,1,0:T(8,128)S(1)} %pad_maximum_fusion.refs_0_, f32[4,2,16,512]{3,2,1,0:T(8,128)S(1)} %collective-permute-done.3.refs_1_, f32[4,256]{1,0:T(4,128)} %refs_2_.3), custom_call_target="tpu_custom_call" | custom-call | tf_op jit(solution)/shard_map/pallas_call | solution.py:155
  31.5 0.0 copy-done
  31.5 1.6 %pad_maximum_fusion.2 = f32[4,32,512]{2,1,0:T(8,128)} fusion(f32[4,16,512]{2,1,0:T(8,128)S(1)} %copy-done, f32[4,16,512]{2,1,0:T(8,128)} %shard_map.55), kind=kLoop, calls=%fused_computation.2 | loop fusion | flops 65536 | bytes 524288 | tf_op jit(solution)/shard_map/concatenate | solution.py:163
  (6 shorter events, 0.1 us)
Async XLA Ops:
  2.0 7.5 %collective-permute-start.4 = (f32[2,16,512]{2,1,0:T(8,128)S(1)}, f32[2,16,512]{2,1,0:T(8,128)S(1)}, u32[]{:S(2)}, u32[]{:S(2)}) collective-permute-start(f32[2,16,512]{2,1,0:T(8,128)S(1)} %get-tuple-element.6), channel_id=1, source_target_pairs={{0,8},{8,0},{16,24},{24,16},{1,9},{9,1},{17,25},{25,17},{2,10},{10... | collective-permute-start | bytes 196616 | tf_op jit(solution)/shard_map/ppermute | solution.py:144
  3.6 7.0 %collective-permute-start.6 = (f32[2,16,512]{2,1,0:T(8,128)S(1)}, f32[2,16,512]{2,1,0:T(8,128)S(1)}, u32[]{:S(2)}, u32[]{:S(2)}) collective-permute-start(f32[2,16,512]{2,1,0:T(8,128)S(1)} %get-tuple-element.11), channel_id=1, source_target_pairs={{0,24},{8,16},{16,8},{24,0},{1,25},{9,17},{17,9},{25,1},{2,26},{10... | collective-permute-start | bytes 196616 | tf_op jit(solution)/shard_map/ppermute | solution.py:144
  6.1 9.4 %collective-permute-start.5 = (f32[2,16,512]{2,1,0:T(8,128)S(1)}, f32[2,16,512]{2,1,0:T(8,128)S(1)}, u32[]{:S(2)}, u32[]{:S(2)}) collective-permute-start(f32[2,16,512]{2,1,0:T(8,128)S(1)} %get-tuple-element.12), channel_id=1, source_target_pairs={{0,16},{8,24},{16,0},{24,8},{1,17},{9,25},{17,1},{25,9},{2,18},{10... | collective-permute-start | bytes 196616 | tf_op jit(solution)/shard_map/ppermute | solution.py:144
  6.2 11.2 %collective-permute-start.2 = (f32[2,16,512]{2,1,0:T(8,128)S(1)}, f32[2,16,512]{2,1,0:T(8,128)S(1)}, u32[]{:S(2)}, u32[]{:S(2)}) collective-permute-start(f32[2,16,512]{2,1,0:T(8,128)S(1)} %get-tuple-element.8), channel_id=1, source_target_pairs={{0,24},{8,16},{16,8},{24,0},{1,25},{9,17},{17,9},{25,1},{2,26},{10... | collective-permute-start | bytes 196616 | tf_op jit(solution)/shard_map/ppermute | solution.py:144
  9.1 9.0 %collective-permute-start.1 = (f32[2,16,512]{2,1,0:T(8,128)S(1)}, f32[2,16,512]{2,1,0:T(8,128)S(1)}, u32[]{:S(2)}, u32[]{:S(2)}) collective-permute-start(f32[2,16,512]{2,1,0:T(8,128)S(1)} %get-tuple-element.9), channel_id=1, source_target_pairs={{0,16},{8,24},{16,0},{24,8},{1,17},{9,25},{17,1},{25,9},{2,18},{10... | collective-permute-start | bytes 196616 | tf_op jit(solution)/shard_map/ppermute | solution.py:144
  9.5 8.7 %collective-permute-start = (f32[2,16,512]{2,1,0:T(8,128)S(1)}, f32[2,16,512]{2,1,0:T(8,128)S(1)}, u32[]{:S(2)}, u32[]{:S(2)}) collective-permute-start(f32[2,16,512]{2,1,0:T(8,128)S(1)} %get-tuple-element.10), channel_id=1, source_target_pairs={{0,8},{8,0},{16,24},{24,16},{1,9},{9,1},{17,25},{25,17},{2,10},{10... | collective-permute-start | bytes 196616 | tf_op jit(solution)/shard_map/ppermute | solution.py:144
  15.5 8.6 %collective-permute-start.7 = (f32[4,2,16,512]{3,2,1,0:T(8,128)S(1)}, f32[4,2,16,512]{3,2,1,0:T(8,128)S(1)}, u32[]{:S(2)}, u32[]{:S(2)}) collective-permute-start(f32[4,2,16,512]{3,2,1,0:T(8,128)S(1)} %pad_maximum_fusion.1.refs_0_), channel_id=1, source_target_pairs={{0,1},{1,2},{2,3},{3,4},{4,5},{5,6},{6,7},{8,9},{9,10},{10,11},{11... | collective-permute-start | bytes 786440 | tf_op jit(solution)/shard_map/ppermute | solution.py:148
  18.2 9.6 %collective-permute-start.3 = (f32[4,2,16,512]{3,2,1,0:T(8,128)S(1)}, f32[4,2,16,512]{3,2,1,0:T(8,128)S(1)}, u32[]{:S(2)}, u32[]{:S(2)}) collective-permute-start(f32[4,2,16,512]{3,2,1,0:T(8,128)S(1)} %pad_maximum_fusion.refs_0_), channel_id=1, source_target_pairs={{0,1},{1,2},{2,3},{3,4},{4,5},{5,6},{6,7},{8,9},{9,10},{10,11},{11... | collective-permute-start | bytes 786440 | tf_op jit(solution)/shard_map/ppermute | solution.py:148
  27.7 3.7 %copy-start = (f32[4,16,512]{2,1,0:T(8,128)S(1)}, f32[4,16,512]{2,1,0:T(8,128)}, u32[]{:S(2)}) copy-start(f32[4,16,512]{2,1,0:T(8,128)} %shard_map.56) | copy-start | bytes 393220

commit v13 on v12

--- a/solution.py
+++ b/solution.py
@@ -42,10 +42,10 @@
     return values
 
 
-def render_kernel(seq_ref, skew_ref, *refs):
-    halves = (len(refs) - 3) // 2
-    own_refs, left_refs = refs[:halves], refs[halves : 2 * halves]
-    cmap_ref, out_ref, shifted_ref = refs[2 * halves :]
+def render_kernel(first_row, seq_ref, skew_ref, own_ref, left_ref, cmap_ref, *refs):
+    out_hbm, shifted_ref, out_ref, sem = refs[-4:]
+    halves = 1
+    own_refs, left_refs = (own_ref,), (left_ref,)
     slabs, layers, half_rows, width = own_refs[0].shape
     rows = half_rows * halves
     layers_overall = layers * slabs
@@ -121,6 +121,9 @@
         return carry
 
     lax.fori_loop(0, (rows // SUBLANES) * pieces, block, 0)
+    copy = pltpu.make_async_copy(out_ref, out_hbm.at[:, pl.ds(first_row, rows), :], sem)
+    copy.start()
+    copy.wait()
 
 
 def shards(thermal_grid, colormap_samples, sheetgroup_viewer_sequence, occupied_lines, skew_offsets):
@@ -148,19 +151,25 @@
         lefts.append(lax.ppermute(own, "region", [(i, i + 1) for i in range(regions - 1)]))
     vmem = pltpu.VMEM
     smem = pltpu.SMEM
-    images = []
-    for own, left in zip(owns, lefts):
+    image = None
+    for c, (own, left) in enumerate(zip(owns, lefts)):
         placed = [pltpu.with_memory_space_constraint(x, vmem) for x in (own, left)]
-        images.append(
-            pl.pallas_call(
-                render_kernel,
-                out_shape=jax.ShapeDtypeStruct((4, half, width), jnp.float32),
-                in_specs=[pl.BlockSpec(memory_space=smem)] * 2 + [pl.BlockSpec(memory_space=vmem)] * 3,
-                out_specs=pl.BlockSpec(memory_space=vmem),
-                scratch_shapes=[pltpu.VMEM((layers, slabs, half, width), jnp.float32)],
-            )(sheetgroup_viewer_sequence, skew_offsets, *placed, colormap_samples)
-        )
-    return jnp.concatenate(images, axis=1) if len(images) > 1 else images[0]
+        extra = [] if image is None else [image]
+        image = pl.pallas_call(
+            functools.partial(render_kernel, c * half),
+            out_shape=jax.ShapeDtypeStruct((4, share, width), jnp.float32),
+            in_specs=[pl.BlockSpec(memory_space=smem)] * 2
+            + [pl.BlockSpec(memory_space=vmem)] * 3
+            + [pl.BlockSpec(memory_space=pl.ANY)] * len(extra),
+            out_specs=pl.BlockSpec(memory_space=pl.ANY),
+            scratch_shapes=[
+                pltpu.VMEM((layers, slabs, half, width), jnp.float32),
+                pltpu.VMEM((4, half, width), jnp.float32),
+                pltpu.SemaphoreType.DMA(()),
+            ],
+            input_output_aliases={5: 0} if extra else {},
+        )(sheetgroup_viewer_sequence, skew_offsets, *placed, colormap_samples, *extra)
+    return image
 
 
 def solution(mesh):

time: 33.4 us -> 31.7 us (0.949)
  other arithmetic: 2.9 us -> 1.28 us
    concatenate x1 -> x0, other arithmetic: 1.62 us -> none  [shards(): return jnp.concatenate(images, axis=1) if len(images) > 1 else images[0]]
  transfers between devices with their start and end apart: 8 -> 8, of which waited for: 3 -> 3; matrix products, arithmetic and copies ran while one was open for 0% -> 0% of each run, Pallas kernels for 11% -> 12%
where the time goes in v13:
time: 31.7 us; the launch traced here: 31.4 us
  starting transfers between devices  13.4 us (42%)
  waiting for transfers between devices  8.05 us (25%)
  Pallas kernels  7.29 us (23%)
  between operations  1.42 us (4%)
  other arithmetic  1.28 us (4%)
    ppermute x6, starting transfers between devices, shards(): piece = lax.ppermute(piece, 'depth', route)  8.62 us
    pallas_call x2, Pallas kernels, shards(): pl.pallas_call(functools.partial(render_kernel, c * half), out_shape=jax....  7.29 us
    ppermute x6, waiting for transfers between devices, shards(): piece = lax.ppermute(piece, 'depth', route)  5.6 us
    ppermute x2, starting transfers between devices, shards(): lax.ppermute(own, 'region', [(i, i + 1) for i in range(regions - 1)])  4.73 us
    ppermute x2, waiting for transfers between devices, shards(): lax.ppermute(own, 'region', [(i, i + 1) for i in range(regions - 1)])  2.45 us
    another operation x3, other arithmetic, shards(): own = jnp.stack(held, axis=0)  1.24 us
  transfers between devices with their start and end apart: 8, of which 3 were waited for; matrix products, arithmetic and copies ran while one was open for 0% of the time, Pallas kernels for 12%

profile of v13, /device:TPU:4, one launch (start us, length us, event | category | flops | bytes accessed | tf_op | source)
XLA Modules:
  0.0 31.4 jit_solution(16466187978381209958)
XLA Ops:
  0.7 1.2 %select_bitcast_fusion = (f32[1,2,16,512]{3,2,1,0:T(8,128)S(1)}, f32[2,16,512]{2,1,0:T(8,128)S(1)}, f32[2,16,512]{2,1,0:T(8,128)S(1)}, f32[2,16,512]{2,1,0:T(8,1...) fusion(f32[2,128,512]{2,1,0:T(8,128)} %param.5, ...), kind=kLoop, calls=%fused_computation.5 | loop fusion | flops 131072 | bytes 1048736 | tf_op jit(solution)/shard_map/stack | solution.py:149
  2.0 1.6 %collective-permute-start.4 = (f32[2,16,512]{2,1,0:T(8,128)S(1)}, f32[2,16,512]{2,1,0:T(8,128)S(1)}, u32[]{:S(2)}, u32[]{:S(2)}) collective-permute-start(f32[2,16,512]{2,1,0:T(8,128)S(1)} %get-tuple-element.6), channel_id=1, source_target_pairs={{0,8},{8,0},{16,24},{24,16},{1,9},{9,1},{17,25},{25,17},{2,10},{10... | collective-permute-start | bytes 196616 | tf_op jit(solution)/shard_map/ppermute | solution.py:147
  3.6 2.5 %collective-permute-start.6 = (f32[2,16,512]{2,1,0:T(8,128)S(1)}, f32[2,16,512]{2,1,0:T(8,128)S(1)}, u32[]{:S(2)}, u32[]{:S(2)}) collective-permute-start(f32[2,16,512]{2,1,0:T(8,128)S(1)} %get-tuple-element.11), channel_id=1, source_target_pairs={{0,24},{8,16},{16,8},{24,0},{1,25},{9,17},{17,9},{25,1},{2,26},{10... | collective-permute-start | bytes 196616 | tf_op jit(solution)/shard_map/ppermute | solution.py:147
  6.1 0.1 collective-permute-start.5
  6.2 2.9 %collective-permute-start.2 = (f32[2,16,512]{2,1,0:T(8,128)S(1)}, f32[2,16,512]{2,1,0:T(8,128)S(1)}, u32[]{:S(2)}, u32[]{:S(2)}) collective-permute-start(f32[2,16,512]{2,1,0:T(8,128)S(1)} %get-tuple-element.7), channel_id=1, source_target_pairs={{0,24},{8,16},{16,8},{24,0},{1,25},{9,17},{17,9},{25,1},{2,26},{10... | collective-permute-start | bytes 196616 | tf_op jit(solution)/shard_map/ppermute | solution.py:147
  9.1 0.3 %collective-permute-start.1 = (f32[2,16,512]{2,1,0:T(8,128)S(1)}, f32[2,16,512]{2,1,0:T(8,128)S(1)}, u32[]{:S(2)}, u32[]{:S(2)}) collective-permute-start(f32[2,16,512]{2,1,0:T(8,128)S(1)} %get-tuple-element.8), channel_id=1, source_target_pairs={{0,16},{8,24},{16,0},{24,8},{1,17},{9,25},{17,1},{25,9},{2,18},{10... | collective-permute-start | bytes 196616 | tf_op jit(solution)/shard_map/ppermute | solution.py:147
  9.5 0.0 collective-permute-done.4
  9.5 1.1 %collective-permute-start = (f32[2,16,512]{2,1,0:T(8,128)S(1)}, f32[2,16,512]{2,1,0:T(8,128)S(1)}, u32[]{:S(2)}, u32[]{:S(2)}) collective-permute-start(f32[2,16,512]{2,1,0:T(8,128)S(1)} %get-tuple-element.9), channel_id=1, source_target_pairs={{0,8},{8,0},{16,24},{24,16},{1,9},{9,1},{17,25},{25,17},{2,10},{10... | collective-permute-start | bytes 196616 | tf_op jit(solution)/shard_map/ppermute | solution.py:147
  10.6 0.0 collective-permute-done.6
  10.6 4.9 %collective-permute-done.5 = f32[2,16,512]{2,1,0:T(8,128)S(1)} collective-permute-done((f32[2,16,512]{2,1,0:T(8,128)S(1)}, f32[2,16,512]{2,1,0:T(8,128)S(1)}, u32[]{:S(2)}, u32[]{:S(2)}) %collective-permute-start.5) | collective-permute-done | bytes 65568 | tf_op jit(solution)/shard_map/ppermute | solution.py:147
  15.5 1.9 %collective-permute-start.7 = (f32[4,2,16,512]{3,2,1,0:T(8,128)S(1)}, f32[4,2,16,512]{3,2,1,0:T(8,128)S(1)}, u32[]{:S(2)}, u32[]{:S(2)}) collective-permute-start(f32[4,2,16,512]{3,2,1,0:T(8,128)S(1)} %pad_maximum_fusion.1.own_ref), channel_id=1, source_target_pairs={{0,1},{1,2},{2,3},{3,4},{4,5},{5,6},{6,7},{8,9},{9,10},{10,11},{11... | collective-permute-start | bytes 786440 | tf_op jit(solution)/shard_map/ppermute | solution.py:151
  17.4 0.0 collective-permute-done.2
  17.4 0.7 %collective-permute-done.1 = f32[2,16,512]{2,1,0:T(8,128)S(1)} collective-permute-done((f32[2,16,512]{2,1,0:T(8,128)S(1)}, f32[2,16,512]{2,1,0:T(8,128)S(1)}, u32[]{:S(2)}, u32[]{:S(2)}) %collective-permute-start.1) | collective-permute-done | bytes 65568 | tf_op jit(solution)/shard_map/ppermute | solution.py:147
  18.1 0.0 collective-permute-done
  18.2 2.8 %collective-permute-start.3 = (f32[4,2,16,512]{3,2,1,0:T(8,128)S(1)}, f32[4,2,16,512]{3,2,1,0:T(8,128)S(1)}, u32[]{:S(2)}, u32[]{:S(2)}) collective-permute-start(f32[4,2,16,512]{3,2,1,0:T(8,128)S(1)} %pad_maximum_fusion.own_ref), channel_id=1, source_target_pairs={{0,1},{1,2},{2,3},{3,4},{4,5},{5,6},{6,7},{8,9},{9,10},{10,11},{11... | collective-permute-start | bytes 786440 | tf_op jit(solution)/shard_map/ppermute | solution.py:151
  21.6 2.4 %collective-permute-done.7.left_ref = f32[4,2,16,512]{3,2,1,0:T(8,128)S(1)} collective-permute-done((f32[4,2,16,512]{3,2,1,0:T(8,128)S(1)}, f32[4,2,16,512]{3,2,1,0:T(8,128)S(1)}, u32[]{:S(2)}, u32[]{:S(2)}) %collective-permute-start.7) | collective-permute-done | bytes 262176 | tf_op jit(solution)/shard_map/ppermute | solution.py:151
  24.1 3.6 %shard_map.55.refs_0_ = f32[4,32,512]{2,1,0:T(8,128)} custom-call(s32[4]{0:T(128)} %seq_ref.3, s32[1]{0:T(128)S(6)} %copy.9.skew_ref, f32[4,2,16,512]{3,2,1,0:T(8,128)S(1)} %pad_maximum_fusion.1.own_ref, f32[4,2,16,512]{3,2,1,0:T(8,128)S(1)} %collective-permute-done.7.left_ref, f32[4,256]{1,0:T(4,128)} %cmap_ref.3), custom_call_target="tpu_custom_call" | custom-call | tf_op jit(solution)/shard_map/pallas_call | solution.py:158
  27.7 0.0 collective-permute-done.3.left_ref
  27.7 3.6 %shard_map.56 = f32[4,32,512]{2,1,0:T(8,128)} custom-call(s32[4]{0:T(128)} %seq_ref.3, s32[1]{0:T(128)S(6)} %copy.9.skew_ref, f32[4,2,16,512]{3,2,1,0:T(8,128)S(1)} %pad_maximum_fusion.own_ref, f32[4,2,16,512]{3,2,1,0:T(8,128)S(1)} %collective-permute-done.3.left_ref, f32[4,256]{1,0:T(4,128)} %cmap_ref.3, ...), custom_call_target="tpu_custom_call", output_to_operand_aliasing={{}: (5, {})} | custom-call | tf_op jit(solution)/shard_map/pallas_call | solution.py:158
  (6 shorter events, 0.1 us)
Async XLA Ops:
  2.0 7.5 %collective-permute-start.4 = (f32[2,16,512]{2,1,0:T(8,128)S(1)}, f32[2,16,512]{2,1,0:T(8,128)S(1)}, u32[]{:S(2)}, u32[]{:S(2)}) collective-permute-start(f32[2,16,512]{2,1,0:T(8,128)S(1)} %get-tuple-element.6), channel_id=1, source_target_pairs={{0,8},{8,0},{16,24},{24,16},{1,9},{9,1},{17,25},{25,17},{2,10},{10... | collective-permute-start | bytes 196616 | tf_op jit(solution)/shard_map/ppermute | solution.py:147
  3.6 7.0 %collective-permute-start.6 = (f32[2,16,512]{2,1,0:T(8,128)S(1)}, f32[2,16,512]{2,1,0:T(8,128)S(1)}, u32[]{:S(2)}, u32[]{:S(2)}) collective-permute-start(f32[2,16,512]{2,1,0:T(8,128)S(1)} %get-tuple-element.11), channel_id=1, source_target_pairs={{0,24},{8,16},{16,8},{24,0},{1,25},{9,17},{17,9},{25,1},{2,26},{10... | collective-permute-start | bytes 196616 | tf_op jit(solution)/shard_map/ppermute | solution.py:147
  6.1 9.4 %collective-permute-start.5 = (f32[2,16,512]{2,1,0:T(8,128)S(1)}, f32[2,16,512]{2,1,0:T(8,128)S(1)}, u32[]{:S(2)}, u32[]{:S(2)}) collective-permute-start(f32[2,16,512]{2,1,0:T(8,128)S(1)} %get-tuple-element.12), channel_id=1, source_target_pairs={{0,16},{8,24},{16,0},{24,8},{1,17},{9,25},{17,1},{25,9},{2,18},{10... | collective-permute-start | bytes 196616 | tf_op jit(solution)/shard_map/ppermute | solution.py:147
  6.2 11.2 %collective-permute-start.2 = (f32[2,16,512]{2,1,0:T(8,128)S(1)}, f32[2,16,512]{2,1,0:T(8,128)S(1)}, u32[]{:S(2)}, u32[]{:S(2)}) collective-permute-start(f32[2,16,512]{2,1,0:T(8,128)S(1)} %get-tuple-element.7), channel_id=1, source_target_pairs={{0,24},{8,16},{16,8},{24,0},{1,25},{9,17},{17,9},{25,1},{2,26},{10... | collective-permute-start | bytes 196616 | tf_op jit(solution)/shard_map/ppermute | solution.py:147
  9.1 9.0 %collective-permute-start.1 = (f32[2,16,512]{2,1,0:T(8,128)S(1)}, f32[2,16,512]{2,1,0:T(8,128)S(1)}, u32[]{:S(2)}, u32[]{:S(2)}) collective-permute-start(f32[2,16,512]{2,1,0:T(8,128)S(1)} %get-tuple-element.8), channel_id=1, source_target_pairs={{0,16},{8,24},{16,0},{24,8},{1,17},{9,25},{17,1},{25,9},{2,18},{10... | collective-permute-start | bytes 196616 | tf_op jit(solution)/shard_map/ppermute | solution.py:147
  9.5 8.7 %collective-permute-start = (f32[2,16,512]{2,1,0:T(8,128)S(1)}, f32[2,16,512]{2,1,0:T(8,128)S(1)}, u32[]{:S(2)}, u32[]{:S(2)}) collective-permute-start(f32[2,16,512]{2,1,0:T(8,128)S(1)} %get-tuple-element.9), channel_id=1, source_target_pairs={{0,8},{8,0},{16,24},{24,16},{1,9},{9,1},{17,25},{25,17},{2,10},{10... | collective-permute-start | bytes 196616 | tf_op jit(solution)/shard_map/ppermute | solution.py:147
  15.5 8.6 %collective-permute-start.7 = (f32[4,2,16,512]{3,2,1,0:T(8,128)S(1)}, f32[4,2,16,512]{3,2,1,0:T(8,128)S(1)}, u32[]{:S(2)}, u32[]{:S(2)}) collective-permute-start(f32[4,2,16,512]{3,2,1,0:T(8,128)S(1)} %pad_maximum_fusion.1.own_ref), channel_id=1, source_target_pairs={{0,1},{1,2},{2,3},{3,4},{4,5},{5,6},{6,7},{8,9},{9,10},{10,11},{11... | collective-permute-start | bytes 786440 | tf_op jit(solution)/shard_map/ppermute | solution.py:151
  18.2 9.6 %collective-permute-start.3 = (f32[4,2,16,512]{3,2,1,0:T(8,128)S(1)}, f32[4,2,16,512]{3,2,1,0:T(8,128)S(1)}, u32[]{:S(2)}, u32[]{:S(2)}) collective-permute-start(f32[4,2,16,512]{3,2,1,0:T(8,128)S(1)} %pad_maximum_fusion.own_ref), channel_id=1, source_target_pairs={{0,1},{1,2},{2,3},{3,4},{4,5},{5,6},{6,7},{8,9},{9,10},{10,11},{11... | collective-permute-start | bytes 786440 | tf_op jit(solution)/shard_map/ppermute | solution.py:151

commit v14 on v13

--- a/solution.py
+++ b/solution.py
@@ -12,15 +12,13 @@
 SUBLANES = 8
 
 
-def partner(i, m, n, sign=1):
-    if n & (n - 1) == 0:
-        return i ^ m
-    return (i + sign * m) % n
+def butterfly(n):
+    return n & (n - 1) == 0
 
 
 def slot_of(s, me, n):
-    if n & (n - 1) == 0:
-        return s ^ me
+    if butterfly(n):
+        return s
     return (s - me + n) % n
 
 
@@ -133,30 +131,49 @@
     share = rows // slabs
     me = lax.axis_index("depth")
     halves = 2 if share % (2 * SUBLANES) == 0 else 1
-    half = share // halves
-    line = lax.broadcasted_iota(jnp.int32, (1, half, 1), 1)
+    chunks = [share // halves] * halves
     owns, lefts = [], []
-    for c in range(halves):
-        held = []
-        for m in range(slabs):
-            start = partner(me, m, slabs, -1) * share + c * half
-            piece = lax.dynamic_slice_in_dim(thermal_grid, start, half, axis=1)
-            piece = jnp.where(start + line < occupied_lines[0, 0], piece, EMPTY)
-            if m > 0:
-                route = [(i, partner(i, m, slabs, -1)) for i in range(slabs)]
-                piece = lax.ppermute(piece, "depth", route)
-            held.append(piece)
-        own = jnp.stack(held, axis=0)
+    start = 0
+    for half in chunks:
+        if butterfly(slabs):
+            rows_here = lax.broadcasted_iota(jnp.int32, (1, slabs, half, 1), 1) * share
+            rows_here = rows_here + lax.broadcasted_iota(jnp.int32, (1, slabs, half, 1), 2) + start
+            cut = thermal_grid.reshape(layers, slabs, share, width)[:, :, start : start + half]
+            cut = jnp.where(rows_here < occupied_lines[0, 0], cut, EMPTY)
+            held = jnp.transpose(cut, (1, 0, 2, 3))
+            for b in reversed(range(slabs.bit_length() - 1)):
+                away = 1 - (me >> b) % 2
+                split = held.reshape(slabs >> (b + 1), 2, 1 << b, layers, half, width)
+                sent = lax.dynamic_index_in_dim(split, away, axis=1, keepdims=False)
+                route = [(i, i ^ (1 << b)) for i in range(slabs)]
+                got = lax.ppermute(sent, "depth", route)
+                side = lax.broadcasted_iota(jnp.int32, (1, 2, 1, 1, 1, 1), 1)
+                split = jnp.where(side == away, got[:, None], split)
+                held = split.reshape(slabs, layers, half, width)
+            own = held
+        else:
+            line = lax.broadcasted_iota(jnp.int32, (1, half, 1), 1)
+            pieces = []
+            for m in range(slabs):
+                first = ((me - m) % slabs) * share + start
+                piece = lax.dynamic_slice_in_dim(thermal_grid, first, half, axis=1)
+                piece = jnp.where(first + line < occupied_lines[0, 0], piece, EMPTY)
+                if m > 0:
+                    route = [(i, (i - m) % slabs) for i in range(slabs)]
+                    piece = lax.ppermute(piece, "depth", route)
+                pieces.append(piece)
+            own = jnp.stack(pieces, axis=0)
         owns.append(own)
         lefts.append(lax.ppermute(own, "region", [(i, i + 1) for i in range(regions - 1)]))
+        start += half
     vmem = pltpu.VMEM
     smem = pltpu.SMEM
     image = None
-    for c, (own, left) in enumerate(zip(owns, lefts)):
+    for c, (own, left, half) in enumerate(zip(owns, lefts, chunks)):
         placed = [pltpu.with_memory_space_constraint(x, vmem) for x in (own, left)]
         extra = [] if image is None else [image]
         image = pl.pallas_call(
-            functools.partial(render_kernel, c * half),
+            functools.partial(render_kernel, sum(chunks[:c])),
             out_shape=jax.ShapeDtypeStruct((4, share, width), jnp.float32),
             in_specs=[pl.BlockSpec(memory_space=smem)] * 2
             + [pl.BlockSpec(memory_space=vmem)] * 3

time: 31.7 us -> 41.2 us (1.30)
  the two profiles are of different devices: /device:TPU:4 before, /device:TPU:28 now
where the time goes in v14:
time: 41.2 us; the launch traced here: 41 us
  waiting for transfers between devices  19.8 us (48%)
  starting transfers between devices  10.6 us (26%)
  Pallas kernels  7.28 us (18%)
  between operations  1.4 us (3%)
  local copies, waits for them, and re-layouts  1.37 us (3%)
  other arithmetic  0.57 us (1%)
    ppermute x4, waiting for transfers between devices, shards(): got = lax.ppermute(sent, 'depth', route)  17.3 us
    pallas_call x2, Pallas kernels, shards(): pl.pallas_call(functools.partial(render_kernel, sum(chunks[:c])), out_sha...  7.28 us
    ppermute x2, starting transfers between devices, shards(): lax.ppermute(own, 'region', [(i, i + 1) for i in range(regions - 1)])  5.42 us
    ppermute x4, starting transfers between devices, shards(): got = lax.ppermute(sent, 'depth', route)  5.14 us
    ppermute x2, waiting for transfers between devices, shards(): lax.ppermute(own, 'region', [(i, i + 1) for i in range(regions - 1)])  2.51 us
    slice x1, local copies, waits for them, and re-layouts, shards(): thermal_grid.reshape(layers, slabs, share, width)[:, :, start:start + half]  1.06 us
  transfers between devices with their start and end apart: 6, of which 5 were waited for; matrix products, arithmetic and copies ran while one was open for 1% of the time, Pallas kernels for 9%

profile of v14, /device:TPU:28, one launch (start us, length us, event | category | flops | bytes accessed | tf_op | source)
XLA Modules:
  0.0 41.0 jit_solution(17626041197642478355)
XLA Ops:
  0.0 1.1 %fusion.5 = (f32[2,4,16,512]{3,2,1,0:T(8,128)S(1)}, f32[2,4,16,512]{3,2,1,0:T(8,128)S(1)}) fusion(f32[2,4,32,512]{3,2,1,0:T(8,128)} %bitcast.39), kind=kLoop, calls=%fused_computation.20 | loop fusion | bytes 1048576 | tf_op jit(solution)/shard_map/slice | solution.py:141
  1.7 0.1 fusion.4
  1.8 0.1 copy_select_fusion.1
  1.9 0.4 collective-permute-start
  2.3 0.1 copy_select_fusion
  2.5 2.7 %collective-permute-start.3 = (f32[1,2,2,16,512]{4,3,2,1,0:T(8,128)S(1)}, f32[1,2,2,16,512]{4,3,2,1,0:T(8,128)S(1)}, u32[]{:S(2)}, u32[]{:S(2)}) collective-permute-start(f32[1,2,2,16,512]{4,3,2,1,0:T(8,128)S(1)} %dynamic-slice_bitcast_fusion), channel_id=1, source_target_pairs={{0,16},{8,24},{16,0},{24,8},{1,17},{9,25},{17,1},{25,9},{2,18},{10... | collective-permute-start | bytes 393224 | tf_op jit(solution)/shard_map/ppermute | solution.py:149
  5.1 8.6 %collective-permute-done = f32[1,2,2,16,512]{4,3,2,1,0:T(8,128)S(1)} collective-permute-done((f32[1,2,2,16,512]{4,3,2,1,0:T(8,128)S(1)}, f32[1,2,2,16,512]{4,3,2,1,0:T(8,128)S(1)}, u32[]{:S(2)}, u32[]{:S(2)}) %collective-permute-start) | collective-permute-done | bytes 131104 | tf_op jit(solution)/shard_map/ppermute | solution.py:149
  13.7 2.7 %collective-permute-done.3 = f32[1,2,2,16,512]{4,3,2,1,0:T(8,128)S(1)} collective-permute-done((f32[1,2,2,16,512]{4,3,2,1,0:T(8,128)S(1)}, f32[1,2,2,16,512]{4,3,2,1,0:T(8,128)S(1)}, u32[]{:S(2)}, u32[]{:S(2)}) %collective-permute-start.3) | collective-permute-done | bytes 131104 | tf_op jit(solution)/shard_map/ppermute | solution.py:149
  16.5 0.1 fusion.2
  16.6 0.1 collective-permute-start.4
  16.6 2.0 %collective-permute-start.1 = (f32[2,1,2,16,512]{4,3,2,0,1:T(8,128)S(1)}, f32[2,1,2,16,512]{4,3,2,0,1:T(8,128)S(1)}, u32[]{:S(2)}, u32[]{:S(2)}) collective-permute-start(f32[2,1,2,16,512]{4,3,2,0,1:T(8,128)S(1)} %get-tuple-element.10), channel_id=1, source_target_pairs={{0,8},{8,0},{16,24},{24,16},{1,9},{9,1},{17,25},{25,17},{2,10},{10... | collective-permute-start | bytes 393224 | tf_op jit(solution)/shard_map/ppermute | solution.py:149
  18.7 0.1 broadcast_in_dim.101
  18.7 0.1 broadcast_in_dim.111
  18.8 0.1 broadcast_in_dim.112
  18.9 4.1 %collective-permute-done.4 = f32[2,1,2,16,512]{4,3,2,0,1:T(8,128)S(1)} collective-permute-done((f32[2,1,2,16,512]{4,3,2,0,1:T(8,128)S(1)}, f32[2,1,2,16,512]{4,3,2,0,1:T(8,128)S(1)}, u32[]{:S(2)}, u32[]{:S(2)}) %collective-permute-start.4) | collective-permute-done | bytes 131104 | tf_op jit(solution)/shard_map/ppermute | solution.py:149
  23.0 1.9 %collective-permute-done.1 = f32[2,1,2,16,512]{4,3,2,0,1:T(8,128)S(1)} collective-permute-done((f32[2,1,2,16,512]{4,3,2,0,1:T(8,128)S(1)}, f32[2,1,2,16,512]{4,3,2,0,1:T(8,128)S(1)}, u32[]{:S(2)}, u32[]{:S(2)}) %collective-permute-start.1) | collective-permute-done | bytes 131104 | tf_op jit(solution)/shard_map/ppermute | solution.py:149
  24.8 0.2 fusion
  25.1 1.9 %collective-permute-start.5 = (f32[4,2,16,512]{3,2,1,0:T(8,128)S(1)}, f32[4,2,16,512]{3,2,1,0:T(8,128)S(1)}, u32[]{:S(2)}, u32[]{:S(2)}) collective-permute-start(f32[4,2,16,512]{3,2,1,0:T(8,128)S(1)} %get-tuple-element.7.own_ref), channel_id=1, source_target_pairs={{0,1},{1,2},{2,3},{3,4},{4,5},{5,6},{6,7},{8,9},{9,10},{10,11},{11... | collective-permute-start | bytes 786440 | tf_op jit(solution)/shard_map/ppermute | solution.py:167
  27.0 3.5 %collective-permute-start.2 = (f32[4,2,16,512]{3,2,1,0:T(8,128)S(1)}, f32[4,2,16,512]{3,2,1,0:T(8,128)S(1)}, u32[]{:S(2)}, u32[]{:S(2)}) collective-permute-start(f32[4,2,16,512]{3,2,1,0:T(8,128)S(1)} %get-tuple-element.8.own_ref), channel_id=1, source_target_pairs={{0,1},{1,2},{2,3},{3,4},{4,5},{5,6},{6,7},{8,9},{9,10},{10,11},{11... | collective-permute-start | bytes 786440 | tf_op jit(solution)/shard_map/ppermute | solution.py:167
  31.1 2.5 %collective-permute-done.5.left_ref = f32[4,2,16,512]{3,2,1,0:T(8,128)S(1)} collective-permute-done((f32[4,2,16,512]{3,2,1,0:T(8,128)S(1)}, f32[4,2,16,512]{3,2,1,0:T(8,128)S(1)}, u32[]{:S(2)}, u32[]{:S(2)}) %collective-permute-start.5) | collective-permute-done | bytes 262176 | tf_op jit(solution)/shard_map/ppermute | solution.py:167
  33.7 3.6 %shard_map.55.refs_0_ = f32[4,32,512]{2,1,0:T(8,128)} custom-call(s32[4]{0:T(128)} %seq_ref.3, s32[1]{0:T(128)S(6)} %copy.19.skew_ref, f32[4,2,16,512]{3,2,1,0:T(8,128)S(1)} %get-tuple-element.7.own_ref, f32[4,2,16,512]{3,2,1,0:T(8,128)S(1)} %collective-permute-done.5.left_ref, f32[4,256]{1,0:T(4,128)} %cmap_ref.3), custom_call_target="tpu_custom_call" | custom-call | tf_op jit(solution)/shard_map/pallas_call | solution.py:175
  37.3 0.0 collective-permute-done.2.left_ref
  37.3 3.6 %shard_map.56 = f32[4,32,512]{2,1,0:T(8,128)} custom-call(s32[4]{0:T(128)} %seq_ref.3, s32[1]{0:T(128)S(6)} %copy.19.skew_ref, f32[4,2,16,512]{3,2,1,0:T(8,128)S(1)} %get-tuple-element.8.own_ref, f32[4,2,16,512]{3,2,1,0:T(8,128)S(1)} %collective-permute-done.2.left_ref, f32[4,256]{1,0:T(4,128)} %cmap_ref.3, ...), custom_call_target="tpu_custom_call", output_to_operand_aliasing={{}: (5, {})} | custom-call | tf_op jit(solution)/shard_map/pallas_call | solution.py:175
  (8 shorter events, 0.1 us)
Async XLA Ops:
  1.9 11.8 %collective-permute-start = (f32[1,2,2,16,512]{4,3,2,1,0:T(8,128)S(1)}, f32[1,2,2,16,512]{4,3,2,1,0:T(8,128)S(1)}, u32[]{:S(2)}, u32[]{:S(2)}) collective-permute-start(f32[1,2,2,16,512]{4,3,2,1,0:T(8,128)S(1)} %dynamic-slice_bitcast_fusion.1), channel_id=1, source_target_pairs={{0,16},{8,24},{16,0},{24,8},{1,17},{9,25},{17,1},{25,9},{2,18},{10... | collective-permute-start | bytes 393224 | tf_op jit(solution)/shard_map/ppermute | solution.py:149
  2.5 14.0 %collective-permute-start.3 = (f32[1,2,2,16,512]{4,3,2,1,0:T(8,128)S(1)}, f32[1,2,2,16,512]{4,3,2,1,0:T(8,128)S(1)}, u32[]{:S(2)}, u32[]{:S(2)}) collective-permute-start(f32[1,2,2,16,512]{4,3,2,1,0:T(8,128)S(1)} %dynamic-slice_bitcast_fusion), channel_id=1, source_target_pairs={{0,16},{8,24},{16,0},{24,8},{1,17},{9,25},{17,1},{25,9},{2,18},{10... | collective-permute-start | bytes 393224 | tf_op jit(solution)/shard_map/ppermute | solution.py:149
  16.6 6.4 %collective-permute-start.4 = (f32[2,1,2,16,512]{4,3,2,0,1:T(8,128)S(1)}, f32[2,1,2,16,512]{4,3,2,0,1:T(8,128)S(1)}, u32[]{:S(2)}, u32[]{:S(2)}) collective-permute-start(f32[2,1,2,16,512]{4,3,2,0,1:T(8,128)S(1)} %get-tuple-element.9), channel_id=1, source_target_pairs={{0,8},{8,0},{16,24},{24,16},{1,9},{9,1},{17,25},{25,17},{2,10},{10... | collective-permute-start | bytes 393224 | tf_op jit(solution)/shard_map/ppermute | solution.py:149
  16.6 8.2 %collective-permute-start.1 = (f32[2,1,2,16,512]{4,3,2,0,1:T(8,128)S(1)}, f32[2,1,2,16,512]{4,3,2,0,1:T(8,128)S(1)}, u32[]{:S(2)}, u32[]{:S(2)}) collective-permute-start(f32[2,1,2,16,512]{4,3,2,0,1:T(8,128)S(1)} %get-tuple-element.10), channel_id=1, source_target_pairs={{0,8},{8,0},{16,24},{24,16},{1,9},{9,1},{17,25},{25,17},{2,10},{10... | collective-permute-start | bytes 393224 | tf_op jit(solution)/shard_map/ppermute | solution.py:149
  25.1 8.6 %collective-permute-start.5 = (f32[4,2,16,512]{3,2,1,0:T(8,128)S(1)}, f32[4,2,16,512]{3,2,1,0:T(8,128)S(1)}, u32[]{:S(2)}, u32[]{:S(2)}) collective-permute-start(f32[4,2,16,512]{3,2,1,0:T(8,128)S(1)} %get-tuple-element.7.own_ref), channel_id=1, source_target_pairs={{0,1},{1,2},{2,3},{3,4},{4,5},{5,6},{6,7},{8,9},{9,10},{10,11},{11... | collective-permute-start | bytes 786440 | tf_op jit(solution)/shard_map/ppermute | solution.py:167
  27.0 10.3 %collective-permute-start.2 = (f32[4,2,16,512]{3,2,1,0:T(8,128)S(1)}, f32[4,2,16,512]{3,2,1,0:T(8,128)S(1)}, u32[]{:S(2)}, u32[]{:S(2)}) collective-permute-start(f32[4,2,16,512]{3,2,1,0:T(8,128)S(1)} %get-tuple-element.8.own_ref), channel_id=1, source_target_pairs={{0,1},{1,2},{2,3},{3,4},{4,5},{5,6},{6,7},{8,9},{9,10},{10,11},{11... | collective-permute-start | bytes 786440 | tf_op jit(solution)/shard_map/ppermute | solution.py:167

commit v15 on v13

--- a/solution.py
+++ b/solution.py
@@ -137,10 +137,11 @@
     line = lax.broadcasted_iota(jnp.int32, (1, half, 1), 1)
     owns, lefts = [], []
     for c in range(halves):
+        source = thermal_grid if c == 0 else lax.optimization_barrier(thermal_grid)
         held = []
         for m in range(slabs):
             start = partner(me, m, slabs, -1) * share + c * half
-            piece = lax.dynamic_slice_in_dim(thermal_grid, start, half, axis=1)
+            piece = lax.dynamic_slice_in_dim(source, start, half, axis=1)
             piece = jnp.where(start + line < occupied_lines[0, 0], piece, EMPTY)
             if m > 0:
                 route = [(i, partner(i, m, slabs, -1)) for i in range(slabs)]

time: 31.7 us -> 31.5 us (level)
    another operation x3 -> x4, other arithmetic: 1.24 us -> 1.18 us  [shards(): own = jnp.stack(held, axis=0)]
where the time goes in v15:
time: 31.5 us; the launch traced here: 31.2 us
  starting transfers between devices  13.4 us (43%)
  waiting for transfers between devices  7.83 us (25%)
  Pallas kernels  7.29 us (23%)
  between operations  1.48 us (5%)
  other arithmetic  1.21 us (4%)
    ppermute x6, starting transfers between devices, shards(): piece = lax.ppermute(piece, 'depth', route)  8.69 us
    pallas_call x2, Pallas kernels, shards(): pl.pallas_call(functools.partial(render_kernel, c * half), out_shape=jax....  7.29 us
    ppermute x6, waiting for transfers between devices, shards(): piece = lax.ppermute(piece, 'depth', route)  5.38 us
    ppermute x2, starting transfers between devices, shards(): lax.ppermute(own, 'region', [(i, i + 1) for i in range(regions - 1)])  4.73 us
    ppermute x2, waiting for transfers between devices, shards(): lax.ppermute(own, 'region', [(i, i + 1) for i in range(regions - 1)])  2.45 us
    another operation x4, other arithmetic, shards(): own = jnp.stack(held, axis=0)  1.18 us
  transfers between devices with their start and end apart: 8, of which 3 were waited for; matrix products, arithmetic and copies ran while one was open for 0% of the time, Pallas kernels for 12%

profile of v15, /device:TPU:4, one launch (start us, length us, event | category | flops | bytes accessed | tf_op | source)
XLA Modules:
  0.0 31.2 jit_solution(12781043913553637719)
XLA Ops:
  0.0 0.0 copy-start
  0.8 1.0 %select_bitcast_fusion = (f32[1,2,16,512]{3,2,1,0:T(8,128)S(1)}, f32[2,16,512]{2,1,0:T(8,128)S(1)}, f32[2,16,512]{2,1,0:T(8,128)S(1)}, f32[2,16,512]{2,1,0:T(8,128)S(1)}) fusion(f32[2,128,512]{2,1,0:T(8,128)} %param.5, s32[]{:T(128)S(6)} %select_n.57, pred[16]{0:T(512)(128)(4,1)S(1)} %get-tuple-element.16, s32[]{:T(128)S(6)} %select_n.59, ...), kind=kLoop, calls=%fused_computation.5 | loop fusion | flops 65536 | bytes 524368 | tf_op jit(solution)/shard_map/stack | solution.py:150
  1.8 1.6 %collective-permute-start.4 = (f32[2,16,512]{2,1,0:T(8,128)S(1)}, f32[2,16,512]{2,1,0:T(8,128)S(1)}, u32[]{:S(2)}, u32[]{:S(2)}) collective-permute-start(f32[2,16,512]{2,1,0:T(8,128)S(1)} %get-tuple-element.6), channel_id=1, source_target_pairs={{0,8},{8,0},{16,24},{24,16},{1,9},{9,1},{17,25},{25,17},{2,10},{10... | collective-permute-start | bytes 196616 | tf_op jit(solution)/shard_map/ppermute | solution.py:148
  3.4 2.5 %collective-permute-start.6 = (f32[2,16,512]{2,1,0:T(8,128)S(1)}, f32[2,16,512]{2,1,0:T(8,128)S(1)}, u32[]{:S(2)}, u32[]{:S(2)}) collective-permute-start(f32[2,16,512]{2,1,0:T(8,128)S(1)} %get-tuple-element.7), channel_id=1, source_target_pairs={{0,24},{8,16},{16,8},{24,0},{1,25},{9,17},{17,9},{25,1},{2,26},{10... | collective-permute-start | bytes 196616 | tf_op jit(solution)/shard_map/ppermute | solution.py:148
  5.9 0.1 collective-permute-start.5
  6.1 0.0 copy-done
  6.1 0.1 select_bitcast_fusion.1
  6.2 3.0 %collective-permute-start.2 = (f32[2,16,512]{2,1,0:T(8,128)S(1)}, f32[2,16,512]{2,1,0:T(8,128)S(1)}, u32[]{:S(2)}, u32[]{:S(2)}) collective-permute-start(f32[2,16,512]{2,1,0:T(8,128)S(1)} %get-tuple-element.10), channel_id=1, source_target_pairs={{0,24},{8,16},{16,8},{24,0},{1,25},{9,17},{17,9},{25,1},{2,26},{10... | collective-permute-start | bytes 196616 | tf_op jit(solution)/shard_map/ppermute | solution.py:148
  9.2 0.3 %collective-permute-start.1 = (f32[2,16,512]{2,1,0:T(8,128)S(1)}, f32[2,16,512]{2,1,0:T(8,128)S(1)}, u32[]{:S(2)}, u32[]{:S(2)}) collective-permute-start(f32[2,16,512]{2,1,0:T(8,128)S(1)} %get-tuple-element.11), channel_id=1, source_target_pairs={{0,16},{8,24},{16,0},{24,8},{1,17},{9,25},{17,1},{25,9},{2,18},{10... | collective-permute-start | bytes 196616 | tf_op jit(solution)/shard_map/ppermute | solution.py:148
  9.5 0.0 collective-permute-done.4
  9.5 1.1 %collective-permute-start = (f32[2,16,512]{2,1,0:T(8,128)S(1)}, f32[2,16,512]{2,1,0:T(8,128)S(1)}, u32[]{:S(2)}, u32[]{:S(2)}) collective-permute-start(f32[2,16,512]{2,1,0:T(8,128)S(1)} %get-tuple-element.12), channel_id=1, source_target_pairs={{0,8},{8,0},{16,24},{24,16},{1,9},{9,1},{17,25},{25,17},{2,10},{10... | collective-permute-start | bytes 196616 | tf_op jit(solution)/shard_map/ppermute | solution.py:148
  10.7 0.0 collective-permute-done.6
  10.7 4.7 %collective-permute-done.5 = f32[2,16,512]{2,1,0:T(8,128)S(1)} collective-permute-done((f32[2,16,512]{2,1,0:T(8,128)S(1)}, f32[2,16,512]{2,1,0:T(8,128)S(1)}, u32[]{:S(2)}, u32[]{:S(2)}) %collective-permute-start.5) | collective-permute-done | bytes 65568 | tf_op jit(solution)/shard_map/ppermute | solution.py:148
  15.3 1.9 %collective-permute-start.7 = (f32[4,2,16,512]{3,2,1,0:T(8,128)S(1)}, f32[4,2,16,512]{3,2,1,0:T(8,128)S(1)}, u32[]{:S(2)}, u32[]{:S(2)}) collective-permute-start(f32[4,2,16,512]{3,2,1,0:T(8,128)S(1)} %pad_maximum_fusion.1.own_ref), channel_id=1, source_target_pairs={{0,1},{1,2},{2,3},{3,4},{4,5},{5,6},{6,7},{8,9},{9,10},{10,11},{11... | collective-permute-start | bytes 786440 | tf_op jit(solution)/shard_map/ppermute | solution.py:152
  17.3 0.0 collective-permute-done.2
  17.3 0.7 %collective-permute-done.1 = f32[2,16,512]{2,1,0:T(8,128)S(1)} collective-permute-done((f32[2,16,512]{2,1,0:T(8,128)S(1)}, f32[2,16,512]{2,1,0:T(8,128)S(1)}, u32[]{:S(2)}, u32[]{:S(2)}) %collective-permute-start.1) | collective-permute-done | bytes 65568 | tf_op jit(solution)/shard_map/ppermute | solution.py:148
  18.0 0.0 collective-permute-done
  18.0 2.8 %collective-permute-start.3 = (f32[4,2,16,512]{3,2,1,0:T(8,128)S(1)}, f32[4,2,16,512]{3,2,1,0:T(8,128)S(1)}, u32[]{:S(2)}, u32[]{:S(2)}) collective-permute-start(f32[4,2,16,512]{3,2,1,0:T(8,128)S(1)} %pad_maximum_fusion.own_ref), channel_id=1, source_target_pairs={{0,1},{1,2},{2,3},{3,4},{4,5},{5,6},{6,7},{8,9},{9,10},{10,11},{11... | collective-permute-start | bytes 786440 | tf_op jit(solution)/shard_map/ppermute | solution.py:152
  21.5 2.4 %collective-permute-done.7.left_ref = f32[4,2,16,512]{3,2,1,0:T(8,128)S(1)} collective-permute-done((f32[4,2,16,512]{3,2,1,0:T(8,128)S(1)}, f32[4,2,16,512]{3,2,1,0:T(8,128)S(1)}, u32[]{:S(2)}, u32[]{:S(2)}) %collective-permute-start.7) | collective-permute-done | bytes 262176 | tf_op jit(solution)/shard_map/ppermute | solution.py:152
  23.9 3.6 %shard_map.55.refs_0_ = f32[4,32,512]{2,1,0:T(8,128)} custom-call(s32[4]{0:T(128)} %seq_ref.3, s32[1]{0:T(128)S(6)} %copy.9.skew_ref, f32[4,2,16,512]{3,2,1,0:T(8,128)S(1)} %pad_maximum_fusion.1.own_ref, f32[4,2,16,512]{3,2,1,0:T(8,128)S(1)} %collective-permute-done.7.left_ref, f32[4,256]{1,0:T(4,128)} %cmap_ref.3), custom_call_target="tpu_custom_call" | custom-call | tf_op jit(solution)/shard_map/pallas_call | solution.py:159
  27.6 0.0 collective-permute-done.3.left_ref
  27.6 3.6 %shard_map.56 = f32[4,32,512]{2,1,0:T(8,128)} custom-call(s32[4]{0:T(128)} %seq_ref.3, s32[1]{0:T(128)S(6)} %copy.9.skew_ref, f32[4,2,16,512]{3,2,1,0:T(8,128)S(1)} %pad_maximum_fusion.own_ref, f32[4,2,16,512]{3,2,1,0:T(8,128)S(1)} %collective-permute-done.3.left_ref, f32[4,256]{1,0:T(4,128)} %cmap_ref.3, ...), custom_call_target="tpu_custom_call", output_to_operand_aliasing={{}: (5, {})} | custom-call | tf_op jit(solution)/shard_map/pallas_call | solution.py:159
  (7 shorter events, 0.1 us)
Async XLA Ops:
  0.0 6.1 %copy-start = (f32[2,128,512]{2,1,0:T(8,128)S(1)}, f32[2,128,512]{2,1,0:T(8,128)}, u32[]{:S(2)}) copy-start(f32[2,128,512]{2,1,0:T(8,128)} %param.5) | copy-start | bytes 1572868
  1.8 7.7 %collective-permute-start.4 = (f32[2,16,512]{2,1,0:T(8,128)S(1)}, f32[2,16,512]{2,1,0:T(8,128)S(1)}, u32[]{:S(2)}, u32[]{:S(2)}) collective-permute-start(f32[2,16,512]{2,1,0:T(8,128)S(1)} %get-tuple-element.6), channel_id=1, source_target_pairs={{0,8},{8,0},{16,24},{24,16},{1,9},{9,1},{17,25},{25,17},{2,10},{10... | collective-permute-start | bytes 196616 | tf_op jit(solution)/shard_map/ppermute | solution.py:148
  3.4 7.2 %collective-permute-start.6 = (f32[2,16,512]{2,1,0:T(8,128)S(1)}, f32[2,16,512]{2,1,0:T(8,128)S(1)}, u32[]{:S(2)}, u32[]{:S(2)}) collective-permute-start(f32[2,16,512]{2,1,0:T(8,128)S(1)} %get-tuple-element.7), channel_id=1, source_target_pairs={{0,24},{8,16},{16,8},{24,0},{1,25},{9,17},{17,9},{25,1},{2,26},{10... | collective-permute-start | bytes 196616 | tf_op jit(solution)/shard_map/ppermute | solution.py:148
  5.9 9.4 %collective-permute-start.5 = (f32[2,16,512]{2,1,0:T(8,128)S(1)}, f32[2,16,512]{2,1,0:T(8,128)S(1)}, u32[]{:S(2)}, u32[]{:S(2)}) collective-permute-start(f32[2,16,512]{2,1,0:T(8,128)S(1)} %get-tuple-element.8), channel_id=1, source_target_pairs={{0,16},{8,24},{16,0},{24,8},{1,17},{9,25},{17,1},{25,9},{2,18},{10... | collective-permute-start | bytes 196616 | tf_op jit(solution)/shard_map/ppermute | solution.py:148
  6.2 11.1 %collective-permute-start.2 = (f32[2,16,512]{2,1,0:T(8,128)S(1)}, f32[2,16,512]{2,1,0:T(8,128)S(1)}, u32[]{:S(2)}, u32[]{:S(2)}) collective-permute-start(f32[2,16,512]{2,1,0:T(8,128)S(1)} %get-tuple-element.10), channel_id=1, source_target_pairs={{0,24},{8,16},{16,8},{24,0},{1,25},{9,17},{17,9},{25,1},{2,26},{10... | collective-permute-start | bytes 196616 | tf_op jit(solution)/shard_map/ppermute | solution.py:148
  9.2 8.8 %collective-permute-start.1 = (f32[2,16,512]{2,1,0:T(8,128)S(1)}, f32[2,16,512]{2,1,0:T(8,128)S(1)}, u32[]{:S(2)}, u32[]{:S(2)}) collective-permute-start(f32[2,16,512]{2,1,0:T(8,128)S(1)} %get-tuple-element.11), channel_id=1, source_target_pairs={{0,16},{8,24},{16,0},{24,8},{1,17},{9,25},{17,1},{25,9},{2,18},{10... | collective-permute-start | bytes 196616 | tf_op jit(solution)/shard_map/ppermute | solution.py:148
  9.5 8.5 %collective-permute-start = (f32[2,16,512]{2,1,0:T(8,128)S(1)}, f32[2,16,512]{2,1,0:T(8,128)S(1)}, u32[]{:S(2)}, u32[]{:S(2)}) collective-permute-start(f32[2,16,512]{2,1,0:T(8,128)S(1)} %get-tuple-element.12), channel_id=1, source_target_pairs={{0,8},{8,0},{16,24},{24,16},{1,9},{9,1},{17,25},{25,17},{2,10},{10... | collective-permute-start | bytes 196616 | tf_op jit(solution)/shard_map/ppermute | solution.py:148
  15.3 8.6 %collective-permute-start.7 = (f32[4,2,16,512]{3,2,1,0:T(8,128)S(1)}, f32[4,2,16,512]{3,2,1,0:T(8,128)S(1)}, u32[]{:S(2)}, u32[]{:S(2)}) collective-permute-start(f32[4,2,16,512]{3,2,1,0:T(8,128)S(1)} %pad_maximum_fusion.1.own_ref), channel_id=1, source_target_pairs={{0,1},{1,2},{2,3},{3,4},{4,5},{5,6},{6,7},{8,9},{9,10},{10,11},{11... | collective-permute-start | bytes 786440 | tf_op jit(solution)/shard_map/ppermute | solution.py:152
  18.0 9.6 %collective-permute-start.3 = (f32[4,2,16,512]{3,2,1,0:T(8,128)S(1)}, f32[4,2,16,512]{3,2,1,0:T(8,128)S(1)}, u32[]{:S(2)}, u32[]{:S(2)}) collective-permute-start(f32[4,2,16,512]{3,2,1,0:T(8,128)S(1)} %pad_maximum_fusion.own_ref), channel_id=1, source_target_pairs={{0,1},{1,2},{2,3},{3,4},{4,5},{5,6},{6,7},{8,9},{9,10},{10,11},{11... | collective-permute-start | bytes 786440 | tf_op jit(solution)/shard_map/ppermute | solution.py:152

commit v16 on v15

--- a/solution.py
+++ b/solution.py
@@ -136,6 +136,13 @@
     half = share // halves
     line = lax.broadcasted_iota(jnp.int32, (1, half, 1), 1)
     owns, lefts = [], []
+    near = None
+    if halves > 1:
+        first = partner(me, 1, slabs, -1) * share
+        rows_all = lax.broadcasted_iota(jnp.int32, (1, share, 1), 1)
+        near = lax.dynamic_slice_in_dim(thermal_grid, first, share, axis=1)
+        near = jnp.where(first + rows_all < occupied_lines[0, 0], near, EMPTY)
+        near = lax.ppermute(near, "depth", [(i, partner(i, 1, slabs, -1)) for i in range(slabs)])
     for c in range(halves):
         source = thermal_grid if c == 0 else lax.optimization_barrier(thermal_grid)
         held = []
@@ -143,7 +150,9 @@
             start = partner(me, m, slabs, -1) * share + c * half
             piece = lax.dynamic_slice_in_dim(source, start, half, axis=1)
             piece = jnp.where(start + line < occupied_lines[0, 0], piece, EMPTY)
-            if m > 0:
+            if m == 1 and near is not None:
+                piece = near[:, c * half : (c + 1) * half]
+            elif m > 0:
                 route = [(i, partner(i, m, slabs, -1)) for i in range(slabs)]
                 piece = lax.ppermute(piece, "depth", route)
             held.append(piece)

time: 31.5 us -> 35.2 us (1.12)
  waiting for transfers between devices: 7.83 us -> 10.1 us
  other arithmetic: 1.21 us -> 3.08 us
  starting transfers between devices: 13.4 us -> 13 us
    ppermute x6 -> x4, starting transfers between devices: 8.69 us -> 5.98 us  [shards(): piece = lax.ppermute(piece, 'depth', route)]
    ppermute x6 -> x4, waiting for transfers between devices: 5.38 us -> 7.61 us  [shards(): piece = lax.ppermute(piece, 'depth', route)]
    ppermute x0 -> x1, starting transfers between devices: none -> 1.64 us  [shards(): lax.ppermute(near, 'depth', [(i, partner(i, 1, slabs, -1)) for i in range...]
    select_n x0 -> x1, other arithmetic: none -> 0.99 us  [shards(): near = jnp.where(first + rows_all < occupied_lines[0, 0], near, EMPTY)]
    another operation x4, other arithmetic: 1.18 us -> 2.05 us  [shards(): own = jnp.stack(held, axis=0)]
    ppermute x2, starting transfers between devices: 4.73 us -> 5.42 us  [shards(): lax.ppermute(own, 'region', [(i, i + 1) for i in range(regions - 1)])]
  transfers between devices with their start and end apart: 8 -> 7, of which waited for: 3 -> 3; matrix products, arithmetic and copies ran while one was open for 0% -> 6% of each run, Pallas kernels for 12% -> 10%
where the time goes in v16:
time: 35.2 us; the launch traced here: 34.9 us
  starting transfers between devices  13 us (37%)
  waiting for transfers between devices  10.1 us (29%)
  Pallas kernels  7.29 us (21%)
  other arithmetic  3.08 us (9%)
  between operations  1.41 us (4%)
    ppermute x4, waiting for transfers between devices, shards(): piece = lax.ppermute(piece, 'depth', route)  7.61 us
    pallas_call x2, Pallas kernels, shards(): pl.pallas_call(functools.partial(render_kernel, c * half), out_shape=jax....  7.29 us
    ppermute x4, starting transfers between devices, shards(): piece = lax.ppermute(piece, 'depth', route)  5.98 us
    ppermute x2, starting transfers between devices, shards(): lax.ppermute(own, 'region', [(i, i + 1) for i in range(regions - 1)])  5.42 us
    ppermute x2, waiting for transfers between devices, shards(): lax.ppermute(own, 'region', [(i, i + 1) for i in range(regions - 1)])  2.46 us
    another operation x4, other arithmetic, shards(): own = jnp.stack(held, axis=0)  2.05 us
    ppermute x1, starting transfers between devices, shards(): lax.ppermute(near, 'depth', [(i, partner(i, 1, slabs, -1)) for i in range...  1.64 us
    select_n x1, other arithmetic, shards(): near = jnp.where(first + rows_all < occupied_lines[0, 0], near, EMPTY)  0.99 us
  transfers between devices with their start and end apart: 7, of which 3 were waited for; matrix products, arithmetic and copies ran while one was open for 6% of the time, Pallas kernels for 10%

profile of v16, /device:TPU:4, one launch (start us, length us, event | category | flops | bytes accessed | tf_op | source)
XLA Modules:
  0.0 34.9 jit_solution(11335279541441937090)
XLA Ops:
  0.7 1.0 %dynamic-slice_select_fusion = f32[2,32,512]{2,1,0:T(8,128)S(1)} fusion(f32[2,128,512]{2,1,0:T(8,128)} %param.5, s32[]{:T(128)S(6)} %select_n.46, pred[32]{0:T(512)(128)(4,1)S(1)} %add_compare_fusion.5), kind=kLoop, calls=%fused_computation.2 | loop fusion | flops 32768 | bytes 262180 | tf_op jit(solution)/shard_map/jit(_where)/select_n | solution.py:144
  1.7 1.6 %collective-permute-start = (f32[2,32,512]{2,1,0:T(8,128)S(1)}, f32[2,32,512]{2,1,0:T(8,128)S(1)}, u32[]{:S(2)}, u32[]{:S(2)}) collective-permute-start(f32[2,32,512]{2,1,0:T(8,128)S(1)} %dynamic-slice_select_fusion), channel_id=1, source_target_pairs={{0,8},{8,0},{16,24},{24,16},{1,9},{9,1},{17,25},{25,17},{2,10},{10... | collective-permute-start | bytes 393224 | tf_op jit(solution)/shard_map/ppermute | solution.py:145
  3.3 1.0 %select_bitcast_fusion.1 = (f32[1,2,16,512]{3,2,1,0:T(8,128)S(1)}, f32[2,16,512]{2,1,0:T(8,128)S(1)}, f32[2,16,512]{2,1,0:T(8,128)S(1)}) fusion(f32[2,128,512]{2,1,0:T(8,128)} %param.5, s32[]{:T(128)S(6)} %select_n.44, pred[16]{0:T(512)(128)(4,1)S(1)} %add_compare_fusion.6, s32[]{:T(128)S(6)} %select_n.50, pred[16]{0:T(512)(128)(4,1)S(1)} %get-tuple-element.15, ...), kind=kLoop, calls=%fused_computation.10 | loop fusion | flops 49152 | bytes 393276 | tf_op jit(solution)/shard_map/stack | solution.py:159
  4.3 2.5 %collective-permute-start.2 = (f32[2,16,512]{2,1,0:T(8,128)S(1)}, f32[2,16,512]{2,1,0:T(8,128)S(1)}, u32[]{:S(2)}, u32[]{:S(2)}) collective-permute-start(f32[2,16,512]{2,1,0:T(8,128)S(1)} %get-tuple-element.9), channel_id=1, source_target_pairs={{0,24},{8,16},{16,8},{24,0},{1,25},{9,17},{17,9},{25,1},{2,26},{10... | collective-permute-start | bytes 196616 | tf_op jit(solution)/shard_map/ppermute | solution.py:157
  6.9 0.2 collective-permute-start.1
  7.1 1.0 %select_bitcast_fusion = (f32[1,2,16,512]{3,2,1,0:T(8,128)S(1)}, f32[2,16,512]{2,1,0:T(8,128)S(1)}, f32[2,16,512]{2,1,0:T(8,128)S(1)}) fusion(f32[2,128,512]{2,1,0:T(8,128)} %param.5, s32[]{:T(128)S(6)} %select_n.52, pred[16]{0:T(512)(128)(4,1)S(1)} %add_compare_fusion.2, s32[]{:T(128)S(6)} %select_n.56, pred[16]{0:T(512)(128)(4,1)S(1)} %get-tuple-element.13, ...), kind=kLoop, calls=%fused_computation.7 | loop fusion | flops 49152 | bytes 393276 | tf_op jit(solution)/shard_map/stack | solution.py:159
  8.1 2.9 %collective-permute-start.5 = (f32[2,16,512]{2,1,0:T(8,128)S(1)}, f32[2,16,512]{2,1,0:T(8,128)S(1)}, u32[]{:S(2)}, u32[]{:S(2)}) collective-permute-start(f32[2,16,512]{2,1,0:T(8,128)S(1)} %get-tuple-element.6), channel_id=1, source_target_pairs={{0,24},{8,16},{16,8},{24,0},{1,25},{9,17},{17,9},{25,1},{2,26},{10... | collective-permute-start | bytes 196616 | tf_op jit(solution)/shard_map/ppermute | solution.py:157
  11.0 0.3 collective-permute-start.4
  11.4 0.0 collective-permute-done
  11.4 3.1 %collective-permute-done.5 = f32[2,16,512]{2,1,0:T(8,128)S(1)} collective-permute-done((f32[2,16,512]{2,1,0:T(8,128)S(1)}, f32[2,16,512]{2,1,0:T(8,128)S(1)}, u32[]{:S(2)}, u32[]{:S(2)}) %collective-permute-start.5) | collective-permute-done | bytes 65568 | tf_op jit(solution)/shard_map/ppermute | solution.py:157
  14.5 4.5 %collective-permute-done.4 = f32[2,16,512]{2,1,0:T(8,128)S(1)} collective-permute-done((f32[2,16,512]{2,1,0:T(8,128)S(1)}, f32[2,16,512]{2,1,0:T(8,128)S(1)}, u32[]{:S(2)}, u32[]{:S(2)}) %collective-permute-start.4) | collective-permute-done | bytes 65568 | tf_op jit(solution)/shard_map/ppermute | solution.py:157
  19.0 1.9 %collective-permute-start.6 = (f32[4,2,16,512]{3,2,1,0:T(8,128)S(1)}, f32[4,2,16,512]{3,2,1,0:T(8,128)S(1)}, u32[]{:S(2)}, u32[]{:S(2)}) collective-permute-start(f32[4,2,16,512]{3,2,1,0:T(8,128)S(1)} %pad_maximum_fusion.1.own_ref), channel_id=1, source_target_pairs={{0,1},{1,2},{2,3},{3,4},{4,5},{5,6},{6,7},{8,9},{9,10},{10,11},{11... | collective-permute-start | bytes 786440 | tf_op jit(solution)/shard_map/ppermute | solution.py:161
  20.9 0.0 collective-permute-done.2
  20.9 0.0 collective-permute-done.1
  21.0 3.5 %collective-permute-start.3 = (f32[4,2,16,512]{3,2,1,0:T(8,128)S(1)}, f32[4,2,16,512]{3,2,1,0:T(8,128)S(1)}, u32[]{:S(2)}, u32[]{:S(2)}) collective-permute-start(f32[4,2,16,512]{3,2,1,0:T(8,128)S(1)} %pad_maximum_fusion.own_ref), channel_id=1, source_target_pairs={{0,1},{1,2},{2,3},{3,4},{4,5},{5,6},{6,7},{8,9},{9,10},{10,11},{11... | collective-permute-start | bytes 786440 | tf_op jit(solution)/shard_map/ppermute | solution.py:161
  25.1 2.5 %collective-permute-done.6.left_ref = f32[4,2,16,512]{3,2,1,0:T(8,128)S(1)} collective-permute-done((f32[4,2,16,512]{3,2,1,0:T(8,128)S(1)}, f32[4,2,16,512]{3,2,1,0:T(8,128)S(1)}, u32[]{:S(2)}, u32[]{:S(2)}) %collective-permute-start.6) | collective-permute-done | bytes 262176 | tf_op jit(solution)/shard_map/ppermute | solution.py:161
  27.6 3.6 %shard_map.55.refs_0_ = f32[4,32,512]{2,1,0:T(8,128)} custom-call(s32[4]{0:T(128)} %seq_ref.3, s32[1]{0:T(128)S(6)} %copy.9.skew_ref, f32[4,2,16,512]{3,2,1,0:T(8,128)S(1)} %pad_maximum_fusion.1.own_ref, f32[4,2,16,512]{3,2,1,0:T(8,128)S(1)} %collective-permute-done.6.left_ref, f32[4,256]{1,0:T(4,128)} %cmap_ref.3), custom_call_target="tpu_custom_call" | custom-call | tf_op jit(solution)/shard_map/pallas_call | solution.py:168
  31.2 0.0 collective-permute-done.3.left_ref
  31.3 3.6 %shard_map.56 = f32[4,32,512]{2,1,0:T(8,128)} custom-call(s32[4]{0:T(128)} %seq_ref.3, s32[1]{0:T(128)S(6)} %copy.9.skew_ref, f32[4,2,16,512]{3,2,1,0:T(8,128)S(1)} %pad_maximum_fusion.own_ref, f32[4,2,16,512]{3,2,1,0:T(8,128)S(1)} %collective-permute-done.3.left_ref, f32[4,256]{1,0:T(4,128)} %cmap_ref.3, ...), custom_call_target="tpu_custom_call", output_to_operand_aliasing={{}: (5, {})} | custom-call | tf_op jit(solution)/shard_map/pallas_call | solution.py:168
  (8 shorter events, 0.1 us)
Async XLA Ops:
  1.7 9.7 %collective-permute-start = (f32[2,32,512]{2,1,0:T(8,128)S(1)}, f32[2,32,512]{2,1,0:T(8,128)S(1)}, u32[]{:S(2)}, u32[]{:S(2)}) collective-permute-start(f32[2,32,512]{2,1,0:T(8,128)S(1)} %dynamic-slice_select_fusion), channel_id=1, source_target_pairs={{0,8},{8,0},{16,24},{24,16},{1,9},{9,1},{17,25},{25,17},{2,10},{10... | collective-permute-start | bytes 393224 | tf_op jit(solution)/shard_map/ppermute | solution.py:145
  4.3 16.6 %collective-permute-start.2 = (f32[2,16,512]{2,1,0:T(8,128)S(1)}, f32[2,16,512]{2,1,0:T(8,128)S(1)}, u32[]{:S(2)}, u32[]{:S(2)}) collective-permute-start(f32[2,16,512]{2,1,0:T(8,128)S(1)} %get-tuple-element.9), channel_id=1, source_target_pairs={{0,24},{8,16},{16,8},{24,0},{1,25},{9,17},{17,9},{25,1},{2,26},{10... | collective-permute-start | bytes 196616 | tf_op jit(solution)/shard_map/ppermute | solution.py:157
  6.9 14.1 %collective-permute-start.1 = (f32[2,16,512]{2,1,0:T(8,128)S(1)}, f32[2,16,512]{2,1,0:T(8,128)S(1)}, u32[]{:S(2)}, u32[]{:S(2)}) collective-permute-start(f32[2,16,512]{2,1,0:T(8,128)S(1)} %get-tuple-element.10), channel_id=1, source_target_pairs={{0,16},{8,24},{16,0},{24,8},{1,17},{9,25},{17,1},{25,9},{2,18},{10... | collective-permute-start | bytes 196616 | tf_op jit(solution)/shard_map/ppermute | solution.py:157
  8.1 6.4 %collective-permute-start.5 = (f32[2,16,512]{2,1,0:T(8,128)S(1)}, f32[2,16,512]{2,1,0:T(8,128)S(1)}, u32[]{:S(2)}, u32[]{:S(2)}) collective-permute-start(f32[2,16,512]{2,1,0:T(8,128)S(1)} %get-tuple-element.6), channel_id=1, source_target_pairs={{0,24},{8,16},{16,8},{24,0},{1,25},{9,17},{17,9},{25,1},{2,26},{10... | collective-permute-start | bytes 196616 | tf_op jit(solution)/shard_map/ppermute | solution.py:157
  11.0 8.0 %collective-permute-start.4 = (f32[2,16,512]{2,1,0:T(8,128)S(1)}, f32[2,16,512]{2,1,0:T(8,128)S(1)}, u32[]{:S(2)}, u32[]{:S(2)}) collective-permute-start(f32[2,16,512]{2,1,0:T(8,128)S(1)} %get-tuple-element.7), channel_id=1, source_target_pairs={{0,16},{8,24},{16,0},{24,8},{1,17},{9,25},{17,1},{25,9},{2,18},{10... | collective-permute-start | bytes 196616 | tf_op jit(solution)/shard_map/ppermute | solution.py:157
  19.0 8.6 %collective-permute-start.6 = (f32[4,2,16,512]{3,2,1,0:T(8,128)S(1)}, f32[4,2,16,512]{3,2,1,0:T(8,128)S(1)}, u32[]{:S(2)}, u32[]{:S(2)}) collective-permute-start(f32[4,2,16,512]{3,2,1,0:T(8,128)S(1)} %pad_maximum_fusion.1.own_ref), channel_id=1, source_target_pairs={{0,1},{1,2},{2,3},{3,4},{4,5},{5,6},{6,7},{8,9},{9,10},{10,11},{11... | collective-permute-start | bytes 786440 | tf_op jit(solution)/shard_map/ppermute | solution.py:161
  21.0 10.3 %collective-permute-start.3 = (f32[4,2,16,512]{3,2,1,0:T(8,128)S(1)}, f32[4,2,16,512]{3,2,1,0:T(8,128)S(1)}, u32[]{:S(2)}, u32[]{:S(2)}) collective-permute-start(f32[4,2,16,512]{3,2,1,0:T(8,128)S(1)} %pad_maximum_fusion.own_ref), channel_id=1, source_target_pairs={{0,1},{1,2},{2,3},{3,4},{4,5},{5,6},{6,7},{8,9},{9,10},{10,11},{11... | collective-permute-start | bytes 786440 | tf_op jit(solution)/shard_map/ppermute | solution.py:161

commit v17 on v15

--- a/solution.py
+++ b/solution.py
@@ -22,6 +22,14 @@
     if n & (n - 1) == 0:
         return s ^ me
     return (s - me + n) % n
+
+
+def left_widths(slabs, layers, width):
+    widths = []
+    for k in range(slabs):
+        reach = ((k * layers + layers - 1) * (width - 1)) // (layers * slabs)
+        widths.append(min(width, max(LANES, -(-reach // LANES) * LANES)))
+    return widths
 
 
 def lookup(cells, tables, knot_count):
@@ -47,6 +55,8 @@
     halves = 1
     own_refs, left_refs = (own_ref,), (left_ref,)
     slabs, layers, half_rows, width = own_refs[0].shape
+    widths = left_widths(slabs, layers, width)
+    offsets = [sum(widths[:k]) for k in range(slabs)]
     rows = half_rows * halves
     layers_overall = layers * slabs
     knot_count = cmap_ref.shape[1]
@@ -69,9 +79,11 @@
                 band = pl.ds(r * SUBLANES, SUBLANES)
                 c, rest = divmod(r * SUBLANES, half_rows)
                 part = pl.ds(rest, SUBLANES)
-                left = jnp.where(first_tile, EMPTY, left_refs[c][s, l, part, :])
+                reach = widths[k]
+                left = left_refs[c][l, part, pl.ds(offsets[k], reach)]
+                left = jnp.where(first_tile, EMPTY, left)
                 joined = jnp.concatenate([left, own_refs[c][s, l, part, :]], axis=1)
-                shifted_ref[l, k, band, :] = pltpu.roll(joined, shift, 1)[:, width:]
+                shifted_ref[l, k, band, :] = pltpu.roll(joined, shift, 1)[:, reach:]
 
     cmap = cmap_ref[...]
     following = pltpu.roll(cmap, knot_count - 1, 1)
@@ -135,6 +147,11 @@
     halves = 2 if share % (2 * SUBLANES) == 0 else 1
     half = share // halves
     line = lax.broadcasted_iota(jnp.int32, (1, half, 1), 1)
+    widths = left_widths(slabs, layers, width)
+    ranks = jnp.arange(slabs, dtype=jnp.int32)
+    at_rank = sheetgroup_viewer_sequence[None, :] == ranks[:, None]
+    slab_at_rank = jnp.sum(jnp.where(at_rank, ranks[None, :], 0), axis=1)
+    rank_slots = [slot_of(slab_at_rank[k], me, slabs) for k in range(slabs)]
     owns, lefts = [], []
     for c in range(halves):
         source = thermal_grid if c == 0 else lax.optimization_barrier(thermal_grid)
@@ -149,7 +166,12 @@
             held.append(piece)
         own = jnp.stack(held, axis=0)
         owns.append(own)
-        lefts.append(lax.ppermute(own, "region", [(i, i + 1) for i in range(regions - 1)]))
+        reach = [
+            lax.dynamic_index_in_dim(own, slot, axis=0, keepdims=False)[:, :, width - w :]
+            for slot, w in zip(rank_slots, widths)
+        ]
+        trimmed = jnp.concatenate(reach, axis=2)
+        lefts.append(lax.ppermute(trimmed, "region", [(i, i + 1) for i in range(regions - 1)]))
     vmem = pltpu.VMEM
     smem = pltpu.SMEM
     image = None

time: 31.5 us -> 32.9 us (1.044)
  the two profiles are of different devices: /device:TPU:4 before, /device:TPU:1 now
where the time goes in v17:
time: 32.9 us; the launch traced here: 32.6 us
  starting transfers between devices  19.1 us (58%)
  Pallas kernels  7.26 us (22%)
  between operations  4.08 us (12%)
  other arithmetic  1.36 us (4%)
  local copies, waits for them, and re-layouts  0.75 us (2%)
    ppermute x2, starting transfers between devices, shards(): lax.ppermute(trimmed, 'region', [(i, i + 1) for i in range(regions - 1)])  10.7 us
    ppermute x6, starting transfers between devices, shards(): piece = lax.ppermute(piece, 'depth', route)  8.46 us
    pallas_call x2, Pallas kernels, shards(): pl.pallas_call(functools.partial(render_kernel, c * half), out_shape=jax....  7.26 us
    another operation x4, other arithmetic, shards(): own = jnp.stack(held, axis=0)  1.18 us
  transfers between devices with their start and end apart: 8, of which 0 were waited for; matrix products, arithmetic and copies ran while one was open for 3% of the time, Pallas kernels for 11%

profile of v17, /device:TPU:1, one launch (start us, length us, event | category | flops | bytes accessed | tf_op | source)
XLA Modules:
  0.0 32.6 jit_solution(9134211192168057054)
XLA Ops:
  0.0 0.0 copy-start
  0.8 1.0 %select_bitcast_fusion = (f32[1,2,16,512]{3,2,1,0:T(8,128)S(1)}, f32[2,16,512]{2,1,0:T(8,128)S(1)}, f32[2,16,512]{2,1,0:T(8,128)S(1)}, f32[2,16,512]{2,1,0:T(8,128)S(1)}) fusion(f32[2,128,512]{2,1,0:T(8,128)} %param.5, s32[]{:T(128)S(6)} %select_n.83, pred[16]{0:T(512)(128)(4,1)S(1)} %get-tuple-element.28, s32[]{:T(128)S(6)} %select_n.85, ...), kind=kLoop, calls=%fused_computation.11 | loop fusion | flops 65536 | bytes 524368 | tf_op jit(solution)/shard_map/stack | solution.py:167
  1.8 2.2 %collective-permute-start.4 = (f32[2,16,512]{2,1,0:T(8,128)S(1)}, f32[2,16,512]{2,1,0:T(8,128)S(1)}, u32[]{:S(2)}, u32[]{:S(2)}) collective-permute-start(f32[2,16,512]{2,1,0:T(8,128)S(1)} %get-tuple-element.6), channel_id=1, source_target_pairs={{0,8},{8,0},{16,24},{24,16},{1,9},{9,1},{17,25},{25,17},{2,10},{10... | collective-permute-start | bytes 196616 | tf_op jit(solution)/shard_map/ppermute | solution.py:165
  4.0 2.3 %collective-permute-start.5 = (f32[2,16,512]{2,1,0:T(8,128)S(1)}, f32[2,16,512]{2,1,0:T(8,128)S(1)}, u32[]{:S(2)}, u32[]{:S(2)}) collective-permute-start(f32[2,16,512]{2,1,0:T(8,128)S(1)} %get-tuple-element.8), channel_id=1, source_target_pairs={{0,16},{8,24},{16,0},{24,8},{1,17},{9,25},{17,1},{25,9},{2,18},{10... | collective-permute-start | bytes 196616 | tf_op jit(solution)/shard_map/ppermute | solution.py:165
  6.3 0.0 collective-permute-start.6
  6.4 0.0 copy-done
  6.4 0.1 select_bitcast_fusion.1
  6.5 0.0 copy-start.1
  6.5 0.4 %collective-permute-start = (f32[2,16,512]{2,1,0:T(8,128)S(1)}, f32[2,16,512]{2,1,0:T(8,128)S(1)}, u32[]{:S(2)}, u32[]{:S(2)}) collective-permute-start(f32[2,16,512]{2,1,0:T(8,128)S(1)} %get-tuple-element.12), channel_id=1, source_target_pairs={{0,8},{8,0},{16,24},{24,16},{1,9},{9,1},{17,25},{25,17},{2,10},{10... | collective-permute-start | bytes 196616 | tf_op jit(solution)/shard_map/ppermute | solution.py:165
  6.9 3.2 %collective-permute-start.1 = (f32[2,16,512]{2,1,0:T(8,128)S(1)}, f32[2,16,512]{2,1,0:T(8,128)S(1)}, u32[]{:S(2)}, u32[]{:S(2)}) collective-permute-start(f32[2,16,512]{2,1,0:T(8,128)S(1)} %get-tuple-element.11), channel_id=1, source_target_pairs={{0,16},{8,24},{16,0},{24,8},{1,17},{9,25},{17,1},{25,9},{2,18},{10... | collective-permute-start | bytes 196616 | tf_op jit(solution)/shard_map/ppermute | solution.py:165
  10.1 0.0 copy-done.1
  10.1 0.1 select_reduce_fusion
  10.2 0.7 %fusion = (s32[1]{0:T(128)}, s32[1]{0:T(128)}, s32[1]{0:T(128)}, s32[1]{0:T(128)}) fusion(s32[4]{0:T(128)S(1)} %select_reduce_fusion), kind=kLoop, calls=%fused_computation.30 | loop fusion | bytes 32 | tf_op jit(solution)/shard_map/slice | solution.py:154
  13.3 0.0 collective-permute-done.4
  13.3 0.4 %collective-permute-start.2 = (f32[2,16,512]{2,1,0:T(8,128)S(1)}, f32[2,16,512]{2,1,0:T(8,128)S(1)}, u32[]{:S(2)}, u32[]{:S(2)}) collective-permute-start(f32[2,16,512]{2,1,0:T(8,128)S(1)} %get-tuple-element.10), channel_id=1, source_target_pairs={{0,24},{8,16},{16,8},{24,0},{1,25},{9,17},{17,9},{25,1},{2,26},{10... | collective-permute-start | bytes 196616 | tf_op jit(solution)/shard_map/ppermute | solution.py:165
  13.7 0.0 collective-permute-done.5
  13.7 0.0 collective-permute-done.6
  13.8 5.0 %collective-permute-start.7 = (f32[2,16,1280]{2,1,0:T(8,128)S(1)}, f32[2,16,1280]{2,1,0:T(8,128)S(1)}, u32[]{:S(2)}, u32[]{:S(2)}) collective-permute-start(f32[2,16,1280]{2,1,0:T(8,128)S(1)} %pad_maximum_fusion.3), channel_id=1, source_target_pairs={{0,1},{1,2},{2,3},{3,4},{4,5},{5,6},{6,7},{8,9},{9,10},{10,11},{11... | collective-permute-start | bytes 491528 | tf_op jit(solution)/shard_map/ppermute | solution.py:174
  18.8 0.0 collective-permute-done
  18.9 0.0 collective-permute-done.1
  18.9 0.0 collective-permute-done.2
  19.0 5.7 %collective-permute-start.3 = (f32[2,16,1280]{2,1,0:T(8,128)S(1)}, f32[2,16,1280]{2,1,0:T(8,128)S(1)}, u32[]{:S(2)}, u32[]{:S(2)}) collective-permute-start(f32[2,16,1280]{2,1,0:T(8,128)S(1)} %pad_maximum_fusion.2), channel_id=1, source_target_pairs={{0,1},{1,2},{2,3},{3,4},{4,5},{5,6},{6,7},{8,9},{9,10},{10,11},{11... | collective-permute-start | bytes 491528 | tf_op jit(solution)/shard_map/ppermute | solution.py:174
  25.3 0.0 collective-permute-done.7.left_ref
  25.3 3.6 %shard_map.55.refs_0_ = f32[4,32,512]{2,1,0:T(8,128)} custom-call(s32[4]{0:T(128)} %seq_ref.3, s32[1]{0:T(128)S(6)} %copy.9.skew_ref, f32[4,2,16,512]{3,2,1,0:T(8,128)S(1)} %pad_maximum_fusion.1.own_ref, f32[2,16,1280]{2,1,0:T(8,128)S(1)} %collective-permute-done.7.left_ref, f32[4,256]{1,0:T(4,128)} %cmap_ref.3), custom_call_target="tpu_custom_call" | custom-call | tf_op jit(solution)/shard_map/pallas_call | solution.py:181
  29.0 0.0 collective-permute-done.3.left_ref
  29.0 3.6 %shard_map.56 = f32[4,32,512]{2,1,0:T(8,128)} custom-call(s32[4]{0:T(128)} %seq_ref.3, s32[1]{0:T(128)S(6)} %copy.9.skew_ref, f32[4,2,16,512]{3,2,1,0:T(8,128)S(1)} %pad_maximum_fusion.own_ref, f32[2,16,1280]{2,1,0:T(8,128)S(1)} %collective-permute-done.3.left_ref, f32[4,256]{1,0:T(4,128)} %cmap_ref.3, ...), custom_call_target="tpu_custom_call", output_to_operand_aliasing={{}: (5, {})} | custom-call | tf_op jit(solution)/shard_map/pallas_call | solution.py:181
  (17 shorter events, 0.2 us)
Async XLA Ops:
  0.0 6.4 %copy-start = (f32[2,128,512]{2,1,0:T(8,128)S(1)}, f32[2,128,512]{2,1,0:T(8,128)}, u32[]{:S(2)}) copy-start(f32[2,128,512]{2,1,0:T(8,128)} %param.5) | copy-start | bytes 1572868
  1.8 11.5 %collective-permute-start.4 = (f32[2,16,512]{2,1,0:T(8,128)S(1)}, f32[2,16,512]{2,1,0:T(8,128)S(1)}, u32[]{:S(2)}, u32[]{:S(2)}) collective-permute-start(f32[2,16,512]{2,1,0:T(8,128)S(1)} %get-tuple-element.6), channel_id=1, source_target_pairs={{0,8},{8,0},{16,24},{24,16},{1,9},{9,1},{17,25},{25,17},{2,10},{10... | collective-permute-start | bytes 196616 | tf_op jit(solution)/shard_map/ppermute | solution.py:165
  4.0 9.7 %collective-permute-start.5 = (f32[2,16,512]{2,1,0:T(8,128)S(1)}, f32[2,16,512]{2,1,0:T(8,128)S(1)}, u32[]{:S(2)}, u32[]{:S(2)}) collective-permute-start(f32[2,16,512]{2,1,0:T(8,128)S(1)} %get-tuple-element.8), channel_id=1, source_target_pairs={{0,16},{8,24},{16,0},{24,8},{1,17},{9,25},{17,1},{25,9},{2,18},{10... | collective-permute-start | bytes 196616 | tf_op jit(solution)/shard_map/ppermute | solution.py:165
  6.3 7.4 %collective-permute-start.6 = (f32[2,16,512]{2,1,0:T(8,128)S(1)}, f32[2,16,512]{2,1,0:T(8,128)S(1)}, u32[]{:S(2)}, u32[]{:S(2)}) collective-permute-start(f32[2,16,512]{2,1,0:T(8,128)S(1)} %get-tuple-element.7), channel_id=1, source_target_pairs={{0,24},{8,16},{16,8},{24,0},{1,25},{9,17},{17,9},{25,1},{2,26},{10... | collective-permute-start | bytes 196616 | tf_op jit(solution)/shard_map/ppermute | solution.py:165
  6.5 3.6 %copy-start.1 = (s32[4]{0:T(128)S(1)}, s32[4]{0:T(128)}, u32[]{:S(2)}) copy-start(s32[4]{0:T(128)} %seq_ref.3) | copy-start | bytes 52
  6.5 12.4 %collective-permute-start = (f32[2,16,512]{2,1,0:T(8,128)S(1)}, f32[2,16,512]{2,1,0:T(8,128)S(1)}, u32[]{:S(2)}, u32[]{:S(2)}) collective-permute-start(f32[2,16,512]{2,1,0:T(8,128)S(1)} %get-tuple-element.12), channel_id=1, source_target_pairs={{0,8},{8,0},{16,24},{24,16},{1,9},{9,1},{17,25},{25,17},{2,10},{10... | collective-permute-start | bytes 196616 | tf_op jit(solution)/shard_map/ppermute | solution.py:165
  6.9 12.0 %collective-permute-start.1 = (f32[2,16,512]{2,1,0:T(8,128)S(1)}, f32[2,16,512]{2,1,0:T(8,128)S(1)}, u32[]{:S(2)}, u32[]{:S(2)}) collective-permute-start(f32[2,16,512]{2,1,0:T(8,128)S(1)} %get-tuple-element.11), channel_id=1, source_target_pairs={{0,16},{8,24},{16,0},{24,8},{1,17},{9,25},{17,1},{25,9},{2,18},{10... | collective-permute-start | bytes 196616 | tf_op jit(solution)/shard_map/ppermute | solution.py:165
  13.3 5.5 %collective-permute-start.2 = (f32[2,16,512]{2,1,0:T(8,128)S(1)}, f32[2,16,512]{2,1,0:T(8,128)S(1)}, u32[]{:S(2)}, u32[]{:S(2)}) collective-permute-start(f32[2,16,512]{2,1,0:T(8,128)S(1)} %get-tuple-element.10), channel_id=1, source_target_pairs={{0,24},{8,16},{16,8},{24,0},{1,25},{9,17},{17,9},{25,1},{2,26},{10... | collective-permute-start | bytes 196616 | tf_op jit(solution)/shard_map/ppermute | solution.py:165
  13.8 11.5 %collective-permute-start.7 = (f32[2,16,1280]{2,1,0:T(8,128)S(1)}, f32[2,16,1280]{2,1,0:T(8,128)S(1)}, u32[]{:S(2)}, u32[]{:S(2)}) collective-permute-start(f32[2,16,1280]{2,1,0:T(8,128)S(1)} %pad_maximum_fusion.3), channel_id=1, source_target_pairs={{0,1},{1,2},{2,3},{3,4},{4,5},{5,6},{6,7},{8,9},{9,10},{10,11},{11... | collective-permute-start | bytes 491528 | tf_op jit(solution)/shard_map/ppermute | solution.py:174
  19.0 10.0 %collective-permute-start.3 = (f32[2,16,1280]{2,1,0:T(8,128)S(1)}, f32[2,16,1280]{2,1,0:T(8,128)S(1)}, u32[]{:S(2)}, u32[]{:S(2)}) collective-permute-start(f32[2,16,1280]{2,1,0:T(8,128)S(1)} %pad_maximum_fusion.2), channel_id=1, source_target_pairs={{0,1},{1,2},{2,3},{3,4},{4,5},{5,6},{6,7},{8,9},{9,10},{10,11},{11... | collective-permute-start | bytes 491528 | tf_op jit(solution)/shard_map/ppermute | solution.py:174

commit v18 on v15

--- a/solution.py
+++ b/solution.py
@@ -42,37 +42,8 @@
     return values
 
 
-def render_kernel(first_row, seq_ref, skew_ref, own_ref, left_ref, cmap_ref, *refs):
-    out_hbm, shifted_ref, out_ref, sem = refs[-4:]
-    halves = 1
-    own_refs, left_refs = (own_ref,), (left_ref,)
-    slabs, layers, half_rows, width = own_refs[0].shape
-    rows = half_rows * halves
-    layers_overall = layers * slabs
+def tables_of(cmap_ref):
     knot_count = cmap_ref.shape[1]
-    first_tile = lax.axis_index("region") == 0
-    me = lax.axis_index("depth")
-    skew = skew_ref[0]
-
-    order = []
-    for k in range(slabs):
-        s = jnp.int32(0)
-        for j in range(slabs):
-            s = s + jnp.where(seq_ref[j] == k, j, 0)
-        order.append(slot_of(s, me, slabs))
-
-    for k in range(slabs):
-        s = order[k]
-        for l in range(layers):
-            shift = ((k * layers + l) * skew) // layers_overall
-            for r in range(rows // SUBLANES):
-                band = pl.ds(r * SUBLANES, SUBLANES)
-                c, rest = divmod(r * SUBLANES, half_rows)
-                part = pl.ds(rest, SUBLANES)
-                left = jnp.where(first_tile, EMPTY, left_refs[c][s, l, part, :])
-                joined = jnp.concatenate([left, own_refs[c][s, l, part, :]], axis=1)
-                shifted_ref[l, k, band, :] = pltpu.roll(joined, shift, 1)[:, width:]
-
     cmap = cmap_ref[...]
     following = pltpu.roll(cmap, knot_count - 1, 1)
     delta = following - cmap
@@ -82,28 +53,97 @@
             for h in range(knot_count // LANES):
                 row = src[c : c + 1, h * LANES : (h + 1) * LANES]
                 tables.append(jnp.broadcast_to(row, (SUBLANES, LANES)))
-
+    return tables
+
+
+def slots_by_rank(seq_ref, slabs):
+    me = lax.axis_index("depth")
+    order = []
+    for k in range(slabs):
+        s = jnp.int32(0)
+        for j in range(slabs):
+            s = s + jnp.where(seq_ref[j] == k, j, 0)
+        order.append(slot_of(s, me, slabs))
+    return order
+
+
+def cell_terms(cells, tables, knot_count, layers_overall):
+    values = lookup(cells, tables, knot_count)
+    absorb = jnp.where(cells < 100.0, values[3] * (6.0 / layers_overall), 0.0)
+    opacity = 1.0 - jnp.exp(-absorb)
+    return [absorb] + [values[c] * opacity for c in range(3)]
+
+
+def own_kernel(seq_ref, skew_ref, own_ref, cmap_ref, terms_ref, shifted_ref):
+    slabs, layers, rows, width = own_ref.shape
+    layers_overall = layers * slabs
+    knot_count = cmap_ref.shape[1]
+    skew = skew_ref[0]
+    order = slots_by_rank(seq_ref, slabs)
+    for k in range(slabs):
+        for l in range(layers):
+            shift = ((k * layers + l) * skew) // layers_overall
+            for r in range(rows // SUBLANES):
+                band = pl.ds(r * SUBLANES, SUBLANES)
+                shifted_ref[l, k, band, :] = pltpu.roll(own_ref[order[k], l, band, :], shift, 1)
+    tables = tables_of(cmap_ref)
     pieces = width // LANES
 
     def block(i, carry):
-        r = i // pieces
+        band = pl.ds(pl.multiple_of((i // pieces) * SUBLANES, SUBLANES), SUBLANES)
+        cols = pl.ds(pl.multiple_of((i % pieces) * LANES, LANES), LANES)
+        for k in range(slabs):
+            for l in range(layers):
+                terms = cell_terms(shifted_ref[l, k, band, cols], tables, knot_count, layers_overall)
+                for t in range(4):
+                    terms_ref[k * layers + l, t, band, cols] = terms[t]
+        return carry
+
+    lax.fori_loop(0, (rows // SUBLANES) * pieces, block, 0)
+
+
+def render_kernel(first_row, seq_ref, skew_ref, own_ref, left_ref, cmap_ref, terms_ref, *refs):
+    out_hbm, shifted_ref, out_ref, sem = refs[-4:]
+    slabs, layers, rows, width = own_ref.shape
+    layers_overall = layers * slabs
+    knot_count = cmap_ref.shape[1]
+    first_tile = lax.axis_index("region") == 0
+    skew = skew_ref[0]
+    order = slots_by_rank(seq_ref, slabs)
+    shifts = {}
+
+    for k in range(slabs):
+        s = order[k]
+        for l in range(layers):
+            shift = ((k * layers + l) * skew) // layers_overall
+            shifts[k, l] = shift
+            for r in range(rows // SUBLANES):
+                band = pl.ds(r * SUBLANES, SUBLANES)
+                left = jnp.where(first_tile, EMPTY, left_ref[s, l, band, :])
+                joined = jnp.concatenate([left, own_ref[s, l, band, :]], axis=1)
+                shifted_ref[l, k, band, :] = pltpu.roll(joined, shift, 1)[:, width:]
+
+    tables = tables_of(cmap_ref)
+    pieces = width // LANES
+
+    def block(i, carry):
         j = i % pieces
-        band = pl.ds(pl.multiple_of(r * SUBLANES, SUBLANES), SUBLANES)
+        band = pl.ds(pl.multiple_of((i // pieces) * SUBLANES, SUBLANES), SUBLANES)
         cols = pl.ds(pl.multiple_of(j * LANES, LANES), LANES)
-        depth_sum = jnp.zeros((SUBLANES, LANES), jnp.float32)
-        image = [jnp.zeros((SUBLANES, LANES), jnp.float32) for _ in range(3)]
+        depth_sum = None
+        image = None
         for k in range(slabs):
             tau = None
             color = None
             for l in range(layers):
-                cells = shifted_ref[l, k, band, cols]
-                values = lookup(cells, tables, knot_count)
-                absorb = jnp.where(cells < 100.0, values[3] * (6.0 / layers_overall), 0.0)
-                through = jnp.exp(-absorb)
-                opacity = 1.0 - through
-                emit = [values[c] * opacity for c in range(3)]
+                terms = lax.cond(
+                    j * LANES < shifts[k, l],
+                    lambda: tuple(cell_terms(shifted_ref[l, k, band, cols], tables, knot_count, layers_overall)),
+                    lambda: tuple(terms_ref[k * layers + l, t, band, cols] for t in range(4)),
+                )
+                absorb, emit = terms[0], terms[1:]
                 if tau is None:
-                    color = emit
+                    color = list(emit)
                     tau = absorb
                 else:
                     fade = jnp.exp(-tau)
@@ -111,10 +151,11 @@
                     tau = tau + absorb
             if k == 0:
                 image = color
+                depth_sum = tau
             else:
                 fade = jnp.exp(-depth_sum)
                 image = [image[c] + fade * color[c] for c in range(3)]
-            depth_sum = depth_sum + tau
+                depth_sum = depth_sum + tau
         for c in range(3):
             out_ref[c, band, cols] = image[c]
         out_ref[3, band, cols] = 1.0 - jnp.exp(-depth_sum)
@@ -154,13 +195,22 @@
     smem = pltpu.SMEM
     image = None
     for c, (own, left) in enumerate(zip(owns, lefts)):
+        own_placed = pltpu.with_memory_space_constraint(own, vmem)
+        terms = pl.pallas_call(
+            own_kernel,
+            out_shape=jax.ShapeDtypeStruct((slabs * layers, 4, half, width), jnp.float32),
+            in_specs=[pl.BlockSpec(memory_space=smem)] * 2 + [pl.BlockSpec(memory_space=vmem)] * 2,
+            out_specs=pl.BlockSpec(memory_space=vmem),
+            scratch_shapes=[pltpu.VMEM((layers, slabs, half, width), jnp.float32)],
+        )(sheetgroup_viewer_sequence, skew_offsets, own_placed, colormap_samples)
         placed = [pltpu.with_memory_space_constraint(x, vmem) for x in (own, left)]
+        terms = pltpu.with_memory_space_constraint(terms, vmem)
         extra = [] if image is None else [image]
         image = pl.pallas_call(
             functools.partial(render_kernel, c * half),
             out_shape=jax.ShapeDtypeStruct((4, share, width), jnp.float32),
             in_specs=[pl.BlockSpec(memory_space=smem)] * 2
-            + [pl.BlockSpec(memory_space=vmem)] * 3
+            + [pl.BlockSpec(memory_space=vmem)] * 4
             + [pl.BlockSpec(memory_space=pl.ANY)] * len(extra),
             out_specs=pl.BlockSpec(memory_space=pl.ANY),
             scratch_shapes=[
@@ -168,8 +218,8 @@
                 pltpu.VMEM((4, half, width), jnp.float32),
                 pltpu.SemaphoreType.DMA(()),
             ],
-            input_output_aliases={5: 0} if extra else {},
-        )(sheetgroup_viewer_sequence, skew_offsets, *placed, colormap_samples, *extra)
+            input_output_aliases={6: 0} if extra else {},
+        )(sheetgroup_viewer_sequence, skew_offsets, *placed, colormap_samples, terms, *extra)
     return image
 
 

time: 31.5 us -> 40.6 us (1.29)
  the two profiles are of different devices: /device:TPU:4 before, /device:TPU:1 now
where the time goes in v18:
time: 40.6 us; the launch traced here: 40.1 us
  starting transfers between devices  18.2 us (45%)
  Pallas kernels  17.9 us (44%)
  between operations  1.52 us (4%)
  waiting for transfers between devices  1.32 us (3%)
  other arithmetic  1.22 us (3%)
    ppermute x2, starting transfers between devices, shards(): lax.ppermute(own, 'region', [(i, i + 1) for i in range(regions - 1)])  10.1 us
    pallas_call x2, Pallas kernels, shards(): pl.pallas_call(functools.partial(render_kernel, c * half), out_shape=jax....  10.1 us
    ppermute x6, starting transfers between devices, shards(): piece = lax.ppermute(piece, 'depth', route)  8.12 us
    pallas_call x2, Pallas kernels, shards(): pl.pallas_call(own_kernel, out_shape=jax.ShapeDtypeStruct((slabs * layers...  7.78 us
    ppermute x6, waiting for transfers between devices, shards(): piece = lax.ppermute(piece, 'depth', route)  1.31 us
    another operation x4, other arithmetic, shards(): own = jnp.stack(held, axis=0)  1.18 us
  transfers between devices with their start and end apart: 8, of which 1 were waited for; matrix products, arithmetic and copies ran while one was open for 0% of the time, Pallas kernels for 32%

profile of v18, /device:TPU:1, one launch (start us, length us, event | category | flops | bytes accessed | tf_op | source)
XLA Modules:
  0.0 40.1 jit_solution(9239151817303227993)
XLA Ops:
  0.0 0.0 copy-start.2
  0.8 1.0 %select_bitcast_fusion = (f32[1,2,16,512]{3,2,1,0:T(8,128)S(1)}, f32[2,16,512]{2,1,0:T(8,128)S(1)}, f32[2,16,512]{2,1,0:T(8,128)S(1)}, f32[2,16,512]{2,1,0:T(8,128)S(1)}) fusion(f32[2,128,512]{2,1,0:T(8,128)} %param.5, s32[]{:T(128)S(6)} %select_n.57, pred[16]{0:T(512)(128)(4,1)S(1)} %get-tuple-element.16, s32[]{:T(128)S(6)} %select_n.59, ...), kind=kLoop, calls=%fused_computation.5 | loop fusion | flops 65536 | bytes 524368 | tf_op jit(solution)/shard_map/stack | solution.py:191
  1.8 2.2 %collective-permute-start.4 = (f32[2,16,512]{2,1,0:T(8,128)S(1)}, f32[2,16,512]{2,1,0:T(8,128)S(1)}, u32[]{:S(2)}, u32[]{:S(2)}) collective-permute-start(f32[2,16,512]{2,1,0:T(8,128)S(1)} %get-tuple-element.6), channel_id=1, source_target_pairs={{0,8},{8,0},{16,24},{24,16},{1,9},{9,1},{17,25},{25,17},{2,10},{10... | collective-permute-start | bytes 196616 | tf_op jit(solution)/shard_map/ppermute | solution.py:189
  4.0 2.3 %collective-permute-start.5 = (f32[2,16,512]{2,1,0:T(8,128)S(1)}, f32[2,16,512]{2,1,0:T(8,128)S(1)}, u32[]{:S(2)}, u32[]{:S(2)}) collective-permute-start(f32[2,16,512]{2,1,0:T(8,128)S(1)} %get-tuple-element.8), channel_id=1, source_target_pairs={{0,16},{8,24},{16,0},{24,8},{1,17},{9,25},{17,1},{25,9},{2,18},{10... | collective-permute-start | bytes 196616 | tf_op jit(solution)/shard_map/ppermute | solution.py:189
  6.3 0.0 collective-permute-start.6
  6.4 0.0 copy-done.2
  6.4 0.1 select_bitcast_fusion.1
  6.5 0.4 collective-permute-start
  6.9 3.2 %collective-permute-start.1 = (f32[2,16,512]{2,1,0:T(8,128)S(1)}, f32[2,16,512]{2,1,0:T(8,128)S(1)}, u32[]{:S(2)}, u32[]{:S(2)}) collective-permute-start(f32[2,16,512]{2,1,0:T(8,128)S(1)} %get-tuple-element.11), channel_id=1, source_target_pairs={{0,16},{8,24},{16,0},{24,8},{1,17},{9,25},{17,1},{25,9},{2,18},{10... | collective-permute-start | bytes 196616 | tf_op jit(solution)/shard_map/ppermute | solution.py:189
  10.1 0.0 collective-permute-done.4
  10.1 0.0 collective-permute-start.2
  10.1 0.0 collective-permute-done.5
  10.1 1.3 %collective-permute-done.6 = f32[2,16,512]{2,1,0:T(8,128)S(1)} collective-permute-done((f32[2,16,512]{2,1,0:T(8,128)S(1)}, f32[2,16,512]{2,1,0:T(8,128)S(1)}, u32[]{:S(2)}, u32[]{:S(2)}) %collective-permute-start.6) | collective-permute-done | bytes 65568 | tf_op jit(solution)/shard_map/ppermute | solution.py:189
  11.4 5.7 %collective-permute-start.7 = (f32[4,2,16,512]{3,2,1,0:T(8,128)S(1)}, f32[4,2,16,512]{3,2,1,0:T(8,128)S(1)}, u32[]{:S(2)}, u32[]{:S(2)}) collective-permute-start(f32[4,2,16,512]{3,2,1,0:T(8,128)S(1)} %pad_maximum_fusion.1.own_ref), channel_id=1, source_target_pairs={{0,1},{1,2},{2,3},{3,4},{4,5},{5,6},{6,7},{8,9},{9,10},{10,11},{11... | collective-permute-start | bytes 786440 | tf_op jit(solution)/shard_map/ppermute | solution.py:193
  17.2 0.0 collective-permute-done
  17.2 0.0 collective-permute-done.1
  17.2 0.0 collective-permute-done.2
  17.2 4.4 %collective-permute-start.3 = (f32[4,2,16,512]{3,2,1,0:T(8,128)S(1)}, f32[4,2,16,512]{3,2,1,0:T(8,128)S(1)}, u32[]{:S(2)}, u32[]{:S(2)}) collective-permute-start(f32[4,2,16,512]{3,2,1,0:T(8,128)S(1)} %pad_maximum_fusion.own_ref), channel_id=1, source_target_pairs={{0,1},{1,2},{2,3},{3,4},{4,5},{5,6},{6,7},{8,9},{9,10},{10,11},{11... | collective-permute-start | bytes 786440 | tf_op jit(solution)/shard_map/ppermute | solution.py:193
  22.2 3.8 %shard_map.56.terms_ref = f32[8,4,16,512]{3,2,1,0:T(8,128)} custom-call(s32[4]{0:T(128)} %seq_ref.7, s32[1]{0:T(128)S(6)} %copy.9.skew_ref, f32[4,2,16,512]{3,2,1,0:T(8,128)S(1)} %pad_maximum_fusion.1.own_ref, f32[4,256]{1,0:T(4,128)} %cmap_ref.7), custom_call_target="tpu_custom_call" | custom-call | tf_op jit(solution)/shard_map/pallas_call | solution.py:199
  26.1 0.0 copy-start
  26.1 3.9 %shard_map.55.terms_ref = f32[8,4,16,512]{3,2,1,0:T(8,128)} custom-call(s32[4]{0:T(128)} %seq_ref.7, s32[1]{0:T(128)S(6)} %copy.9.skew_ref, f32[4,2,16,512]{3,2,1,0:T(8,128)S(1)} %pad_maximum_fusion.own_ref, f32[4,256]{1,0:T(4,128)} %cmap_ref.7), custom_call_target="tpu_custom_call" | custom-call | tf_op jit(solution)/shard_map/pallas_call | solution.py:199
  30.0 0.0 copy-start.1
  30.0 0.0 collective-permute-done.7.left_ref
  30.0 0.0 copy-done
  30.0 5.1 %shard_map.57.refs_0_ = f32[4,32,512]{2,1,0:T(8,128)} custom-call(s32[4]{0:T(128)} %seq_ref.7, s32[1]{0:T(128)S(6)} %copy.9.skew_ref, f32[4,2,16,512]{3,2,1,0:T(8,128)S(1)} %pad_maximum_fusion.1.own_ref, f32[4,2,16,512]{3,2,1,0:T(8,128)S(1)} %collective-permute-done.7.left_ref, f32[4,256]{1,0:T(4,128)} %cmap_ref.7, f32[8,4,16,512]{3,2,1,0:T(8,128)S(1)} %copy-done), custom_call_target="tpu_custom_call" | custom-call | tf_op jit(solution)/shard_map/pallas_call | solution.py:209
  35.1 0.0 collective-permute-done.3.left_ref
  35.1 0.0 copy-done.1
  35.1 5.0 %shard_map.58 = f32[4,32,512]{2,1,0:T(8,128)} custom-call(s32[4]{0:T(128)} %seq_ref.7, s32[1]{0:T(128)S(6)} %copy.9.skew_ref, f32[4,2,16,512]{3,2,1,0:T(8,128)S(1)} %pad_maximum_fusion.own_ref, f32[4,2,16,512]{3,2,1,0:T(8,128)S(1)} %collective-permute-done.3.left_ref, f32[4,256]{1,0:T(4,128)} %cmap_ref.7, ...), custom_call_target="tpu_custom_call", output_to_operand_aliasing={{}: (6, {})} | custom-call | tf_op jit(solution)/shard_map/pallas_call | solution.py:209
  (7 shorter events, 0.1 us)
Async XLA Ops:
  0.0 6.4 %copy-start.2 = (f32[2,128,512]{2,1,0:T(8,128)S(1)}, f32[2,128,512]{2,1,0:T(8,128)}, u32[]{:S(2)}) copy-start(f32[2,128,512]{2,1,0:T(8,128)} %param.5) | copy-start | bytes 1572868
  1.8 8.3 %collective-permute-start.4 = (f32[2,16,512]{2,1,0:T(8,128)S(1)}, f32[2,16,512]{2,1,0:T(8,128)S(1)}, u32[]{:S(2)}, u32[]{:S(2)}) collective-permute-start(f32[2,16,512]{2,1,0:T(8,128)S(1)} %get-tuple-element.6), channel_id=1, source_target_pairs={{0,8},{8,0},{16,24},{24,16},{1,9},{9,1},{17,25},{25,17},{2,10},{10... | collective-permute-start | bytes 196616 | tf_op jit(solution)/shard_map/ppermute | solution.py:189
  4.0 6.1 %collective-permute-start.5 = (f32[2,16,512]{2,1,0:T(8,128)S(1)}, f32[2,16,512]{2,1,0:T(8,128)S(1)}, u32[]{:S(2)}, u32[]{:S(2)}) collective-permute-start(f32[2,16,512]{2,1,0:T(8,128)S(1)} %get-tuple-element.8), channel_id=1, source_target_pairs={{0,16},{8,24},{16,0},{24,8},{1,17},{9,25},{17,1},{25,9},{2,18},{10... | collective-permute-start | bytes 196616 | tf_op jit(solution)/shard_map/ppermute | solution.py:189
  6.3 5.1 %collective-permute-start.6 = (f32[2,16,512]{2,1,0:T(8,128)S(1)}, f32[2,16,512]{2,1,0:T(8,128)S(1)}, u32[]{:S(2)}, u32[]{:S(2)}) collective-permute-start(f32[2,16,512]{2,1,0:T(8,128)S(1)} %get-tuple-element.7), channel_id=1, source_target_pairs={{0,24},{8,16},{16,8},{24,0},{1,25},{9,17},{17,9},{25,1},{2,26},{10... | collective-permute-start | bytes 196616 | tf_op jit(solution)/shard_map/ppermute | solution.py:189
  6.5 10.7 %collective-permute-start = (f32[2,16,512]{2,1,0:T(8,128)S(1)}, f32[2,16,512]{2,1,0:T(8,128)S(1)}, u32[]{:S(2)}, u32[]{:S(2)}) collective-permute-start(f32[2,16,512]{2,1,0:T(8,128)S(1)} %get-tuple-element.12), channel_id=1, source_target_pairs={{0,8},{8,0},{16,24},{24,16},{1,9},{9,1},{17,25},{25,17},{2,10},{10... | collective-permute-start | bytes 196616 | tf_op jit(solution)/shard_map/ppermute | solution.py:189
  6.9 10.3 %collective-permute-start.1 = (f32[2,16,512]{2,1,0:T(8,128)S(1)}, f32[2,16,512]{2,1,0:T(8,128)S(1)}, u32[]{:S(2)}, u32[]{:S(2)}) collective-permute-start(f32[2,16,512]{2,1,0:T(8,128)S(1)} %get-tuple-element.11), channel_id=1, source_target_pairs={{0,16},{8,24},{16,0},{24,8},{1,17},{9,25},{17,1},{25,9},{2,18},{10... | collective-permute-start | bytes 196616 | tf_op jit(solution)/shard_map/ppermute | solution.py:189
  10.1 7.1 %collective-permute-start.2 = (f32[2,16,512]{2,1,0:T(8,128)S(1)}, f32[2,16,512]{2,1,0:T(8,128)S(1)}, u32[]{:S(2)}, u32[]{:S(2)}) collective-permute-start(f32[2,16,512]{2,1,0:T(8,128)S(1)} %get-tuple-element.10), channel_id=1, source_target_pairs={{0,24},{8,16},{16,8},{24,0},{1,25},{9,17},{17,9},{25,1},{2,26},{10... | collective-permute-start | bytes 196616 | tf_op jit(solution)/shard_map/ppermute | solution.py:189
  11.4 18.6 %collective-permute-start.7 = (f32[4,2,16,512]{3,2,1,0:T(8,128)S(1)}, f32[4,2,16,512]{3,2,1,0:T(8,128)S(1)}, u32[]{:S(2)}, u32[]{:S(2)}) collective-permute-start(f32[4,2,16,512]{3,2,1,0:T(8,128)S(1)} %pad_maximum_fusion.1.own_ref), channel_id=1, source_target_pairs={{0,1},{1,2},{2,3},{3,4},{4,5},{5,6},{6,7},{8,9},{9,10},{10,11},{11... | collective-permute-start | bytes 786440 | tf_op jit(solution)/shard_map/ppermute | solution.py:193
  17.2 17.9 %collective-permute-start.3 = (f32[4,2,16,512]{3,2,1,0:T(8,128)S(1)}, f32[4,2,16,512]{3,2,1,0:T(8,128)S(1)}, u32[]{:S(2)}, u32[]{:S(2)}) collective-permute-start(f32[4,2,16,512]{3,2,1,0:T(8,128)S(1)} %pad_maximum_fusion.own_ref), channel_id=1, source_target_pairs={{0,1},{1,2},{2,3},{3,4},{4,5},{5,6},{6,7},{8,9},{9,10},{10,11},{11... | collective-permute-start | bytes 786440 | tf_op jit(solution)/shard_map/ppermute | solution.py:193
  26.1 3.9 %copy-start = (f32[8,4,16,512]{3,2,1,0:T(8,128)S(1)}, f32[8,4,16,512]{3,2,1,0:T(8,128)}, u32[]{:S(2)}) copy-start(f32[8,4,16,512]{3,2,1,0:T(8,128)} %shard_map.56.terms_ref) | copy-start | bytes 3145732
  30.0 5.1 %copy-start.1 = (f32[8,4,16,512]{3,2,1,0:T(8,128)S(1)}, f32[8,4,16,512]{3,2,1,0:T(8,128)}, u32[]{:S(2)}) copy-start(f32[8,4,16,512]{3,2,1,0:T(8,128)} %shard_map.55.terms_ref) | copy-start | bytes 3145732

commit v19 on v15

--- a/solution.py
+++ b/solution.py
@@ -120,7 +120,7 @@
         out_ref[3, band, cols] = 1.0 - jnp.exp(-depth_sum)
         return carry
 
-    lax.fori_loop(0, (rows // SUBLANES) * pieces, block, 0)
+    lax.fori_loop(0, (rows // SUBLANES) * pieces, block, 0, unroll=4)
     copy = pltpu.make_async_copy(out_ref, out_hbm.at[:, pl.ds(first_row, rows), :], sem)
     copy.start()
     copy.wait()

time: 31.5 us -> 30.3 us (0.962)
  Pallas kernels: 7.29 us -> 6.11 us
    pallas_call x2, Pallas kernels: 7.29 us -> 6.11 us  [shards(): pl.pallas_call(functools.partial(render_kernel, c * half), out_shape=jax....]
  transfers between devices with their start and end apart: 8 -> 8, of which waited for: 3 -> 3; matrix products, arithmetic and copies ran while one was open for 0% -> 1% of each run, Pallas kernels for 12% -> 10%
where the time goes in v19:
time: 30.3 us; the launch traced here: 30 us
  starting transfers between devices  13.4 us (44%)
  waiting for transfers between devices  7.83 us (26%)
  Pallas kernels  6.11 us (20%)
  between operations  1.48 us (5%)
  other arithmetic  1.21 us (4%)
    ppermute x6, starting transfers between devices, shards(): piece = lax.ppermute(piece, 'depth', route)  8.69 us
    pallas_call x2, Pallas kernels, shards(): pl.pallas_call(functools.partial(render_kernel, c * half), out_shape=jax....  6.11 us
    ppermute x6, waiting for transfers between devices, shards(): piece = lax.ppermute(piece, 'depth', route)  5.38 us
    ppermute x2, starting transfers between devices, shards(): lax.ppermute(own, 'region', [(i, i + 1) for i in range(regions - 1)])  4.73 us
    ppermute x2, waiting for transfers between devices, shards(): lax.ppermute(own, 'region', [(i, i + 1) for i in range(regions - 1)])  2.45 us
    another operation x4, other arithmetic, shards(): own = jnp.stack(held, axis=0)  1.18 us
  transfers between devices with their start and end apart: 8, of which 3 were waited for; matrix products, arithmetic and copies ran while one was open for 1% of the time, Pallas kernels for 10%

profile of v19, /device:TPU:4, one launch (start us, length us, event | category | flops | bytes accessed | tf_op | source)
XLA Modules:
  0.0 30.0 jit_solution(11421952975378927848)
XLA Ops:
  0.0 0.0 copy-start
  0.8 1.0 %select_bitcast_fusion = (f32[1,2,16,512]{3,2,1,0:T(8,128)S(1)}, f32[2,16,512]{2,1,0:T(8,128)S(1)}, f32[2,16,512]{2,1,0:T(8,128)S(1)}, f32[2,16,512]{2,1,0:T(8,128)S(1)}) fusion(f32[2,128,512]{2,1,0:T(8,128)} %param.5, s32[]{:T(128)S(6)} %select_n.57, pred[16]{0:T(512)(128)(4,1)S(1)} %get-tuple-element.16, s32[]{:T(128)S(6)} %select_n.59, ...), kind=kLoop, calls=%fused_computation.5 | loop fusion | flops 65536 | bytes 524368 | tf_op jit(solution)/shard_map/stack | solution.py:150
  1.8 1.6 %collective-permute-start.4 = (f32[2,16,512]{2,1,0:T(8,128)S(1)}, f32[2,16,512]{2,1,0:T(8,128)S(1)}, u32[]{:S(2)}, u32[]{:S(2)}) collective-permute-start(f32[2,16,512]{2,1,0:T(8,128)S(1)} %get-tuple-element.6), channel_id=1, source_target_pairs={{0,8},{8,0},{16,24},{24,16},{1,9},{9,1},{17,25},{25,17},{2,10},{10... | collective-permute-start | bytes 196616 | tf_op jit(solution)/shard_map/ppermute | solution.py:148
  3.4 2.5 %collective-permute-start.6 = (f32[2,16,512]{2,1,0:T(8,128)S(1)}, f32[2,16,512]{2,1,0:T(8,128)S(1)}, u32[]{:S(2)}, u32[]{:S(2)}) collective-permute-start(f32[2,16,512]{2,1,0:T(8,128)S(1)} %get-tuple-element.7), channel_id=1, source_target_pairs={{0,24},{8,16},{16,8},{24,0},{1,25},{9,17},{17,9},{25,1},{2,26},{10... | collective-permute-start | bytes 196616 | tf_op jit(solution)/shard_map/ppermute | solution.py:148
  5.9 0.1 collective-permute-start.5
  6.1 0.0 copy-done
  6.1 0.1 select_bitcast_fusion.1
  6.2 3.0 %collective-permute-start.2 = (f32[2,16,512]{2,1,0:T(8,128)S(1)}, f32[2,16,512]{2,1,0:T(8,128)S(1)}, u32[]{:S(2)}, u32[]{:S(2)}) collective-permute-start(f32[2,16,512]{2,1,0:T(8,128)S(1)} %get-tuple-element.10), channel_id=1, source_target_pairs={{0,24},{8,16},{16,8},{24,0},{1,25},{9,17},{17,9},{25,1},{2,26},{10... | collective-permute-start | bytes 196616 | tf_op jit(solution)/shard_map/ppermute | solution.py:148
  9.2 0.3 %collective-permute-start.1 = (f32[2,16,512]{2,1,0:T(8,128)S(1)}, f32[2,16,512]{2,1,0:T(8,128)S(1)}, u32[]{:S(2)}, u32[]{:S(2)}) collective-permute-start(f32[2,16,512]{2,1,0:T(8,128)S(1)} %get-tuple-element.11), channel_id=1, source_target_pairs={{0,16},{8,24},{16,0},{24,8},{1,17},{9,25},{17,1},{25,9},{2,18},{10... | collective-permute-start | bytes 196616 | tf_op jit(solution)/shard_map/ppermute | solution.py:148
  9.5 0.0 collective-permute-done.4
  9.5 1.1 %collective-permute-start = (f32[2,16,512]{2,1,0:T(8,128)S(1)}, f32[2,16,512]{2,1,0:T(8,128)S(1)}, u32[]{:S(2)}, u32[]{:S(2)}) collective-permute-start(f32[2,16,512]{2,1,0:T(8,128)S(1)} %get-tuple-element.12), channel_id=1, source_target_pairs={{0,8},{8,0},{16,24},{24,16},{1,9},{9,1},{17,25},{25,17},{2,10},{10... | collective-permute-start | bytes 196616 | tf_op jit(solution)/shard_map/ppermute | solution.py:148
  10.7 0.0 collective-permute-done.6
  10.7 4.7 %collective-permute-done.5 = f32[2,16,512]{2,1,0:T(8,128)S(1)} collective-permute-done((f32[2,16,512]{2,1,0:T(8,128)S(1)}, f32[2,16,512]{2,1,0:T(8,128)S(1)}, u32[]{:S(2)}, u32[]{:S(2)}) %collective-permute-start.5) | collective-permute-done | bytes 65568 | tf_op jit(solution)/shard_map/ppermute | solution.py:148
  15.3 1.9 %collective-permute-start.7 = (f32[4,2,16,512]{3,2,1,0:T(8,128)S(1)}, f32[4,2,16,512]{3,2,1,0:T(8,128)S(1)}, u32[]{:S(2)}, u32[]{:S(2)}) collective-permute-start(f32[4,2,16,512]{3,2,1,0:T(8,128)S(1)} %pad_maximum_fusion.1.own_ref), channel_id=1, source_target_pairs={{0,1},{1,2},{2,3},{3,4},{4,5},{5,6},{6,7},{8,9},{9,10},{10,11},{11... | collective-permute-start | bytes 786440 | tf_op jit(solution)/shard_map/ppermute | solution.py:152
  17.3 0.0 collective-permute-done.2
  17.3 0.7 %collective-permute-done.1 = f32[2,16,512]{2,1,0:T(8,128)S(1)} collective-permute-done((f32[2,16,512]{2,1,0:T(8,128)S(1)}, f32[2,16,512]{2,1,0:T(8,128)S(1)}, u32[]{:S(2)}, u32[]{:S(2)}) %collective-permute-start.1) | collective-permute-done | bytes 65568 | tf_op jit(solution)/shard_map/ppermute | solution.py:148
  18.0 0.0 collective-permute-done
  18.0 2.8 %collective-permute-start.3 = (f32[4,2,16,512]{3,2,1,0:T(8,128)S(1)}, f32[4,2,16,512]{3,2,1,0:T(8,128)S(1)}, u32[]{:S(2)}, u32[]{:S(2)}) collective-permute-start(f32[4,2,16,512]{3,2,1,0:T(8,128)S(1)} %pad_maximum_fusion.own_ref), channel_id=1, source_target_pairs={{0,1},{1,2},{2,3},{3,4},{4,5},{5,6},{6,7},{8,9},{9,10},{10,11},{11... | collective-permute-start | bytes 786440 | tf_op jit(solution)/shard_map/ppermute | solution.py:152
  21.5 2.4 %collective-permute-done.7.left_ref = f32[4,2,16,512]{3,2,1,0:T(8,128)S(1)} collective-permute-done((f32[4,2,16,512]{3,2,1,0:T(8,128)S(1)}, f32[4,2,16,512]{3,2,1,0:T(8,128)S(1)}, u32[]{:S(2)}, u32[]{:S(2)}) %collective-permute-start.7) | collective-permute-done | bytes 262176 | tf_op jit(solution)/shard_map/ppermute | solution.py:152
  23.9 3.1 %shard_map.55.refs_0_ = f32[4,32,512]{2,1,0:T(8,128)} custom-call(s32[4]{0:T(128)} %seq_ref.3, s32[1]{0:T(128)S(6)} %copy.9.skew_ref, f32[4,2,16,512]{3,2,1,0:T(8,128)S(1)} %pad_maximum_fusion.1.own_ref, f32[4,2,16,512]{3,2,1,0:T(8,128)S(1)} %collective-permute-done.7.left_ref, f32[4,256]{1,0:T(4,128)} %cmap_ref.3), custom_call_target="tpu_custom_call" | custom-call | tf_op jit(solution)/shard_map/pallas_call | solution.py:159
  27.0 0.0 collective-permute-done.3.left_ref
  27.0 3.1 %shard_map.56 = f32[4,32,512]{2,1,0:T(8,128)} custom-call(s32[4]{0:T(128)} %seq_ref.3, s32[1]{0:T(128)S(6)} %copy.9.skew_ref, f32[4,2,16,512]{3,2,1,0:T(8,128)S(1)} %pad_maximum_fusion.own_ref, f32[4,2,16,512]{3,2,1,0:T(8,128)S(1)} %collective-permute-done.3.left_ref, f32[4,256]{1,0:T(4,128)} %cmap_ref.3, ...), custom_call_target="tpu_custom_call", output_to_operand_aliasing={{}: (5, {})} | custom-call | tf_op jit(solution)/shard_map/pallas_call | solution.py:159
  (7 shorter events, 0.1 us)
Async XLA Ops:
  0.0 6.1 %copy-start = (f32[2,128,512]{2,1,0:T(8,128)S(1)}, f32[2,128,512]{2,1,0:T(8,128)}, u32[]{:S(2)}) copy-start(f32[2,128,512]{2,1,0:T(8,128)} %param.5) | copy-start | bytes 1572868
  1.8 7.7 %collective-permute-start.4 = (f32[2,16,512]{2,1,0:T(8,128)S(1)}, f32[2,16,512]{2,1,0:T(8,128)S(1)}, u32[]{:S(2)}, u32[]{:S(2)}) collective-permute-start(f32[2,16,512]{2,1,0:T(8,128)S(1)} %get-tuple-element.6), channel_id=1, source_target_pairs={{0,8},{8,0},{16,24},{24,16},{1,9},{9,1},{17,25},{25,17},{2,10},{10... | collective-permute-start | bytes 196616 | tf_op jit(solution)/shard_map/ppermute | solution.py:148
  3.4 7.2 %collective-permute-start.6 = (f32[2,16,512]{2,1,0:T(8,128)S(1)}, f32[2,16,512]{2,1,0:T(8,128)S(1)}, u32[]{:S(2)}, u32[]{:S(2)}) collective-permute-start(f32[2,16,512]{2,1,0:T(8,128)S(1)} %get-tuple-element.7), channel_id=1, source_target_pairs={{0,24},{8,16},{16,8},{24,0},{1,25},{9,17},{17,9},{25,1},{2,26},{10... | collective-permute-start | bytes 196616 | tf_op jit(solution)/shard_map/ppermute | solution.py:148
  5.9 9.4 %collective-permute-start.5 = (f32[2,16,512]{2,1,0:T(8,128)S(1)}, f32[2,16,512]{2,1,0:T(8,128)S(1)}, u32[]{:S(2)}, u32[]{:S(2)}) collective-permute-start(f32[2,16,512]{2,1,0:T(8,128)S(1)} %get-tuple-element.8), channel_id=1, source_target_pairs={{0,16},{8,24},{16,0},{24,8},{1,17},{9,25},{17,1},{25,9},{2,18},{10... | collective-permute-start | bytes 196616 | tf_op jit(solution)/shard_map/ppermute | solution.py:148
  6.2 11.1 %collective-permute-start.2 = (f32[2,16,512]{2,1,0:T(8,128)S(1)}, f32[2,16,512]{2,1,0:T(8,128)S(1)}, u32[]{:S(2)}, u32[]{:S(2)}) collective-permute-start(f32[2,16,512]{2,1,0:T(8,128)S(1)} %get-tuple-element.10), channel_id=1, source_target_pairs={{0,24},{8,16},{16,8},{24,0},{1,25},{9,17},{17,9},{25,1},{2,26},{10... | collective-permute-start | bytes 196616 | tf_op jit(solution)/shard_map/ppermute | solution.py:148
  9.2 8.8 %collective-permute-start.1 = (f32[2,16,512]{2,1,0:T(8,128)S(1)}, f32[2,16,512]{2,1,0:T(8,128)S(1)}, u32[]{:S(2)}, u32[]{:S(2)}) collective-permute-start(f32[2,16,512]{2,1,0:T(8,128)S(1)} %get-tuple-element.11), channel_id=1, source_target_pairs={{0,16},{8,24},{16,0},{24,8},{1,17},{9,25},{17,1},{25,9},{2,18},{10... | collective-permute-start | bytes 196616 | tf_op jit(solution)/shard_map/ppermute | solution.py:148
  9.5 8.5 %collective-permute-start = (f32[2,16,512]{2,1,0:T(8,128)S(1)}, f32[2,16,512]{2,1,0:T(8,128)S(1)}, u32[]{:S(2)}, u32[]{:S(2)}) collective-permute-start(f32[2,16,512]{2,1,0:T(8,128)S(1)} %get-tuple-element.12), channel_id=1, source_target_pairs={{0,8},{8,0},{16,24},{24,16},{1,9},{9,1},{17,25},{25,17},{2,10},{10... | collective-permute-start | bytes 196616 | tf_op jit(solution)/shard_map/ppermute | solution.py:148
  15.3 8.6 %collective-permute-start.7 = (f32[4,2,16,512]{3,2,1,0:T(8,128)S(1)}, f32[4,2,16,512]{3,2,1,0:T(8,128)S(1)}, u32[]{:S(2)}, u32[]{:S(2)}) collective-permute-start(f32[4,2,16,512]{3,2,1,0:T(8,128)S(1)} %pad_maximum_fusion.1.own_ref), channel_id=1, source_target_pairs={{0,1},{1,2},{2,3},{3,4},{4,5},{5,6},{6,7},{8,9},{9,10},{10,11},{11... | collective-permute-start | bytes 786440 | tf_op jit(solution)/shard_map/ppermute | solution.py:152
  18.0 9.0 %collective-permute-start.3 = (f32[4,2,16,512]{3,2,1,0:T(8,128)S(1)}, f32[4,2,16,512]{3,2,1,0:T(8,128)S(1)}, u32[]{:S(2)}, u32[]{:S(2)}) collective-permute-start(f32[4,2,16,512]{3,2,1,0:T(8,128)S(1)} %pad_maximum_fusion.own_ref), channel_id=1, source_target_pairs={{0,1},{1,2},{2,3},{3,4},{4,5},{5,6},{6,7},{8,9},{9,10},{10,11},{11... | collective-permute-start | bytes 786440 | tf_op jit(solution)/shard_map/ppermute | solution.py:152

commit v20 on v19

--- a/solution.py
+++ b/solution.py
@@ -13,14 +13,10 @@
 
 
 def partner(i, m, n, sign=1):
-    if n & (n - 1) == 0:
-        return i ^ m
     return (i + sign * m) % n
 
 
 def slot_of(s, me, n):
-    if n & (n - 1) == 0:
-        return s ^ me
     return (s - me + n) % n
 
 

time: 30.3 us -> 31.4 us (1.036)
  starting transfers between devices: 13.4 us -> 16 us
  waiting for transfers between devices: 7.83 us -> 6.33 us
    ppermute x6, starting transfers between devices: 8.69 us -> 10.5 us  [shards(): piece = lax.ppermute(piece, 'depth', route)]
    ppermute x6, waiting for transfers between devices: 5.38 us -> 3.88 us  [shards(): piece = lax.ppermute(piece, 'depth', route)]
    ppermute x2, starting transfers between devices: 4.73 us -> 5.42 us  [shards(): lax.ppermute(own, 'region', [(i, i + 1) for i in range(regions - 1)])]
  transfers between devices with their start and end apart: 8 -> 8, of which waited for: 3 -> 2; matrix products, arithmetic and copies ran while one was open for 1% -> 0% of each run, Pallas kernels for 10% -> 10%
where the time goes in v20:
time: 31.4 us; the launch traced here: 31.1 us
  starting transfers between devices  16 us (51%)
  waiting for transfers between devices  6.33 us (20%)
  Pallas kernels  6.11 us (19%)
  between operations  1.51 us (5%)
  other arithmetic  1.21 us (4%)
    ppermute x6, starting transfers between devices, shards(): piece = lax.ppermute(piece, 'depth', route)  10.5 us
    pallas_call x2, Pallas kernels, shards(): pl.pallas_call(functools.partial(render_kernel, c * half), out_shape=jax....  6.11 us
    ppermute x2, starting transfers between devices, shards(): lax.ppermute(own, 'region', [(i, i + 1) for i in range(regions - 1)])  5.42 us
    ppermute x6, waiting for transfers between devices, shards(): piece = lax.ppermute(piece, 'depth', route)  3.88 us
    ppermute x2, waiting for transfers between devices, shards(): lax.ppermute(own, 'region', [(i, i + 1) for i in range(regions - 1)])  2.45 us
    another operation x4, other arithmetic, shards(): own = jnp.stack(held, axis=0)  1.18 us
  transfers between devices with their start and end apart: 8, of which 2 were waited for; matrix products, arithmetic and copies ran while one was open for 0% of the time, Pallas kernels for 10%

profile of v20, /device:TPU:4, one launch (start us, length us, event | category | flops | bytes accessed | tf_op | source)
XLA Modules:
  0.0 31.1 jit_solution(1813230152753188805)
XLA Ops:
  0.0 0.0 copy-start
  0.8 1.0 %select_bitcast_fusion = (f32[1,2,16,512]{3,2,1,0:T(8,128)S(1)}, f32[2,16,512]{2,1,0:T(8,128)S(1)}, f32[2,16,512]{2,1,0:T(8,128)S(1)}, f32[2,16,512]{2,1,0:T(8,128)S(1)}) fusion(f32[2,128,512]{2,1,0:T(8,128)} %param.5, s32[]{:T(128)S(6)} %select_n.88, pred[16]{0:T(512)(128)(4,1)S(1)} %get-tuple-element.16, s32[]{:T(128)S(6)} %select_n.90, ...), kind=kLoop, calls=%fused_computation.5 | loop fusion | flops 65536 | bytes 524368 | tf_op jit(solution)/shard_map/stack | solution.py:146
  1.8 3.7 %collective-permute-start.4 = (f32[2,16,512]{2,1,0:T(8,128)S(1)}, f32[2,16,512]{2,1,0:T(8,128)S(1)}, u32[]{:S(2)}, u32[]{:S(2)}) collective-permute-start(f32[2,16,512]{2,1,0:T(8,128)S(1)} %get-tuple-element.6), channel_id=1, source_target_pairs={{0,24},{8,0},{16,8},{24,16},{1,25},{9,1},{17,9},{25,17},{2,26},{10... | collective-permute-start | bytes 196616 | tf_op jit(solution)/shard_map/ppermute | solution.py:144
  5.5 0.0 collective-permute-start.6
  5.5 1.0 %collective-permute-start.5 = (f32[2,16,512]{2,1,0:T(8,128)S(1)}, f32[2,16,512]{2,1,0:T(8,128)S(1)}, u32[]{:S(2)}, u32[]{:S(2)}) collective-permute-start(f32[2,16,512]{2,1,0:T(8,128)S(1)} %get-tuple-element.8), channel_id=1, source_target_pairs={{0,16},{8,24},{16,0},{24,8},{1,17},{9,25},{17,1},{25,9},{2,18},{10... | collective-permute-start | bytes 196616 | tf_op jit(solution)/shard_map/ppermute | solution.py:144
  6.5 0.0 copy-done
  6.5 0.1 select_bitcast_fusion.1
  6.6 3.4 %collective-permute-start.2 = (f32[2,16,512]{2,1,0:T(8,128)S(1)}, f32[2,16,512]{2,1,0:T(8,128)S(1)}, u32[]{:S(2)}, u32[]{:S(2)}) collective-permute-start(f32[2,16,512]{2,1,0:T(8,128)S(1)} %get-tuple-element.10), channel_id=1, source_target_pairs={{0,8},{8,16},{16,24},{24,0},{1,9},{9,17},{17,25},{25,1},{2,10},{10... | collective-permute-start | bytes 196616 | tf_op jit(solution)/shard_map/ppermute | solution.py:144
  10.1 0.0 collective-permute-start.1
  10.1 0.0 collective-permute-done.4
  10.1 2.4 %collective-permute-start = (f32[2,16,512]{2,1,0:T(8,128)S(1)}, f32[2,16,512]{2,1,0:T(8,128)S(1)}, u32[]{:S(2)}, u32[]{:S(2)}) collective-permute-start(f32[2,16,512]{2,1,0:T(8,128)S(1)} %get-tuple-element.12), channel_id=1, source_target_pairs={{0,24},{8,0},{16,8},{24,16},{1,25},{9,1},{17,9},{25,17},{2,26},{10... | collective-permute-start | bytes 196616 | tf_op jit(solution)/shard_map/ppermute | solution.py:144
  12.5 0.0 collective-permute-done.6
  12.5 3.9 %collective-permute-done.5 = f32[2,16,512]{2,1,0:T(8,128)S(1)} collective-permute-done((f32[2,16,512]{2,1,0:T(8,128)S(1)}, f32[2,16,512]{2,1,0:T(8,128)S(1)}, u32[]{:S(2)}, u32[]{:S(2)}) %collective-permute-start.5) | collective-permute-done | bytes 65568 | tf_op jit(solution)/shard_map/ppermute | solution.py:144
  16.4 1.9 %collective-permute-start.7 = (f32[4,2,16,512]{3,2,1,0:T(8,128)S(1)}, f32[4,2,16,512]{3,2,1,0:T(8,128)S(1)}, u32[]{:S(2)}, u32[]{:S(2)}) collective-permute-start(f32[4,2,16,512]{3,2,1,0:T(8,128)S(1)} %pad_maximum_fusion.1.own_ref), channel_id=1, source_target_pairs={{0,1},{1,2},{2,3},{3,4},{4,5},{5,6},{6,7},{8,9},{9,10},{10,11},{11... | collective-permute-start | bytes 786440 | tf_op jit(solution)/shard_map/ppermute | solution.py:148
  18.3 0.0 collective-permute-done.2
  18.3 0.0 collective-permute-done.1
  18.4 0.0 collective-permute-done
  18.4 3.5 %collective-permute-start.3 = (f32[4,2,16,512]{3,2,1,0:T(8,128)S(1)}, f32[4,2,16,512]{3,2,1,0:T(8,128)S(1)}, u32[]{:S(2)}, u32[]{:S(2)}) collective-permute-start(f32[4,2,16,512]{3,2,1,0:T(8,128)S(1)} %pad_maximum_fusion.own_ref), channel_id=1, source_target_pairs={{0,1},{1,2},{2,3},{3,4},{4,5},{5,6},{6,7},{8,9},{9,10},{10,11},{11... | collective-permute-start | bytes 786440 | tf_op jit(solution)/shard_map/ppermute | solution.py:148
  22.5 2.4 %collective-permute-done.7.left_ref = f32[4,2,16,512]{3,2,1,0:T(8,128)S(1)} collective-permute-done((f32[4,2,16,512]{3,2,1,0:T(8,128)S(1)}, f32[4,2,16,512]{3,2,1,0:T(8,128)S(1)}, u32[]{:S(2)}, u32[]{:S(2)}) %collective-permute-start.7) | collective-permute-done | bytes 262176 | tf_op jit(solution)/shard_map/ppermute | solution.py:148
  25.0 3.1 %shard_map.55.refs_0_ = f32[4,32,512]{2,1,0:T(8,128)} custom-call(s32[4]{0:T(128)} %seq_ref.3, s32[1]{0:T(128)S(6)} %copy.9.skew_ref, f32[4,2,16,512]{3,2,1,0:T(8,128)S(1)} %pad_maximum_fusion.1.own_ref, f32[4,2,16,512]{3,2,1,0:T(8,128)S(1)} %collective-permute-done.7.left_ref, f32[4,256]{1,0:T(4,128)} %cmap_ref.3), custom_call_target="tpu_custom_call" | custom-call | tf_op jit(solution)/shard_map/pallas_call | solution.py:155
  28.1 0.0 collective-permute-done.3.left_ref
  28.1 3.1 %shard_map.56 = f32[4,32,512]{2,1,0:T(8,128)} custom-call(s32[4]{0:T(128)} %seq_ref.3, s32[1]{0:T(128)S(6)} %copy.9.skew_ref, f32[4,2,16,512]{3,2,1,0:T(8,128)S(1)} %pad_maximum_fusion.own_ref, f32[4,2,16,512]{3,2,1,0:T(8,128)S(1)} %collective-permute-done.3.left_ref, f32[4,256]{1,0:T(4,128)} %cmap_ref.3, ...), custom_call_target="tpu_custom_call", output_to_operand_aliasing={{}: (5, {})} | custom-call | tf_op jit(solution)/shard_map/pallas_call | solution.py:155
  (7 shorter events, 0.1 us)
Async XLA Ops:
  0.0 6.5 %copy-start = (f32[2,128,512]{2,1,0:T(8,128)S(1)}, f32[2,128,512]{2,1,0:T(8,128)}, u32[]{:S(2)}) copy-start(f32[2,128,512]{2,1,0:T(8,128)} %param.5) | copy-start | bytes 1572868
  1.8 8.3 %collective-permute-start.4 = (f32[2,16,512]{2,1,0:T(8,128)S(1)}, f32[2,16,512]{2,1,0:T(8,128)S(1)}, u32[]{:S(2)}, u32[]{:S(2)}) collective-permute-start(f32[2,16,512]{2,1,0:T(8,128)S(1)} %get-tuple-element.6), channel_id=1, source_target_pairs={{0,24},{8,0},{16,8},{24,16},{1,25},{9,1},{17,9},{25,17},{2,26},{10... | collective-permute-start | bytes 196616 | tf_op jit(solution)/shard_map/ppermute | solution.py:144
  5.5 7.0 %collective-permute-start.6 = (f32[2,16,512]{2,1,0:T(8,128)S(1)}, f32[2,16,512]{2,1,0:T(8,128)S(1)}, u32[]{:S(2)}, u32[]{:S(2)}) collective-permute-start(f32[2,16,512]{2,1,0:T(8,128)S(1)} %get-tuple-element.7), channel_id=1, source_target_pairs={{0,8},{8,16},{16,24},{24,0},{1,9},{9,17},{17,25},{25,1},{2,10},{10... | collective-permute-start | bytes 196616 | tf_op jit(solution)/shard_map/ppermute | solution.py:144
  5.5 10.9 %collective-permute-start.5 = (f32[2,16,512]{2,1,0:T(8,128)S(1)}, f32[2,16,512]{2,1,0:T(8,128)S(1)}, u32[]{:S(2)}, u32[]{:S(2)}) collective-permute-start(f32[2,16,512]{2,1,0:T(8,128)S(1)} %get-tuple-element.8), channel_id=1, source_target_pairs={{0,16},{8,24},{16,0},{24,8},{1,17},{9,25},{17,1},{25,9},{2,18},{10... | collective-permute-start | bytes 196616 | tf_op jit(solution)/shard_map/ppermute | solution.py:144
  6.6 11.7 %collective-permute-start.2 = (f32[2,16,512]{2,1,0:T(8,128)S(1)}, f32[2,16,512]{2,1,0:T(8,128)S(1)}, u32[]{:S(2)}, u32[]{:S(2)}) collective-permute-start(f32[2,16,512]{2,1,0:T(8,128)S(1)} %get-tuple-element.10), channel_id=1, source_target_pairs={{0,8},{8,16},{16,24},{24,0},{1,9},{9,17},{17,25},{25,1},{2,10},{10... | collective-permute-start | bytes 196616 | tf_op jit(solution)/shard_map/ppermute | solution.py:144
  10.1 8.3 %collective-permute-start.1 = (f32[2,16,512]{2,1,0:T(8,128)S(1)}, f32[2,16,512]{2,1,0:T(8,128)S(1)}, u32[]{:S(2)}, u32[]{:S(2)}) collective-permute-start(f32[2,16,512]{2,1,0:T(8,128)S(1)} %get-tuple-element.11), channel_id=1, source_target_pairs={{0,16},{8,24},{16,0},{24,8},{1,17},{9,25},{17,1},{25,9},{2,18},{10... | collective-permute-start | bytes 196616 | tf_op jit(solution)/shard_map/ppermute | solution.py:144
  10.1 8.3 %collective-permute-start = (f32[2,16,512]{2,1,0:T(8,128)S(1)}, f32[2,16,512]{2,1,0:T(8,128)S(1)}, u32[]{:S(2)}, u32[]{:S(2)}) collective-permute-start(f32[2,16,512]{2,1,0:T(8,128)S(1)} %get-tuple-element.12), channel_id=1, source_target_pairs={{0,24},{8,0},{16,8},{24,16},{1,25},{9,1},{17,9},{25,17},{2,26},{10... | collective-permute-start | bytes 196616 | tf_op jit(solution)/shard_map/ppermute | solution.py:144
  16.4 8.6 %collective-permute-start.7 = (f32[4,2,16,512]{3,2,1,0:T(8,128)S(1)}, f32[4,2,16,512]{3,2,1,0:T(8,128)S(1)}, u32[]{:S(2)}, u32[]{:S(2)}) collective-permute-start(f32[4,2,16,512]{3,2,1,0:T(8,128)S(1)} %pad_maximum_fusion.1.own_ref), channel_id=1, source_target_pairs={{0,1},{1,2},{2,3},{3,4},{4,5},{5,6},{6,7},{8,9},{9,10},{10,11},{11... | collective-permute-start | bytes 786440 | tf_op jit(solution)/shard_map/ppermute | solution.py:148
  18.4 9.7 %collective-permute-start.3 = (f32[4,2,16,512]{3,2,1,0:T(8,128)S(1)}, f32[4,2,16,512]{3,2,1,0:T(8,128)S(1)}, u32[]{:S(2)}, u32[]{:S(2)}) collective-permute-start(f32[4,2,16,512]{3,2,1,0:T(8,128)S(1)} %pad_maximum_fusion.own_ref), channel_id=1, source_target_pairs={{0,1},{1,2},{2,3},{3,4},{4,5},{5,6},{6,7},{8,9},{9,10},{10,11},{11... | collective-permute-start | bytes 786440 | tf_op jit(solution)/shard_map/ppermute | solution.py:148
